TPU v7x, 256 devices: a whole 4x4x8 slice. The times are simulated.
256 devices in a mesh: ctx: 64 (over y, z, core), head: 4 (over x).
Axes of the slice: x: 4, y: 4, z: 8, core: 2. Of those that a mesh axis runs over, the one named last changes fastest.
Arguments:
- queries: bfloat16 [8192, 4096], P('ctx', 'head'), may hold values from -6 to 6
- key_heads: bfloat16 [8192, 4096], P('ctx', 'head'), may hold values from -0.59765625 to 0.59765625
- value_heads: bfloat16 [8192, 4096], P('ctx', 'head'), may hold values from -12 to 12
- gate_logits: bfloat16 [8192, 4096], P('ctx', 'head'), may hold values from -9 to 9
- log_decay: float32 [8192, 32], P('ctx', 'head'), may hold values from -2 to 0
- attn_gain: float32 [4096], P('head'), may hold values from 0.25 to 1.75
- out_weight: bfloat16 [32, 128, 6144], P('head', 'ctx'), may hold values from -0.09375 to 0.09375
- residual: bfloat16 [8192, 6144], P('ctx'), may hold values from -24 to 24
- norm_gain: float32 [6144], replicated, may hold values from 0.25 to 1.75
- router_weight: bfloat16 [6144, 32], replicated, may hold values from -0.078125 to 0.078125
- expert_ids: int32 [8192, 2], P('ctx'), may hold values from 0 to 31, as said below
- expert_gate: bfloat16 [36864, 6144], P(('ctx', 'head')), may hold values from -0.078125 to 0.078125
- expert_up: bfloat16 [36864, 6144], P(('ctx', 'head')), may hold values from -0.078125 to 0.078125
- expert_down: bfloat16 [36864, 6144], P('ctx', 'head'), may hold values from -0.09375 to 0.09375
Outputs:
- layer_out: bfloat16 [8192, 6144], P('ctx', 'head')
Inputs may be any that keep to these rules, and one draw needn't show every extreme that they name: `expert_ids`: A row's two ids differ; within the 128 rows of one block no id is named by more than 10 rows.
All inputs are finite; a program needn't handle non-finite values.
Results may differ from a plain program's by a relative error of at most 0.008.
Values may be sent and summed in bfloat16 or wider, within the bound.
No kernel may reach another device: no remote copies, remote signals or barrier semaphores. Data moves between devices by JAX's collectives and lax.ppermute only.
A program may use at most 128 MiB of HBM per device.

v0:
```python
import jax
import jax.numpy as jnp
from jax import lax
from jax.sharding import PartitionSpec as P

EXP = 8
MOST = 10


epsilon = 1e-06
highest = lax.Precision.HIGHEST


def prefix(value, axis, join, neutral):
    place = lax.axis_index(axis)
    gathered = jax.tree.map(
        lambda a, kind: lax.all_gather(a.astype(kind), axis), value, (jnp.bfloat16, jnp.bfloat16)
    )
    state = jax.tree.map(lambda a, e: jnp.zeros_like(a) + jnp.asarray(e, a.dtype), value, neutral)

    def one(hop, state):
        return join(
            state,
            jax.tree.map(
                lambda a, own: lax.dynamic_index_in_dim(a, hop, 0, False).astype(own.dtype),
                gathered,
                value,
            ),
        )

    return lax.fori_loop(0, place, one, state)


def chain_combine(earlier, later):
    return (earlier[0] * later[0], later[0][:, None, None] * earlier[1] + later[1])


def body(
    queries,
    key_heads,
    value_heads,
    gate_logits,
    log_decay,
    attn_gain,
    out_weight,
    residual,
    norm_gain,
    router_weight,
    expert_ids,
    expert_gate,
    expert_up,
    expert_down,
):
    ctx_count = lax.axis_size("ctx")
    head_count = lax.axis_size("head")
    head_index = lax.axis_index("head")
    tok_rows = queries.shape[0]
    local_heads = log_decay.shape[1]
    head_dim = queries.shape[1] // local_heads
    model_width = residual.shape[1]
    share_width = model_width // head_count
    query_blocks = queries.reshape(tok_rows, local_heads, head_dim)
    key_blocks = key_heads.reshape(tok_rows, local_heads, head_dim)
    value_blocks = value_heads.reshape(tok_rows, local_heads, head_dim)
    cumulative = jnp.cumsum(log_decay, axis=0)
    block_total = cumulative[-1]
    keys_decayed = (
        key_blocks.astype(jnp.float32) * jnp.exp(block_total[None, :] - cumulative)[:, :, None]
    ).astype(jnp.bfloat16)
    local_state = jnp.einsum(
        "thd,the->hde", keys_decayed, value_blocks, preferred_element_type=jnp.float32
    )
    identity = (
        jnp.ones((local_heads,), jnp.float32),
        jnp.zeros((local_heads, head_dim, head_dim), jnp.float32),
    )
    _, entering = prefix((jnp.exp(block_total), local_state), "ctx", chain_combine, identity)
    sequence_offsets = jnp.arange(tok_rows)
    causal = (sequence_offsets[:, None] >= sequence_offsets[None, :])[None, :, :]
    cum_heads = cumulative.T
    decay_gaps = jnp.where(causal, cum_heads[:, :, None] - cum_heads[:, None, :], 0.0)
    scores = jnp.einsum(
        "thd,shd->hts", query_blocks, key_blocks, preferred_element_type=jnp.float32
    )
    attn_probs = jnp.where(causal, scores * jnp.exp(decay_gaps), 0.0).astype(jnp.bfloat16)
    within = jnp.einsum(
        "hts,shd->thd", attn_probs, value_blocks, preferred_element_type=jnp.float32
    )
    carried = jnp.einsum(
        "thd,hde->the", query_blocks.astype(jnp.float32), entering, precision=highest
    )
    attended = within + carried * jnp.exp(cumulative)[:, :, None]
    rms_scale = lax.rsqrt(jnp.mean(attended * attended, axis=-1, keepdims=True) + epsilon)
    gate_open = jax.nn.sigmoid(
        gate_logits.astype(jnp.float32).reshape(tok_rows, local_heads, head_dim)
    )
    attn_mixed = (
        attended * rms_scale * attn_gain.reshape(local_heads, head_dim) * gate_open
    ).astype(jnp.bfloat16)
    row_whole = lax.all_gather(out_weight, "ctx", axis=1, tiled=True)
    partial_sum = jnp.einsum(
        "thr,hrd->td", attn_mixed, row_whole, preferred_element_type=jnp.float32
    )
    projected = lax.psum(partial_sum.astype(jnp.bfloat16), "head").astype(jnp.float32)
    hidden_full = residual.astype(jnp.float32) + projected
    normed_full = (
        hidden_full
        * lax.rsqrt(jnp.mean(hidden_full * hidden_full, axis=-1, keepdims=True) + epsilon)
        * norm_gain[None, :]
    ).astype(jnp.bfloat16)
    hidden_share = lax.dynamic_slice_in_dim(hidden_full, head_index * share_width, share_width, 1)
    logits = jnp.dot(normed_full, router_weight, preferred_element_type=jnp.float32)
    columns = jnp.arange(router_weight.shape[1], dtype=jnp.int32)
    picked = jnp.sum(
        jnp.where(columns[None, None, :] == expert_ids[:, :, None], logits[:, None, :], 0.0),
        axis=-1,
    )
    route_gates = jax.nn.sigmoid(picked - picked[:, ::-1])
    route_ids = expert_ids.reshape(-1)
    onehot = (route_ids[:, None] == jnp.arange(EXP, dtype=jnp.int32)[None, :]).astype(jnp.int32)
    before = jnp.cumsum(onehot, axis=0) - onehot
    slot_index = jnp.sum(before * onehot, axis=1)
    slot_range = jnp.arange(MOST, dtype=jnp.int32)
    placed = (onehot.T[:, None, :] == 1) & (slot_index[None, None, :] == slot_range[None, :, None])
    chooser = (
        jnp.sum(placed.reshape(EXP, MOST, tok_rows, 2).astype(jnp.float32), axis=3)
        .astype(jnp.bfloat16)
        .reshape(EXP * MOST, tok_rows)
    )
    weighted = jnp.sum(
        (placed.astype(jnp.float32) * route_gates.reshape(-1)[None, None, :]).reshape(
            EXP, MOST, tok_rows, 2
        ),
        axis=3,
    )
    group = ctx_count // EXP
    packed = (
        jnp.dot(chooser, normed_full, preferred_element_type=jnp.float32)
        .astype(jnp.bfloat16)
        .reshape(EXP, MOST, model_width)
    )
    outgoing = jnp.repeat(packed, group, axis=0)
    arrived = lax.all_to_all(outgoing, "ctx", split_axis=0, concat_axis=0, tiled=True)
    sources = arrived.shape[0]
    slots_now = arrived.shape[1]
    flat_rows = arrived.reshape(sources * slots_now, model_width)
    gate_part = jnp.einsum("rd,fd->rf", flat_rows, expert_gate, preferred_element_type=jnp.float32)
    up_part = jnp.einsum("rd,fd->rf", flat_rows, expert_up, preferred_element_type=jnp.float32)
    hidden_units = (
        (jax.nn.silu(gate_part) * up_part).astype(jnp.bfloat16).reshape(sources, slots_now, -1)
    )
    joined = lax.all_gather(hidden_units, "head", axis=2, tiled=True)
    partial_value = jnp.einsum(
        "nmf,fd->nmd", joined, expert_down, preferred_element_type=jnp.float32
    ).astype(jnp.bfloat16)
    returned = lax.all_to_all(partial_value, "ctx", split_axis=0, concat_axis=0, tiled=True)
    summed = jnp.sum(returned.astype(jnp.float32).reshape(EXP, group, MOST, share_width), axis=1)
    mixture = jnp.einsum("est,esd->td", weighted, summed, precision=highest)
    return (hidden_share + mixture).astype(jnp.bfloat16)


def solution(mesh):
    return jax.shard_map(
        body,
        mesh=mesh,
        in_specs=(
            P("ctx", "head"),
            P("ctx", "head"),
            P("ctx", "head"),
            P("ctx", "head"),
            P("ctx", "head"),
            P("head"),
            P("head", "ctx", None),
            P("ctx", None),
            P(),
            P(),
            P("ctx", None),
            P(("ctx", "head"), None),
            P(("ctx", "head"), None),
            P("ctx", "head"),
        ),
        out_specs=P("ctx", "head"),
        check_vma=False,
    )
```

profile of v0, /device:TPU:1, one launch (start us, length us, event | category | flops | bytes accessed | tf_op | source)
XLA Modules:
  0.0 722.4 jit_solution(2604290321409180493)
XLA Ops:
  6.5 0.9 copy.83
  7.7 1.1 copy.116
  8.9 1.9 convolution_convert_fusion.2
  10.8 1.7 copy.96
  12.6 44.3 %all-gather.1 = bf16[64,1,8]{2,1,0:T(2,128)(2,1)S(1)} all-gather(bf16[1,1,8]{2,1,0:T(2,128)(2,1)S(1)} %get-tuple-element.82), channel_id=1, replica_groups=mesh['ctx'=64,'head'=4] {'ctx'}, dimensions={0}, use_global_device_ids=true | all-gather | bytes 1040 | tf_op jit(solution)/shard_map/all_gather | solution.py:17
  57.0 1.1 add_divide_fusion
  58.1 1.0 copy.95
  59.2 55.2 %all-gather.7.cloned.1.call-done = bf16[512,128,128]{2,1,0:T(8,128)(2,1)} async-done(((bf16[8,128,128]{2,1,0:T(8,128)(2,1)}), bf16[512,128,128]{2,1,0:T(8,128)(2,1)}) %all-gather.7.cloned.1.call-update) | async-done | bytes 16777232 | tf_op jit(solution)/shard_map/all_gather | solution.py:17
  114.5 1.2 while.12
  114.5 1.1 convert_add_fusion.5
  115.7 1.5 fusion.14
  117.2 2.3 multiply_reduce_fusion.1
  119.5 84.2 %all-gather.5.cloned.1.call-done = bf16[8,128,6144]{2,0,1:T(8,128)(2,1)} async-done(((bf16[8,2,6144]{2,0,1:T(8,128)(2,1)}), bf16[8,128,6144]{2,0,1:T(8,128)(2,1)}) %all-gather.5.cloned.1.call-update) | async-done | bytes 12582928 | tf_op jit(solution)/shard_map/all_gather | solution.py:100
  203.7 20.6 %fusion.5 = bf16[128,6144]{1,0:T(8,128)(2,1)} fusion(bf16[8,128,6144]{2,0,1:T(8,128)(2,1)} %all-gather.5.cloned.1.call-done, f32[128,8,128]{0,2,1:T(8,128)} %bitcast.96, f32[128,8,128]{0,2,1:T(8,128)} %get-tuple-element.84, f32[8,128]{1,0:T(8,128)S(1)} %bitcast.100, f32[128,8]{0,1:T(8,128)S(1)} %add_rsqrt_fusion), kind=kOutput, calls=%fused_computation.5 | convolution fusion | flops 1611923456 | bytes 15212544 | tf_op jit(solution)/shard_map/thr,hrd->td/dot_general | solution.py:101
  225.9 50.4 %all-reduce.2.cloned.1.call-done = bf16[128,6144]{1,0:T(8,128)(2,1)} async-done(((bf16[128,6144]{1,0:T(8,128)(2,1)}), bf16[128,6144]{1,0:T(8,128)(2,1)}) %all-reduce.2.cloned.1.call-update) | async-done | bytes 1572880 | tf_op jit(solution)/shard_map/psum | solution.py:104
  276.4 3.8 convert_add_fusion.1
  280.2 0.8 fusion.44
  281.2 3.2 convolution_convert_fusion
  284.4 1.4 reshape.183
  285.8 6.2 broadcast_in_dim.57
  292.0 286.8 %all_to_all.10 = bf16[64,10,6144]{2,1,0:T(8,128)(2,1)} all-to-all(bf16[64,10,6144]{2,1,0:T(8,128)(2,1)} %bitcast.95), channel_id=1, replica_groups=mesh['ctx'=64,'head'=4] {'ctx'}, dimensions={0} | all-to-all | bytes 15728640 | tf_op jit(solution)/shard_map/all_to_all | solution.py:143
  578.8 13.8 %reshape.185 = bf16[640,6144]{1,0:T(8,128)(2,1)} reshape(bf16[64,10,6144]{2,1,0:T(8,128)(2,1)} %all_to_all.10) | data formatting | bytes 15728640 | tf_op jit(solution)/shard_map/reshape | solution.py:146
  592.6 6.5 fusion.48
  599.1 2.6 fusion.16
  602.1 0.9 copy.104
  603.0 22.7 %all_gather.20 = bf16[64,10,576]{0,1,2:T(8,128)(2,1)S(1)} all-gather(bf16[64,10,144]{0,1,2:T(8,128)(2,1)S(1)} %copy.104), channel_id=1, replica_groups=mesh['ctx'=64,'head'=4] {'head'}, dimensions={2}, use_global_device_ids=true | all-gather | bytes 921600 | tf_op jit(solution)/shard_map/all_gather | solution.py:152
  625.7 1.8 convolution_convert_fusion.1
  627.5 2.9 copy.106
  630.4 6.6 all-to-all-start.1
  637.0 73.4 %all-to-all-done.1 = bf16[64,10,1536]{2,1,0:T(8,128)(2,1)} async-done(((bf16[64,10,1536]{2,1,0:T(8,128)(2,1)}), bf16[64,10,1536]{2,1,0:T(8,128)(2,1)}, u32[]{:S(2)}, u32[]{:S(2)}) %all-to-all-start.1) | async-done | bytes 1966112 | tf_op jit(solution)/shard_map/all_to_all | solution.py:156
  710.4 2.6 convert_reduce_fusion
  713.0 2.9 fusion.9
  (59 shorter events, 2.6 us)
Async XLA Ops:
  6.5 619.2 %copy-start = (bf16[576,1536]{1,0:T(8,128)(2,1)S(1)}, bf16[576,1536]{1,0:T(8,128)(2,1)}, u32[]{:S(2)}) copy-start(bf16[576,1536]{1,0:T(8,128)(2,1)} %param.29) | copy-start | bytes 5308420
  6.5 107.9 %all-gather.7.cloned.1.call-start = ((), (), s32[]{:S(2)}) async-start(), calls=%async_computation.4 | async-start | bytes 17039360 | tf_op jit(solution)/shard_map/all_gather | solution.py:17
  10.8 193.0 %all-gather.5.cloned.1.call-start = ((), (), s32[]{:S(2)}) async-start(), calls=%async_computation.2 | async-start | bytes 12779520 | tf_op jit(solution)/shard_map/all_gather | solution.py:100
  12.5 263.9 %all-reduce.2.cloned.1.call-start = ((), (), s32[]{:S(2)}) async-start(), calls=%async_computation.3 | async-start | bytes 3145728 | tf_op jit(solution)/shard_map/psum | solution.py:104
  114.4 2.8 copy-start.5
  115.7 88.1 %copy-start.4 = (f32[1024]{0:T(1024)S(1)}, f32[1024]{0:T(1024)}, u32[]{:S(2)}) copy-start(f32[1024]{0:T(1024)} %param.21) | copy-start | bytes 12292
  203.7 20.6 %copy-start.7 = (s32[128,2]{0,1:T(2,128)S(1)}, s32[128,2]{0,1:T(2,128)}, u32[]{:S(2)}) copy-start(s32[128,2]{0,1:T(2,128)} %param.26) | copy-start | bytes 3076
  203.7 72.7 %copy-start.2 = (bf16[128,6144]{1,0:T(8,128)(2,1)S(1)}, bf16[128,6144]{1,0:T(8,128)(2,1)}, u32[]{:S(2)}) copy-start(bf16[128,6144]{1,0:T(8,128)(2,1)} %param.23) | copy-start | bytes 4718596
  225.9 54.3 %copy-start.6 = (f32[6144]{0:T(1024)S(1)}, f32[6144]{0:T(1024)}, u32[]{:S(2)}) copy-start(f32[6144]{0:T(1024)} %param.24) | copy-start | bytes 73732
  276.4 3.8 copy-start.3
  276.4 3.8 copy-start.9
  592.6 6.5 copy-start.1
  592.6 6.5 copy-start.8
  630.4 80.0 %all-to-all-start.1 = ((bf16[64,10,1536]{2,1,0:T(8,128)(2,1)}), bf16[64,10,1536]{2,1,0:T(8,128)(2,1)}, u32[]{:S(2)}, u32[]{:S(2)}) async-start(bf16[64,10,1536]{2,1,0:T(8,128)(2,1)} %copy.106), calls=%async_computation.1 | async-start | bytes 6291456 | tf_op jit(solution)/shard_map/all_to_all | solution.py:156
Sparse Core Ops, SparseCore 0:
  10.9 103.4 all-gather.6
  117.2 86.5 all-gather.4
  224.4 51.8 all-reduce.1
where the time goes:
time: 725 us; the launch traced here: 722 us
  blocking collectives  354 us (49%)
  waiting for transfers between devices  263 us (36%)
  matrix products  44.1 us (6%)
  local copies, waits for them, and re-layouts  31.4 us (4%)
  between operations  13.4 us (2%)
  other arithmetic  9.72 us (1%)
    all_to_all x1, blocking collectives, body(): lax.all_to_all(outgoing, 'ctx', split_axis=0, concat_axis=0, tiled=True)  287 us
    all_gather x1, waiting for transfers between devices, body(): row_whole = lax.all_gather(out_weight, 'ctx', axis=1, tiled=True)  84.2 us
    all_to_all x1, waiting for transfers between devices, body(): lax.all_to_all(partial_value, 'ctx', split_axis=0, concat_axis=0, tiled=T...  73.4 us
    all_gather x1, waiting for transfers between devices, prefix(): lax.all_gather(a.astype(kind), axis)  55.2 us
    psum x1, waiting for transfers between devices, body(): lax.psum(partial_sum.astype(jnp.bfloat16), 'head').astype(jnp.float32)  50.4 us
    all_gather x1, blocking collectives, prefix(): lax.all_gather(a.astype(kind), axis)  44.3 us
    all_gather x1, blocking collectives, body(): joined = lax.all_gather(hidden_units, 'head', axis=2, tiled=True)  22.7 us
    dot_general x1, matrix products, body(): jnp.einsum('thr,hrd->td', attn_mixed, row_whole, preferred_element_type=j...  20.6 us
  transfers between devices with their start and end apart: 4, of which 4 were waited for; matrix products, arithmetic and copies ran while one was open for 1% of the time, Pallas kernels for 0%

commit v1 on v0

--- a/solution.py
+++ b/solution.py
@@ -1,7 +1,7 @@
 import jax
 import jax.numpy as jnp
 from jax import lax
-from jax.sharding import PartitionSpec as P
+from jax.sharding import Mesh, PartitionSpec as P
 
 EXP = 8
 MOST = 10
@@ -11,28 +11,37 @@
 highest = lax.Precision.HIGHEST
 
 
-def prefix(value, axis, join, neutral):
-    place = lax.axis_index(axis)
-    gathered = jax.tree.map(
-        lambda a, kind: lax.all_gather(a.astype(kind), axis), value, (jnp.bfloat16, jnp.bfloat16)
-    )
-    state = jax.tree.map(lambda a, e: jnp.zeros_like(a) + jnp.asarray(e, a.dtype), value, neutral)
-
-    def one(hop, state):
-        return join(
-            state,
-            jax.tree.map(
-                lambda a, own: lax.dynamic_index_in_dim(a, hop, 0, False).astype(own.dtype),
-                gathered,
-                value,
-            ),
-        )
-
-    return lax.fori_loop(0, place, one, state)
+def chain_weights(factors, target):
+    count = factors.shape[0]
+    index = jnp.arange(count)
+    inside = (index[:, None] < index[None, :]) & (index[None, :] < target)
+    spans = jnp.prod(jnp.where(inside[:, :, None], factors[None, :, :], 1.0), axis=1)
+    return jnp.where((index < target)[:, None], spans, 0.0)
 
 
-def chain_combine(earlier, later):
-    return (earlier[0] * later[0], later[0][:, None, None] * earlier[1] + later[1])
+def pack_state(factor, state):
+    heads, dim, _ = state.shape
+    extra = jnp.broadcast_to(factor[:, None, None], (heads, 8, dim))
+    return jnp.concatenate([state, extra], axis=1).astype(jnp.bfloat16)
+
+
+def unpack_state(packed):
+    dim = packed.shape[-1]
+    return packed[..., dim, 0].astype(jnp.float32), packed[..., :dim, :].astype(jnp.float32)
+
+
+def group_scan(factor, state, axis):
+    place = lax.axis_index(axis)
+    count = lax.axis_size(axis)
+    factors, states = unpack_state(lax.all_gather(pack_state(factor, state), axis))
+    into = chain_weights(factors, place)
+    entering = jnp.einsum("kh,khde->hde", into, states, precision=highest)
+    whole = chain_weights(factors, count)
+    total_state = jnp.einsum("kh,khde->hde", whole, states, precision=highest)
+    index = jnp.arange(count)
+    before = jnp.prod(jnp.where((index < place)[:, None], factors, 1.0), axis=0)
+    total_factor = jnp.prod(factors, axis=0)
+    return before, entering, total_factor, total_state
 
 
 def body(
@@ -51,7 +60,7 @@
     expert_up,
     expert_down,
 ):
-    ctx_count = lax.axis_size("ctx")
+    ctx_count = lax.axis_size(("g", "j"))
     head_count = lax.axis_size("head")
     head_index = lax.axis_index("head")
     tok_rows = queries.shape[0]
@@ -70,11 +79,11 @@
     local_state = jnp.einsum(
         "thd,the->hde", keys_decayed, value_blocks, preferred_element_type=jnp.float32
     )
-    identity = (
-        jnp.ones((local_heads,), jnp.float32),
-        jnp.zeros((local_heads, head_dim, head_dim), jnp.float32),
+    before, inner_entering, group_factor, group_state = group_scan(
+        jnp.exp(block_total), local_state, "j"
     )
-    _, entering = prefix((jnp.exp(block_total), local_state), "ctx", chain_combine, identity)
+    _, outer_entering, _, _ = group_scan(group_factor, group_state, "g")
+    entering = before[:, None, None] * outer_entering + inner_entering
     sequence_offsets = jnp.arange(tok_rows)
     causal = (sequence_offsets[:, None] >= sequence_offsets[None, :])[None, :, :]
     cum_heads = cumulative.T
@@ -97,7 +106,7 @@
     attn_mixed = (
         attended * rms_scale * attn_gain.reshape(local_heads, head_dim) * gate_open
     ).astype(jnp.bfloat16)
-    row_whole = lax.all_gather(out_weight, "ctx", axis=1, tiled=True)
+    row_whole = lax.all_gather(out_weight, ("g", "j"), axis=1, tiled=True)
     partial_sum = jnp.einsum(
         "thr,hrd->td", attn_mixed, row_whole, preferred_element_type=jnp.float32
     )
@@ -118,8 +127,8 @@
     route_gates = jax.nn.sigmoid(picked - picked[:, ::-1])
     route_ids = expert_ids.reshape(-1)
     onehot = (route_ids[:, None] == jnp.arange(EXP, dtype=jnp.int32)[None, :]).astype(jnp.int32)
-    before = jnp.cumsum(onehot, axis=0) - onehot
-    slot_index = jnp.sum(before * onehot, axis=1)
+    before_count = jnp.cumsum(onehot, axis=0) - onehot
+    slot_index = jnp.sum(before_count * onehot, axis=1)
     slot_range = jnp.arange(MOST, dtype=jnp.int32)
     placed = (onehot.T[:, None, :] == 1) & (slot_index[None, None, :] == slot_range[None, :, None])
     chooser = (
@@ -139,10 +148,10 @@
         .astype(jnp.bfloat16)
         .reshape(EXP, MOST, model_width)
     )
-    outgoing = jnp.repeat(packed, group, axis=0)
-    arrived = lax.all_to_all(outgoing, "ctx", split_axis=0, concat_axis=0, tiled=True)
-    sources = arrived.shape[0]
-    slots_now = arrived.shape[1]
+    by_group = lax.all_to_all(packed, "g", split_axis=0, concat_axis=0, tiled=True)
+    arrived = lax.all_gather(by_group, "j", axis=1, tiled=False)
+    sources = arrived.shape[0] * arrived.shape[1]
+    slots_now = arrived.shape[2]
     flat_rows = arrived.reshape(sources * slots_now, model_width)
     gate_part = jnp.einsum("rd,fd->rf", flat_rows, expert_gate, preferred_element_type=jnp.float32)
     up_part = jnp.einsum("rd,fd->rf", flat_rows, expert_up, preferred_element_type=jnp.float32)
@@ -153,32 +162,38 @@
     partial_value = jnp.einsum(
         "nmf,fd->nmd", joined, expert_down, preferred_element_type=jnp.float32
     ).astype(jnp.bfloat16)
-    returned = lax.all_to_all(partial_value, "ctx", split_axis=0, concat_axis=0, tiled=True)
+    returned = lax.all_to_all(partial_value, ("g", "j"), split_axis=0, concat_axis=0, tiled=True)
     summed = jnp.sum(returned.astype(jnp.float32).reshape(EXP, group, MOST, share_width), axis=1)
     mixture = jnp.einsum("est,esd->td", weighted, summed, precision=highest)
     return (hidden_share + mixture).astype(jnp.bfloat16)
 
 
 def solution(mesh):
+    ctx_count = mesh.shape["ctx"]
+    head_count = mesh.shape["head"]
+    split = Mesh(
+        mesh.devices.reshape(EXP, ctx_count // EXP, head_count), ("g", "j", "head")
+    )
+    ctx = ("g", "j")
     return jax.shard_map(
         body,
-        mesh=mesh,
+        mesh=split,
         in_specs=(
-            P("ctx", "head"),
-            P("ctx", "head"),
-            P("ctx", "head"),
-            P("ctx", "head"),
-            P("ctx", "head"),
+            P(ctx, "head"),
+            P(ctx, "head"),
+            P(ctx, "head"),
+            P(ctx, "head"),
+            P(ctx, "head"),
             P("head"),
-            P("head", "ctx", None),
-            P("ctx", None),
+            P("head", ctx, None),
+            P(ctx, None),
             P(),
             P(),
-            P("ctx", None),
-            P(("ctx", "head"), None),
-            P(("ctx", "head"), None),
-            P("ctx", "head"),
+            P(ctx, None),
+            P(("g", "j", "head"), None),
+            P(("g", "j", "head"), None),
+            P(ctx, "head"),
         ),
-        out_specs=P("ctx", "head"),
+        out_specs=P(ctx, "head"),
         check_vma=False,
     )

time: 725 us -> 586 us (0.81)
  blocking collectives: 354 us -> 62.8 us
  waiting for transfers between devices: 263 us -> 410 us
  local copies, waits for them, and re-layouts: 31.4 us -> 22.8 us
    all_to_all x1, blocking collectives: 287 us -> 41.2 us  [body(): lax.all_to_all(packed, 'g', split_axis=0, concat_axis=0, tiled=True)]
    all_gather x2 -> x4, waiting for transfers between devices: 139 us -> 286 us  [the longest x2 112 us: group_scan(): lax.all_gather(pack_state(factor, state), axis)]
    all_gather x1 -> x0, blocking collectives: 44.3 us -> none  [prefix(): lax.all_gather(a.astype(kind), axis)]
    reshape x1 -> x0, local copies, waits for them, and re-layouts: 13.8 us -> none  [body(): flat_rows = arrived.reshape(sources * slots_now, model_width)]
    all_gather x0 -> x1, local copies, waits for them, and re-layouts: none -> 7.53 us  [body(): arrived = lax.all_gather(by_group, 'j', axis=1, tiled=False)]
  transfers between devices with their start and end apart: 4 -> 6, of which waited for: 4 -> 6; matrix products, arithmetic and copies ran while one was open for 1% -> 2% of each run, Pallas kernels for 0% -> 0%
where the time goes in v1:
time: 586 us; the launch traced here: 582 us
  waiting for transfers between devices  410 us (70%)
  blocking collectives  62.8 us (11%)
  matrix products  43.9 us (7%)
  local copies, waits for them, and re-layouts  22.8 us (4%)
  other arithmetic  14.9 us (3%)
  between operations  13.8 us (2%)
  starting transfers between devices  13.5 us (2%)
    all_gather x2, waiting for transfers between devices, group_scan(): lax.all_gather(pack_state(factor, state), axis)  112 us
    all_gather x1, waiting for transfers between devices, body(): arrived = lax.all_gather(by_group, 'j', axis=1, tiled=False)  90.1 us
    all_gather x1, waiting for transfers between devices, body(): row_whole = lax.all_gather(out_weight, ('g', 'j'), axis=1, tiled=True)  84.7 us
    all_to_all x1, waiting for transfers between devices, body(): lax.all_to_all(partial_value, ('g', 'j'), split_axis=0, concat_axis=0, ti...  73.4 us
    psum x1, waiting for transfers between devices, body(): lax.psum(partial_sum.astype(jnp.bfloat16), 'head').astype(jnp.float32)  50.4 us
    all_to_all x1, blocking collectives, body(): lax.all_to_all(packed, 'g', split_axis=0, concat_axis=0, tiled=True)  41.2 us
    all_gather x1, blocking collectives, body(): joined = lax.all_gather(hidden_units, 'head', axis=2, tiled=True)  21.6 us
    dot_general x1, matrix products, body(): jnp.einsum('thr,hrd->td', attn_mixed, row_whole, preferred_element_type=j...  20.2 us
  transfers between devices with their start and end apart: 6, of which 6 were waited for; matrix products, arithmetic and copies ran while one was open for 2% of the time, Pallas kernels for 0%

profile of v1, /device:TPU:1, one launch (start us, length us, event | category | flops | bytes accessed | tf_op | source)
XLA Modules:
  0.0 582.1 jit_solution(9805344236142896750)
XLA Ops:
  7.7 1.1 copy.182
  8.9 1.3 fusion.19
  11.1 41.6 %all-gather.6.cloned.1.call-done = bf16[8,8,136,128]{3,2,1,0:T(8,128)(2,1)} async-done(((bf16[1,8,136,128]{3,2,1,0:T(8,128)(2,1)}), bf16[8,8,136,128]{3,2,1,0:T(8,128)(2,1)}) %all-gather.6.cloned.1.call-update) | async-done | bytes 2228240 | tf_op jit(solution)/shard_map/all_gather | solution.py:36
  52.7 1.1 slice_reduce_fusion.1
  54.2 1.6 slice-done
  55.8 2.5 fusion.10
  60.9 1.0 copy.140
  62.0 2.1 multiply_reduce_fusion
  64.3 70.0 %all-gather.8.cloned.1.call-done = bf16[8,8,136,128]{3,2,1,0:T(8,128)(2,1)} async-done(((bf16[1,8,136,128]{3,2,1,0:T(8,128)(2,1)}), bf16[8,8,136,128]{3,2,1,0:T(8,128)(2,1)}) %all-gather.8.cloned.1.call-update) | async-done | bytes 2228240 | tf_op jit(solution)/shard_map/all_gather | solution.py:36
  134.3 0.9 slice.31
  135.6 2.1 multiply_reduce_fusion.1
  137.9 2.5 fusion.16
  140.4 1.8 multiply_reduce_fusion.3
  142.2 84.7 %all-gather.10.cloned.1.call-done = bf16[8,128,6144]{2,0,1:T(8,128)(2,1)} async-done(((bf16[8,2,6144]{2,0,1:T(8,128)(2,1)}), bf16[8,128,6144]{2,0,1:T(8,128)(2,1)}) %all-gather.10.cloned.1.call-update) | async-done | bytes 12582928 | tf_op jit(solution)/shard_map/all_gather | solution.py:109
  227.0 20.2 %fusion.5 = bf16[128,6144]{1,0:T(8,128)(2,1)} fusion(bf16[8,128,6144]{2,0,1:T(8,128)(2,1)} %all-gather.10.cloned.1.call-done, f32[128,8,128]{0,2,1:T(8,128)S(1)} %bitcast.109, f32[128,8,128]{0,2,1:T(8,128)S(1)} %get-tuple-element.18, f32[8,128]{1,0:T(8,128)S(1)} %bitcast.113, f32[128,8]{0,1:T(8,128)S(1)} %add_rsqrt_fusion), kind=kOutput, calls=%fused_computation.3 | convolution fusion | flops 1611923456 | bytes 15212544 | tf_op jit(solution)/shard_map/thr,hrd->td/dot_general | solution.py:110
  248.9 50.4 %all-reduce.2.cloned.1.call-done = bf16[128,6144]{1,0:T(8,128)(2,1)} async-done(((bf16[128,6144]{1,0:T(8,128)(2,1)}), bf16[128,6144]{1,0:T(8,128)(2,1)}) %all-reduce.2.cloned.1.call-update) | async-done | bytes 1572880 | tf_op jit(solution)/shard_map/psum | solution.py:113
  299.3 3.8 convert_add_fusion
  304.1 3.2 convolution_convert_fusion
  307.3 1.4 reshape.335
  308.7 41.2 %all_to_all.10 = bf16[8,10,6144]{2,1,0:T(8,128)(2,1)S(1)} all-to-all(bf16[8,10,6144]{2,1,0:T(8,128)(2,1)S(1)} %reshape.335), channel_id=1, replica_groups=mesh['g'=8,'j'=8,'head'=4] {'g'}, dimensions={0} | all-to-all | bytes 1966080 | tf_op jit(solution)/shard_map/all_to_all | solution.py:151
  349.9 1.5 copy.148
  351.4 90.1 %all-gather.12.cloned.1.call-done = bf16[8,80,6144]{2,0,1:T(8,128)(2,1)} async-done(((bf16[8,10,6144]{2,0,1:T(8,128)(2,1)}), bf16[8,80,6144]{2,0,1:T(8,128)(2,1)}) %all-gather.12.cloned.1.call-update) | async-done | bytes 7864336 | tf_op jit(solution)/shard_map/all_gather | solution.py:152
  441.5 7.5 %copy.149 = bf16[8,80,6144]{2,1,0:T(8,128)(2,1)S(1)} copy(bf16[8,80,6144]{2,0,1:T(8,128)(2,1)} %all-gather.12.cloned.1.call-done) | data formatting | bytes 15728640 | tf_op jit(solution)/shard_map/all_gather | solution.py:152
  449.1 4.3 fusion.57
  453.4 2.6 fusion.18
  457.3 21.6 %all_gather.25 = bf16[64,10,576]{0,1,2:T(8,128)(2,1)S(1)} all-gather(bf16[64,10,144]{0,1,2:T(8,128)(2,1)S(1)} %copy.151), channel_id=1, replica_groups=mesh['g'=8,'j'=8,'head'=4] {'head'}, dimensions={2}, use_global_device_ids=true | all-gather | bytes 921600 | tf_op jit(solution)/shard_map/all_gather | solution.py:161
  478.9 1.8 convolution_convert_fusion.1
  480.7 2.9 copy.153
  483.6 12.8 %all-to-all-start.1 = ((bf16[64,10,1536]{2,1,0:T(8,128)(2,1)}), bf16[64,10,1536]{2,1,0:T(8,128)(2,1)}, u32[]{:S(2)}, u32[]{:S(2)}) async-start(bf16[64,10,1536]{2,1,0:T(8,128)(2,1)} %copy.153), calls=%async_computation.1 | async-start | bytes 6291456 | tf_op jit(solution)/shard_map/all_to_all | solution.py:165
  496.4 73.4 %all-to-all-done.1 = bf16[64,10,1536]{2,1,0:T(8,128)(2,1)} async-done(((bf16[64,10,1536]{2,1,0:T(8,128)(2,1)}), bf16[64,10,1536]{2,1,0:T(8,128)(2,1)}, u32[]{:S(2)}, u32[]{:S(2)}) %all-to-all-start.1) | async-done | bytes 1966112 | tf_op jit(solution)/shard_map/all_to_all | solution.py:165
  569.8 2.6 convert_reduce_fusion
  572.4 2.9 fusion.9
  (93 shorter events, 9.6 us)
Async XLA Ops:
  6.5 472.4 %copy-start = (bf16[576,1536]{1,0:T(8,128)(2,1)S(1)}, bf16[576,1536]{1,0:T(8,128)(2,1)}, u32[]{:S(2)}) copy-start(bf16[576,1536]{1,0:T(8,128)(2,1)} %param.27) | copy-start | bytes 5308420
  6.5 46.1 %all-gather.6.cloned.1.call-start = ((), (), s32[]{:S(2)}) async-start(), calls=%async_computation.2 | async-start | bytes 2506752 | tf_op jit(solution)/shard_map/all_gather | solution.py:36
  8.9 45.3 %copy-start.4 = (bf16[128,1024]{0,1:T(8,128)(2,1)}, bf16[128,1024]{0,1:T(8,128)(2,1)S(1)}, u32[]{:S(2)}) copy-start(bf16[128,1024]{0,1:T(8,128)(2,1)S(1)} %copy.182) | copy-start | bytes 786436
  11.0 123.3 %all-gather.8.cloned.1.call-start = ((), (), s32[]{:S(2)}) async-start(), calls=%async_computation.3 | async-start | bytes 2506752 | tf_op jit(solution)/shard_map/all_gather | solution.py:36
  54.2 1.6 slice-start
  55.8 3.4 copy-start.7
  55.8 4.9 copy-start.6
  59.2 167.8 %all-gather.10.cloned.1.call-start = ((), (), s32[]{:S(2)}) async-start(), calls=%async_computation.4 | async-start | bytes 12779520 | tf_op jit(solution)/shard_map/all_gather | solution.py:109
  60.0 239.3 %all-reduce.2.cloned.1.call-start = ((), (), s32[]{:S(2)}) async-start(), calls=%async_computation.5 | async-start | bytes 3145728 | tf_op jit(solution)/shard_map/psum | solution.py:113
  137.9 89.1 %copy-start.3 = (f32[128,1024]{0,1:T(8,128)S(1)}, f32[128,1024]{0,1:T(8,128)}, u32[]{:S(2)}) copy-start(f32[128,1024]{0,1:T(8,128)} %copy.140) | copy-start | bytes 1572868
  137.9 89.1 %copy-start.5 = (f32[1024]{0:T(1024)S(1)}, f32[1024]{0:T(1024)}, u32[]{:S(2)}) copy-start(f32[1024]{0:T(1024)} %param.19) | copy-start | bytes 12292
  227.0 20.3 %copy-start.9 = (s32[128,2]{0,1:T(2,128)S(1)}, s32[128,2]{0,1:T(2,128)}, u32[]{:S(2)}) copy-start(s32[128,2]{0,1:T(2,128)} %param.24) | copy-start | bytes 3076
  247.2 52.1 %copy-start.1 = (bf16[128,6144]{1,0:T(8,128)(2,1)S(1)}, bf16[128,6144]{1,0:T(8,128)(2,1)}, u32[]{:S(2)}) copy-start(bf16[128,6144]{1,0:T(8,128)(2,1)} %param.21) | copy-start | bytes 4718596
  247.2 194.3 %all-gather.12.cloned.1.call-start = ((), (), s32[]{:S(2)}) async-start(), calls=%async_computation.6 | async-start | bytes 8847360 | tf_op jit(solution)/shard_map/all_gather | solution.py:152
  248.8 54.3 %copy-start.8 = (f32[6144]{0:T(1024)S(1)}, f32[6144]{0:T(1024)}, u32[]{:S(2)}) copy-start(f32[6144]{0:T(1024)} %param.22) | copy-start | bytes 73732
  299.3 3.8 copy-start.2
  299.3 3.8 copy-start.11
  449.1 4.3 copy-start.10
  483.6 86.2 %all-to-all-start.1 = ((bf16[64,10,1536]{2,1,0:T(8,128)(2,1)}), bf16[64,10,1536]{2,1,0:T(8,128)(2,1)}, u32[]{:S(2)}, u32[]{:S(2)}) async-start(bf16[64,10,1536]{2,1,0:T(8,128)(2,1)} %copy.153), calls=%async_computation.1 | async-start | bytes 6291456 | tf_op jit(solution)/shard_map/all_to_all | solution.py:165
Sparse Core Ops, SparseCore 0:
  11.1 41.5 all-gather.5
  59.3 74.9 all-gather.7
  137.1 89.8 all-gather.9
  247.3 51.9 all-reduce.1
  351.5 89.9 all-gather.11

commit v2 on v1

--- a/solution.py
+++ b/solution.py
@@ -11,37 +11,36 @@
 highest = lax.Precision.HIGHEST
 
 
-def chain_weights(factors, target):
-    count = factors.shape[0]
-    index = jnp.arange(count)
-    inside = (index[:, None] < index[None, :]) & (index[None, :] < target)
-    spans = jnp.prod(jnp.where(inside[:, :, None], factors[None, :, :], 1.0), axis=1)
-    return jnp.where((index < target)[:, None], spans, 0.0)
-
-
 def pack_state(factor, state):
     heads, dim, _ = state.shape
     extra = jnp.broadcast_to(factor[:, None, None], (heads, 8, dim))
-    return jnp.concatenate([state, extra], axis=1).astype(jnp.bfloat16)
+    return jnp.concatenate([state, extra], axis=1)
 
 
 def unpack_state(packed):
     dim = packed.shape[-1]
-    return packed[..., dim, 0].astype(jnp.float32), packed[..., :dim, :].astype(jnp.float32)
+    return packed[:, dim, 0], packed[:, :dim, :]
 
 
-def group_scan(factor, state, axis):
+def prefix_scan(factor, state, axis, count):
     place = lax.axis_index(axis)
-    count = lax.axis_size(axis)
-    factors, states = unpack_state(lax.all_gather(pack_state(factor, state), axis))
-    into = chain_weights(factors, place)
-    entering = jnp.einsum("kh,khde->hde", into, states, precision=highest)
-    whole = chain_weights(factors, count)
-    total_state = jnp.einsum("kh,khde->hde", whole, states, precision=highest)
-    index = jnp.arange(count)
-    before = jnp.prod(jnp.where((index < place)[:, None], factors, 1.0), axis=0)
-    total_factor = jnp.prod(factors, axis=0)
-    return before, entering, total_factor, total_state
+
+    def shift(value, distance):
+        return lax.ppermute(value, axis, [(i, i + distance) for i in range(count - distance)])
+
+    identity = pack_state(jnp.ones_like(factor), jnp.zeros_like(state))
+    current = jnp.where(place >= 1, shift(pack_state(factor, state), 1), identity)
+    distance = 1
+    while distance < count:
+        earlier_factor, earlier_state = unpack_state(shift(current, distance))
+        later_factor, later_state = unpack_state(current)
+        joined = pack_state(
+            earlier_factor * later_factor,
+            later_factor[:, None, None] * earlier_state + later_state,
+        )
+        current = jnp.where(place >= distance, joined, current)
+        distance *= 2
+    return unpack_state(current)[1]
 
 
 def body(
@@ -79,11 +78,7 @@
     local_state = jnp.einsum(
         "thd,the->hde", keys_decayed, value_blocks, preferred_element_type=jnp.float32
     )
-    before, inner_entering, group_factor, group_state = group_scan(
-        jnp.exp(block_total), local_state, "j"
-    )
-    _, outer_entering, _, _ = group_scan(group_factor, group_state, "g")
-    entering = before[:, None, None] * outer_entering + inner_entering
+    entering = prefix_scan(jnp.exp(block_total), local_state, ("g", "j"), ctx_count)
     sequence_offsets = jnp.arange(tok_rows)
     causal = (sequence_offsets[:, None] >= sequence_offsets[None, :])[None, :, :]
     cum_heads = cumulative.T

time: 586 us -> 548 us (0.935)
  waiting for transfers between devices: 410 us -> 340 us
  starting transfers between devices: 13.5 us -> 53 us
    all_gather x2 -> x0, waiting for transfers between devices: 112 us -> none  [group_scan(): lax.all_gather(pack_state(factor, state), axis)]
    ppermute x0 -> x7, waiting for transfers between devices: none -> 105 us  [shift(): lax.ppermute(value, axis, [(i, i + distance) for i in range(count - dista...]
    all_gather x1, waiting for transfers between devices: 84.7 us -> 0.02 us  [body(): row_whole = lax.all_gather(out_weight, ('g', 'j'), axis=1, tiled=True)]
    ppermute x0 -> x7, starting transfers between devices: none -> 40.1 us  [shift(): lax.ppermute(value, axis, [(i, i + distance) for i in range(count - dista...]
    psum x1, waiting for transfers between devices: 50.4 us -> 71.4 us  [body(): lax.psum(partial_sum.astype(jnp.bfloat16), 'head').astype(jnp.float32)]
  transfers between devices with their start and end apart: 6 -> 11, of which waited for: 6 -> 10; matrix products, arithmetic and copies ran while one was open for 2% -> 3% of each run, Pallas kernels for 0% -> 0%
where the time goes in v2:
time: 548 us; the launch traced here: 544 us
  waiting for transfers between devices  340 us (62%)
  blocking collectives  62.8 us (11%)
  starting transfers between devices  53 us (10%)
  matrix products  41.1 us (8%)
  local copies, waits for them, and re-layouts  20.9 us (4%)
  between operations  13.8 us (3%)
  other arithmetic  12.9 us (2%)
    ppermute x7, waiting for transfers between devices, shift(): lax.ppermute(value, axis, [(i, i + distance) for i in range(count - dista...  105 us
    all_gather x1, waiting for transfers between devices, body(): arrived = lax.all_gather(by_group, 'j', axis=1, tiled=False)  90.1 us
    all_to_all x1, waiting for transfers between devices, body(): lax.all_to_all(partial_value, ('g', 'j'), split_axis=0, concat_axis=0, ti...  73.4 us
    psum x1, waiting for transfers between devices, body(): lax.psum(partial_sum.astype(jnp.bfloat16), 'head').astype(jnp.float32)  71.4 us
    all_to_all x1, blocking collectives, body(): lax.all_to_all(packed, 'g', split_axis=0, concat_axis=0, tiled=True)  41.2 us
    ppermute x7, starting transfers between devices, shift(): lax.ppermute(value, axis, [(i, i + distance) for i in range(count - dista...  40.1 us
    all_gather x1, blocking collectives, body(): joined = lax.all_gather(hidden_units, 'head', axis=2, tiled=True)  21.6 us
    dot_general x1, matrix products, body(): jnp.einsum('thr,hrd->td', attn_mixed, row_whole, preferred_element_type=j...  20.2 us
  transfers between devices with their start and end apart: 11, of which 10 were waited for; matrix products, arithmetic and copies ran while one was open for 3% of the time, Pallas kernels for 0%

profile of v2, /device:TPU:1, one launch (start us, length us, event | category | flops | bytes accessed | tf_op | source)
XLA Modules:
  0.0 544.4 jit_solution(7572002795783939130)
XLA Ops:
  6.5 1.8 copy.120
  12.6 4.9 collective-permute-start
  17.6 6.4 %collective-permute-done = f32[8,136,128]{2,1,0:T(8,128)S(1)} collective-permute-done((f32[8,136,128]{2,1,0:T(8,128)S(1)}, f32[8,136,128]{2,1,0:T(8,128)S(1)}, u32[]{:S(2)}, u32[]{:S(2)}) %collective-permute-start) | collective-permute-done | bytes 557088 | tf_op jit(solution)/shard_map/ppermute | solution.py:29
  24.1 4.4 collective-permute-start.1
  28.5 7.9 %collective-permute-done.1 = f32[8,136,128]{2,1,0:T(8,128)S(1)} collective-permute-done((f32[8,136,128]{2,1,0:T(8,128)S(1)}, f32[8,136,128]{2,1,0:T(8,128)S(1)}, u32[]{:S(2)}, u32[]{:S(2)}) %collective-permute-start.1) | collective-permute-done | bytes 557088 | tf_op jit(solution)/shard_map/ppermute | solution.py:29
  36.8 4.3 collective-permute-start.2
  41.1 15.8 %collective-permute-done.2 = f32[8,136,128]{2,1,0:T(8,128)S(1)} collective-permute-done((f32[8,136,128]{2,1,0:T(8,128)S(1)}, f32[8,136,128]{2,1,0:T(8,128)S(1)}, u32[]{:S(2)}, u32[]{:S(2)}) %collective-permute-start.2) | collective-permute-done | bytes 557088 | tf_op jit(solution)/shard_map/ppermute | solution.py:29
  57.3 5.2 collective-permute-start.3
  62.5 32.9 %collective-permute-done.3 = f32[8,136,128]{2,1,0:T(8,128)S(1)} collective-permute-done((f32[8,136,128]{2,1,0:T(8,128)S(1)}, f32[8,136,128]{2,1,0:T(8,128)S(1)}, u32[]{:S(2)}, u32[]{:S(2)}) %collective-permute-start.3) | collective-permute-done | bytes 557088 | tf_op jit(solution)/shard_map/ppermute | solution.py:29
  95.8 4.9 collective-permute-start.4
  100.7 30.8 %collective-permute-done.4 = f32[8,136,128]{2,1,0:T(8,128)S(1)} collective-permute-done((f32[8,136,128]{2,1,0:T(8,128)S(1)}, f32[8,136,128]{2,1,0:T(8,128)S(1)}, u32[]{:S(2)}, u32[]{:S(2)}) %collective-permute-start.4) | collective-permute-done | bytes 557088 | tf_op jit(solution)/shard_map/ppermute | solution.py:29
  131.9 3.6 collective-permute-start.5
  135.5 8.1 %collective-permute-done.5 = f32[8,136,128]{2,1,0:T(8,128)S(1)} collective-permute-done((f32[8,136,128]{2,1,0:T(8,128)S(1)}, f32[8,136,128]{2,1,0:T(8,128)S(1)}, u32[]{:S(2)}, u32[]{:S(2)}) %collective-permute-start.5) | collective-permute-done | bytes 557088 | tf_op jit(solution)/shard_map/ppermute | solution.py:29
  144.0 12.9 %collective-permute-start.6 = (f32[8,136,128]{2,1,0:T(8,128)S(1)}, f32[8,136,128]{2,1,0:T(8,128)}, u32[]{:S(2)}, u32[]{:S(2)}) collective-permute-start(f32[8,136,128]{2,1,0:T(8,128)S(1)} %maximum_select_fusion.4), channel_id=1, source_target_pairs={{0,128},{4,132},{8,136},{12,140},{16,144},{20,148},{24,152},{28,15... | collective-permute-start | bytes 1671176 | tf_op jit(solution)/shard_map/ppermute | solution.py:29
  159.2 2.8 collective-permute-done.6
  164.2 2.4 fusion.14
  168.3 20.2 %fusion.5 = bf16[128,6144]{1,0:T(8,128)(2,1)} fusion(bf16[8,128,6144]{2,0,1:T(8,128)(2,1)} %all-gather.4.cloned.1.call-done, f32[128,8,128]{0,2,1:T(8,128)S(1)} %bitcast.81, f32[128,8,128]{0,2,1:T(8,128)S(1)} %get-tuple-element.24, f32[8,128]{1,0:T(8,128)S(1)} %bitcast.85, f32[128,8]{0,1:T(8,128)S(1)} %add_rsqrt_fusion), kind=kOutput, calls=%fused_computation.3 | convolution fusion | flops 1611923456 | bytes 15212544 | tf_op jit(solution)/shard_map/thr,hrd->td/dot_general | solution.py:105
  190.2 71.4 %all-reduce.3.cloned.1.call-done = bf16[128,6144]{1,0:T(8,128)(2,1)} async-done(((bf16[128,6144]{1,0:T(8,128)(2,1)}), bf16[128,6144]{1,0:T(8,128)(2,1)}) %all-reduce.3.cloned.1.call-update) | async-done | bytes 1572880 | tf_op jit(solution)/shard_map/psum | solution.py:108
  261.6 3.8 convert_add_fusion
  266.3 3.2 convolution_convert_fusion
  271.0 41.2 %all_to_all.10 = bf16[8,10,6144]{2,1,0:T(8,128)(2,1)S(1)} all-to-all(bf16[8,10,6144]{2,1,0:T(8,128)(2,1)S(1)} %reshape.176), channel_id=1, replica_groups=mesh['g'=8,'j'=8,'head'=4] {'g'}, dimensions={0} | all-to-all | bytes 1966080 | tf_op jit(solution)/shard_map/all_to_all | solution.py:146
  313.7 90.1 %all-gather.6.cloned.1.call-done = bf16[8,80,6144]{2,0,1:T(8,128)(2,1)} async-done(((bf16[8,10,6144]{2,0,1:T(8,128)(2,1)}), bf16[8,80,6144]{2,0,1:T(8,128)(2,1)}) %all-gather.6.cloned.1.call-update) | async-done | bytes 7864336 | tf_op jit(solution)/shard_map/all_gather | solution.py:147
  403.8 7.5 %copy.128 = bf16[8,80,6144]{2,1,0:T(8,128)(2,1)S(1)} copy(bf16[8,80,6144]{2,0,1:T(8,128)(2,1)} %all-gather.6.cloned.1.call-done) | data formatting | bytes 15728640 | tf_op jit(solution)/shard_map/all_gather | solution.py:147
  411.3 4.3 fusion.63
  415.7 2.6 fusion.16
  419.6 21.6 %all_gather.15 = bf16[64,10,576]{0,1,2:T(8,128)(2,1)S(1)} all-gather(bf16[64,10,144]{0,1,2:T(8,128)(2,1)S(1)} %copy.130), channel_id=1, replica_groups=mesh['g'=8,'j'=8,'head'=4] {'head'}, dimensions={2}, use_global_device_ids=true | all-gather | bytes 921600 | tf_op jit(solution)/shard_map/all_gather | solution.py:156
  441.2 1.8 convolution_convert_fusion.1
  443.0 2.9 copy.132
  445.9 12.8 %all-to-all-start.1 = ((bf16[64,10,1536]{2,1,0:T(8,128)(2,1)}), bf16[64,10,1536]{2,1,0:T(8,128)(2,1)}, u32[]{:S(2)}, u32[]{:S(2)}) async-start(bf16[64,10,1536]{2,1,0:T(8,128)(2,1)} %copy.132), calls=%async_computation.1 | async-start | bytes 6291456 | tf_op jit(solution)/shard_map/all_to_all | solution.py:160
  458.7 73.4 %all-to-all-done.1 = bf16[64,10,1536]{2,1,0:T(8,128)(2,1)} async-done(((bf16[64,10,1536]{2,1,0:T(8,128)(2,1)}), bf16[64,10,1536]{2,1,0:T(8,128)(2,1)}, u32[]{:S(2)}, u32[]{:S(2)}) %all-to-all-start.1) | async-done | bytes 1966112 | tf_op jit(solution)/shard_map/all_to_all | solution.py:160
  532.1 2.6 convert_reduce_fusion
  534.7 2.9 fusion.9
  (95 shorter events, 19.2 us)
Async XLA Ops:
  6.5 434.6 %copy-start = (bf16[576,1536]{1,0:T(8,128)(2,1)S(1)}, bf16[576,1536]{1,0:T(8,128)(2,1)}, u32[]{:S(2)}) copy-start(bf16[576,1536]{1,0:T(8,128)(2,1)} %param.27) | copy-start | bytes 5308420
  6.5 161.7 %all-gather.4.cloned.1.call-start = ((), (), s32[]{:S(2)}) async-start(), calls=%async_computation.2 | async-start | bytes 12779520 | tf_op jit(solution)/shard_map/all_gather | solution.py:104
  8.4 253.2 %all-reduce.3.cloned.1.call-start = ((), (), s32[]{:S(2)}) async-start(), calls=%async_computation.3 | async-start | bytes 3145728 | tf_op jit(solution)/shard_map/psum | solution.py:108
  11.2 1.4 copy-start.3
  12.6 11.4 %collective-permute-start = (f32[8,136,128]{2,1,0:T(8,128)S(1)}, f32[8,136,128]{2,1,0:T(8,128)S(1)}, u32[]{:S(2)}, u32[]{:S(2)}) collective-permute-start(f32[8,136,128]{2,1,0:T(8,128)S(1)} %pad_maximum_fusion), channel_id=1, source_target_pairs={{0,4},{4,8},{8,12},{12,16},{16,20},{20,24},{24,28},{28,32},{32,36}... | collective-permute-start | bytes 1671176 | tf_op jit(solution)/shard_map/ppermute | solution.py:29
  24.1 12.3 %collective-permute-start.1 = (f32[8,136,128]{2,1,0:T(8,128)S(1)}, f32[8,136,128]{2,1,0:T(8,128)S(1)}, u32[]{:S(2)}, u32[]{:S(2)}) collective-permute-start(f32[8,136,128]{2,1,0:T(8,128)S(1)} %pad_select_fusion), channel_id=1, source_target_pairs={{0,4},{4,8},{8,12},{12,16},{16,20},{20,24},{24,28},{28,32},{32,36}... | collective-permute-start | bytes 1671176 | tf_op jit(solution)/shard_map/ppermute | solution.py:29
  36.8 20.1 %collective-permute-start.2 = (f32[8,136,128]{2,1,0:T(8,128)S(1)}, f32[8,136,128]{2,1,0:T(8,128)S(1)}, u32[]{:S(2)}, u32[]{:S(2)}) collective-permute-start(f32[8,136,128]{2,1,0:T(8,128)S(1)} %maximum_select_fusion), channel_id=1, source_target_pairs={{0,8},{4,12},{8,16},{12,20},{16,24},{20,28},{24,32},{28,36},{32,40... | collective-permute-start | bytes 1671176 | tf_op jit(solution)/shard_map/ppermute | solution.py:29
  57.3 38.2 %collective-permute-start.3 = (f32[8,136,128]{2,1,0:T(8,128)S(1)}, f32[8,136,128]{2,1,0:T(8,128)S(1)}, u32[]{:S(2)}, u32[]{:S(2)}) collective-permute-start(f32[8,136,128]{2,1,0:T(8,128)S(1)} %maximum_select_fusion.1), channel_id=1, source_target_pairs={{0,16},{4,20},{8,24},{12,28},{16,32},{20,36},{24,40},{28,44},{32,4... | collective-permute-start | bytes 1671176 | tf_op jit(solution)/shard_map/ppermute | solution.py:29
  95.8 35.6 %collective-permute-start.4 = (f32[8,136,128]{2,1,0:T(8,128)S(1)}, f32[8,136,128]{2,1,0:T(8,128)S(1)}, u32[]{:S(2)}, u32[]{:S(2)}) collective-permute-start(f32[8,136,128]{2,1,0:T(8,128)S(1)} %maximum_select_fusion.2), channel_id=1, source_target_pairs={{0,32},{4,36},{8,40},{12,44},{16,48},{20,52},{24,56},{28,60},{32,6... | collective-permute-start | bytes 1671176 | tf_op jit(solution)/shard_map/ppermute | solution.py:29
  131.9 11.7 %collective-permute-start.5 = (f32[8,136,128]{2,1,0:T(8,128)S(1)}, f32[8,136,128]{2,1,0:T(8,128)S(1)}, u32[]{:S(2)}, u32[]{:S(2)}) collective-permute-start(f32[8,136,128]{2,1,0:T(8,128)S(1)} %maximum_select_fusion.3), channel_id=1, source_target_pairs={{0,64},{4,68},{8,72},{12,76},{16,80},{20,84},{24,88},{28,92},{32,9... | collective-permute-start | bytes 1671176 | tf_op jit(solution)/shard_map/ppermute | solution.py:29
  144.0 18.0 %collective-permute-start.6 = (f32[8,136,128]{2,1,0:T(8,128)S(1)}, f32[8,136,128]{2,1,0:T(8,128)}, u32[]{:S(2)}, u32[]{:S(2)}) collective-permute-start(f32[8,136,128]{2,1,0:T(8,128)S(1)} %maximum_select_fusion.4), channel_id=1, source_target_pairs={{0,128},{4,132},{8,136},{12,140},{16,144},{20,148},{24,152},{28,15... | collective-permute-start | bytes 1671176 | tf_op jit(solution)/shard_map/ppermute | solution.py:29
  159.2 7.4 %copy-start.4 = (bf16[128,1024]{0,1:T(8,128)(2,1)S(1)}, bf16[128,1024]{0,1:T(8,128)(2,1)}, u32[]{:S(2)}) copy-start(bf16[128,1024]{0,1:T(8,128)(2,1)} %copy-done.3) | copy-start | bytes 786436
  164.1 4.2 copy-start.5
  168.3 20.3 %copy-start.7 = (s32[128,2]{0,1:T(2,128)S(1)}, s32[128,2]{0,1:T(2,128)}, u32[]{:S(2)}) copy-start(s32[128,2]{0,1:T(2,128)} %param.24) | copy-start | bytes 3076
  188.5 73.1 %copy-start.1 = (bf16[128,6144]{1,0:T(8,128)(2,1)S(1)}, bf16[128,6144]{1,0:T(8,128)(2,1)}, u32[]{:S(2)}) copy-start(bf16[128,6144]{1,0:T(8,128)(2,1)} %param.21) | copy-start | bytes 4718596
  188.5 215.3 %all-gather.6.cloned.1.call-start = ((), (), s32[]{:S(2)}) async-start(), calls=%async_computation.4 | async-start | bytes 8847360 | tf_op jit(solution)/shard_map/all_gather | solution.py:147
  190.2 75.2 %copy-start.6 = (f32[6144]{0:T(1024)S(1)}, f32[6144]{0:T(1024)}, u32[]{:S(2)}) copy-start(f32[6144]{0:T(1024)} %param.22) | copy-start | bytes 73732
  261.6 3.8 copy-start.2
  261.6 3.8 copy-start.9
  411.3 4.3 copy-start.8
  445.9 86.2 %all-to-all-start.1 = ((bf16[64,10,1536]{2,1,0:T(8,128)(2,1)}), bf16[64,10,1536]{2,1,0:T(8,128)(2,1)}, u32[]{:S(2)}, u32[]{:S(2)}) async-start(bf16[64,10,1536]{2,1,0:T(8,128)(2,1)} %copy.132), calls=%async_computation.1 | async-start | bytes 6291456 | tf_op jit(solution)/shard_map/all_to_all | solution.py:160
Sparse Core Ops, SparseCore 0:
  10.1 132.7 all-gather.3
  188.6 72.9 all-reduce.2
  313.8 89.9 all-gather.5

commit v3 on v2

--- a/solution.py
+++ b/solution.py
@@ -105,15 +105,24 @@
     partial_sum = jnp.einsum(
         "thr,hrd->td", attn_mixed, row_whole, preferred_element_type=jnp.float32
     )
-    projected = lax.psum(partial_sum.astype(jnp.bfloat16), "head").astype(jnp.float32)
-    hidden_full = residual.astype(jnp.float32) + projected
-    normed_full = (
-        hidden_full
-        * lax.rsqrt(jnp.mean(hidden_full * hidden_full, axis=-1, keepdims=True) + epsilon)
-        * norm_gain[None, :]
-    ).astype(jnp.bfloat16)
-    hidden_share = lax.dynamic_slice_in_dim(hidden_full, head_index * share_width, share_width, 1)
-    logits = jnp.dot(normed_full, router_weight, preferred_element_type=jnp.float32)
+    projected = lax.psum_scatter(
+        partial_sum.astype(jnp.bfloat16), "head", scatter_dimension=1, tiled=True
+    ).astype(jnp.float32)
+    share_start = head_index * share_width
+    residual_share = lax.dynamic_slice_in_dim(residual, share_start, share_width, 1)
+    gain_share = lax.dynamic_slice_in_dim(norm_gain, share_start, share_width, 0)
+    router_share = lax.dynamic_slice_in_dim(router_weight, share_start, share_width, 0)
+    hidden_share = residual_share.astype(jnp.float32) + projected
+    router_part = jnp.dot(
+        hidden_share * gain_share[None, :],
+        router_share.astype(jnp.float32),
+        precision=highest,
+    )
+    square_part = jnp.sum(hidden_share * hidden_share, axis=-1, keepdims=True)
+    stats = lax.psum(jnp.concatenate([square_part, router_part], axis=1), "head")
+    row_scale = lax.rsqrt(stats[:, :1] / model_width + epsilon)
+    logits = stats[:, 1:] * row_scale
+    normed_share = (hidden_share * row_scale * gain_share[None, :]).astype(jnp.bfloat16)
     columns = jnp.arange(router_weight.shape[1], dtype=jnp.int32)
     picked = jnp.sum(
         jnp.where(columns[None, None, :] == expert_ids[:, :, None], logits[:, None, :], 0.0),
@@ -139,15 +148,19 @@
     )
     group = ctx_count // EXP
     packed = (
-        jnp.dot(chooser, normed_full, preferred_element_type=jnp.float32)
+        jnp.dot(chooser, normed_share, preferred_element_type=jnp.float32)
         .astype(jnp.bfloat16)
-        .reshape(EXP, MOST, model_width)
+        .reshape(EXP, MOST, share_width)
     )
     by_group = lax.all_to_all(packed, "g", split_axis=0, concat_axis=0, tiled=True)
-    arrived = lax.all_gather(by_group, "j", axis=1, tiled=False)
-    sources = arrived.shape[0] * arrived.shape[1]
+    arrived = lax.all_gather(by_group, ("j", "head"), axis=1, tiled=False)
+    sources = ctx_count
     slots_now = arrived.shape[2]
-    flat_rows = arrived.reshape(sources * slots_now, model_width)
+    flat_rows = (
+        arrived.reshape(EXP, group, head_count, slots_now, share_width)
+        .transpose(0, 1, 3, 2, 4)
+        .reshape(sources * slots_now, model_width)
+    )
     gate_part = jnp.einsum("rd,fd->rf", flat_rows, expert_gate, preferred_element_type=jnp.float32)
     up_part = jnp.einsum("rd,fd->rf", flat_rows, expert_up, preferred_element_type=jnp.float32)
     hidden_units = (

time: 548 us -> 523 us (0.954); the launches traced: 544 us -> 513 us
  waiting for transfers between devices: 340 us -> 241 us
  blocking collectives: 62.8 us -> 140 us
  starting transfers between devices: 53 us -> 40 us
  local copies, waits for them, and re-layouts: 20.9 us -> 29 us
    all_to_all x0 -> x1, blocking collectives: none -> 84.4 us  [body(): lax.all_to_all(partial_value, ('g', 'j'), split_axis=0, concat_axis=0, ti...]
    all_to_all x1 -> x0, waiting for transfers between devices: 73.4 us -> none  [body(): lax.all_to_all(partial_value, ('g', 'j'), split_axis=0, concat_axis=0, ti...]
    psum x1 -> x0, waiting for transfers between devices: 71.4 us -> none  [body(): lax.psum(partial_sum.astype(jnp.bfloat16), 'head').astype(jnp.float32)]
    reduce_scatter x0 -> x1, waiting for transfers between devices: none -> 42.3 us  [body(): lax.psum_scatter(partial_sum.astype(jnp.bfloat16), 'head', scatter_dimens...]
    all_to_all x1, blocking collectives: 41.2 us -> 20 us  [body(): lax.all_to_all(packed, 'g', split_axis=0, concat_axis=0, tiled=True)]
    all_to_all x1 -> x0, starting transfers between devices: 12.8 us -> none  [body(): lax.all_to_all(partial_value, ('g', 'j'), split_axis=0, concat_axis=0, ti...]
    psum x0 -> x1, blocking collectives: none -> 12.6 us  [body(): lax.psum(jnp.concatenate([square_part, router_part], axis=1), 'head')]
    transpose x0 -> x1, local copies, waits for them, and re-layouts: none -> 12.5 us  [body(): flat_rows = arrived.reshape(EXP, group, head_count, slots_now, share_widt...]
  transfers between devices with their start and end apart: 11 -> 10, of which waited for: 10 -> 9; matrix products, arithmetic and copies ran while one was open for 3% -> 3% of each run, Pallas kernels for 0% -> 0%
where the time goes in v3:
time: 523 us; the launch traced here: 513 us
  waiting for transfers between devices  241 us (46%)
  blocking collectives  140 us (27%)
  matrix products  40.5 us (8%)
  starting transfers between devices  40 us (8%)
  local copies, waits for them, and re-layouts  29 us (6%)
  between operations  13.8 us (3%)
  other arithmetic  8.5 us (2%)
    ppermute x7, waiting for transfers between devices, shift(): lax.ppermute(value, axis, [(i, i + distance) for i in range(count - dista...  105 us
    all_gather x1, waiting for transfers between devices, body(): arrived = lax.all_gather(by_group, ('j', 'head'), axis=1, tiled=False)  93.9 us
    all_to_all x1, blocking collectives, body(): lax.all_to_all(partial_value, ('g', 'j'), split_axis=0, concat_axis=0, ti...  84.4 us
    reduce_scatter x1, waiting for transfers between devices, body(): lax.psum_scatter(partial_sum.astype(jnp.bfloat16), 'head', scatter_dimens...  42.3 us
    ppermute x7, starting transfers between devices, shift(): lax.ppermute(value, axis, [(i, i + distance) for i in range(count - dista...  40 us
    all_gather x1, blocking collectives, body(): joined = lax.all_gather(hidden_units, 'head', axis=2, tiled=True)  23.2 us
    dot_general x1, matrix products, body(): jnp.einsum('thr,hrd->td', attn_mixed, row_whole, preferred_element_type=j...  20.4 us
    all_to_all x1, blocking collectives, body(): lax.all_to_all(packed, 'g', split_axis=0, concat_axis=0, tiled=True)  20 us
  transfers between devices with their start and end apart: 10, of which 9 were waited for; matrix products, arithmetic and copies ran while one was open for 3% of the time, Pallas kernels for 0%

profile of v3, /device:TPU:1, one launch (start us, length us, event | category | flops | bytes accessed | tf_op | source)
XLA Modules:
  0.0 513.2 jit_solution(8328680779308808837)
XLA Ops:
  6.5 1.8 copy.94
  12.6 4.9 collective-permute-start
  17.6 6.4 %collective-permute-done = f32[8,136,128]{2,1,0:T(8,128)S(1)} collective-permute-done((f32[8,136,128]{2,1,0:T(8,128)S(1)}, f32[8,136,128]{2,1,0:T(8,128)S(1)}, u32[]{:S(2)}, u32[]{:S(2)}) %collective-permute-start) | collective-permute-done | bytes 557088 | tf_op jit(solution)/shard_map/ppermute | solution.py:29
  24.1 4.4 collective-permute-start.1
  28.5 7.9 %collective-permute-done.1 = f32[8,136,128]{2,1,0:T(8,128)S(1)} collective-permute-done((f32[8,136,128]{2,1,0:T(8,128)S(1)}, f32[8,136,128]{2,1,0:T(8,128)S(1)}, u32[]{:S(2)}, u32[]{:S(2)}) %collective-permute-start.1) | collective-permute-done | bytes 557088 | tf_op jit(solution)/shard_map/ppermute | solution.py:29
  36.8 4.3 collective-permute-start.2
  41.1 15.8 %collective-permute-done.2 = f32[8,136,128]{2,1,0:T(8,128)S(1)} collective-permute-done((f32[8,136,128]{2,1,0:T(8,128)S(1)}, f32[8,136,128]{2,1,0:T(8,128)S(1)}, u32[]{:S(2)}, u32[]{:S(2)}) %collective-permute-start.2) | collective-permute-done | bytes 557088 | tf_op jit(solution)/shard_map/ppermute | solution.py:29
  57.3 5.2 %collective-permute-start.3 = (f32[8,136,128]{2,1,0:T(8,128)S(1)}, f32[8,136,128]{2,1,0:T(8,128)S(1)}, u32[]{:S(2)}, u32[]{:S(2)}) collective-permute-start(f32[8,136,128]{2,1,0:T(8,128)S(1)} %maximum_select_fusion.1), channel_id=1, source_target_pairs={{0,16},{4,20},{8,24},{12,28},{16,32},{20,36},{24,40},{28,44},{32,4... | collective-permute-start | bytes 1671176 | tf_op jit(solution)/shard_map/ppermute | solution.py:29
  62.5 32.9 %collective-permute-done.3 = f32[8,136,128]{2,1,0:T(8,128)S(1)} collective-permute-done((f32[8,136,128]{2,1,0:T(8,128)S(1)}, f32[8,136,128]{2,1,0:T(8,128)S(1)}, u32[]{:S(2)}, u32[]{:S(2)}) %collective-permute-start.3) | collective-permute-done | bytes 557088 | tf_op jit(solution)/shard_map/ppermute | solution.py:29
  95.8 4.9 collective-permute-start.4
  100.7 30.8 %collective-permute-done.4 = f32[8,136,128]{2,1,0:T(8,128)S(1)} collective-permute-done((f32[8,136,128]{2,1,0:T(8,128)S(1)}, f32[8,136,128]{2,1,0:T(8,128)S(1)}, u32[]{:S(2)}, u32[]{:S(2)}) %collective-permute-start.4) | collective-permute-done | bytes 557088 | tf_op jit(solution)/shard_map/ppermute | solution.py:29
  132.0 3.5 collective-permute-start.5
  135.5 8.1 %collective-permute-done.5 = f32[8,136,128]{2,1,0:T(8,128)S(1)} collective-permute-done((f32[8,136,128]{2,1,0:T(8,128)S(1)}, f32[8,136,128]{2,1,0:T(8,128)S(1)}, u32[]{:S(2)}, u32[]{:S(2)}) %collective-permute-start.5) | collective-permute-done | bytes 557088 | tf_op jit(solution)/shard_map/ppermute | solution.py:29
  144.0 12.8 %collective-permute-start.6 = (f32[8,136,128]{2,1,0:T(8,128)S(1)}, f32[8,136,128]{2,1,0:T(8,128)}, u32[]{:S(2)}, u32[]{:S(2)}) collective-permute-start(f32[8,136,128]{2,1,0:T(8,128)S(1)} %maximum_select_fusion.4), channel_id=1, source_target_pairs={{0,128},{4,132},{8,136},{12,140},{16,144},{20,148},{24,152},{28,15... | collective-permute-start | bytes 1671176 | tf_op jit(solution)/shard_map/ppermute | solution.py:29
  159.1 3.1 collective-permute-done.6
  164.4 2.4 fusion.14
  166.7 1.6 multiply_reduce_fusion.1
  168.4 20.4 %fusion.5 = bf16[128,6144]{1,0:T(8,128)(2,1)} fusion(bf16[8,128,6144]{2,0,1:T(8,128)(2,1)} %all-gather.4.cloned.1.call-done, f32[128,8,128]{0,2,1:T(8,128)S(1)} %bitcast.90, f32[128,8,128]{0,2,1:T(8,128)S(1)} %get-tuple-element.22, f32[8,128]{1,0:T(8,128)S(1)} %bitcast.94, f32[128,8]{0,1:T(8,128)S(1)} %add_rsqrt_fusion), kind=kOutput, calls=%fused_computation.3 | convolution fusion | flops 1611923456 | bytes 15212544 | tf_op jit(solution)/shard_map/thr,hrd->td/dot_general | solution.py:105
  191.3 42.3 %reduce-scatter.2.cloned.1.call-done = bf16[128,1536]{1,0:T(8,128)(2,1)} async-done(((bf16[128,6144]{1,0:T(8,128)(2,1)}), bf16[128,1536]{1,0:T(8,128)(2,1)}) %reduce-scatter.2.cloned.1.call-update) | async-done | bytes 393232 | tf_op jit(solution)/shard_map/reduce_scatter | solution.py:108
  233.6 1.4 multiply_reduce_fusion
  235.0 1.8 fusion.17
  236.8 12.6 %psum.7 = f32[128,33]{0,1:T(8,128)S(1)} all-reduce(f32[128,33]{0,1:T(8,128)S(1)} %pad_maximum_fusion.2), channel_id=1, replica_groups=mesh['g'=8,'j'=8,'head'=4] {'head'}, use_global_device_ids=true, to_apply=%region_7.8 | all-reduce | flops 4224 | bytes 33792 | tf_op jit(solution)/shard_map/psum | solution.py:122
  250.9 20.0 %all_to_all.10 = bf16[8,10,1536]{2,1,0:T(8,128)(2,1)S(1)} all-to-all(bf16[8,10,1536]{2,1,0:T(8,128)(2,1)S(1)} %reshape.171), channel_id=1, replica_groups=mesh['g'=8,'j'=8,'head'=4] {'g'}, dimensions={0} | all-to-all | bytes 491520 | tf_op jit(solution)/shard_map/all_to_all | solution.py:155
  271.8 93.9 %all-gather.6.cloned.1.call-done = bf16[8,320,1536]{2,0,1:T(8,128)(2,1)} async-done(((bf16[8,10,1536]{2,0,1:T(8,128)(2,1)}), bf16[8,320,1536]{2,0,1:T(8,128)(2,1)}) %all-gather.6.cloned.1.call-update) | async-done | bytes 7864336 | tf_op jit(solution)/shard_map/all_gather | solution.py:156
  365.6 12.5 %copy.102 = bf16[8,8,10,4,1536]{4,3,2,1,0:T(4,128)(2,1)} copy(bf16[8,8,10,4,1536]{4,0,2,3,1:T(8,128)(2,1)} %bitcast.87) | data formatting | bytes 15728640 | tf_op jit(solution)/shard_map/transpose | solution.py:161
  378.1 5.7 %copy.118 = bf16[80,8,4,1536]{3,1,2,0:T(8,128)(2,1)S(1)} copy(bf16[80,8,4,1536]{3,2,1,0:T(4,128)(2,1)} %bitcast.86) | data formatting | bytes 15728640
  383.8 4.3 fusion.75
  388.1 2.8 fusion.16
  392.1 23.2 %all_gather.15 = bf16[64,10,576]{0,1,2:T(8,128)(2,1)S(1)} all-gather(bf16[64,10,144]{0,1,2:T(8,128)(2,1)S(1)} %copy.104), channel_id=1, replica_groups=mesh['g'=8,'j'=8,'head'=4] {'head'}, dimensions={2}, use_global_device_ids=true | all-gather | bytes 921600 | tf_op jit(solution)/shard_map/all_gather | solution.py:169
  415.3 1.8 convolution_convert_fusion
  418.3 84.4 %all_to_all.11 = bf16[64,10,1536]{2,1,0:T(8,128)(2,1)S(1)} all-to-all(bf16[64,10,1536]{2,1,0:T(8,128)(2,1)S(1)} %copy.106), channel_id=1, replica_groups=mesh['g'=8,'j'=8,'head'=4] {'g','j'}, dimensions={0} | all-to-all | bytes 3932160 | tf_op jit(solution)/shard_map/all_to_all | solution.py:173
  503.7 2.8 fusion.9
  (97 shorter events, 18.9 us)
Async XLA Ops:
  6.5 408.8 %copy-start = (bf16[576,1536]{1,0:T(8,128)(2,1)S(1)}, bf16[576,1536]{1,0:T(8,128)(2,1)}, u32[]{:S(2)}) copy-start(bf16[576,1536]{1,0:T(8,128)(2,1)} %param.27) | copy-start | bytes 5308420
  6.5 161.9 %all-gather.4.cloned.1.call-start = ((), (), s32[]{:S(2)}) async-start(), calls=%async_computation.3 | async-start | bytes 12779520 | tf_op jit(solution)/shard_map/all_gather | solution.py:104
  8.4 225.2 %reduce-scatter.2.cloned.1.call-start = ((), (), s32[]{:S(2)}) async-start(), calls=%async_computation.4 | async-start | bytes 1966080 | tf_op jit(solution)/shard_map/reduce_scatter | solution.py:108
  11.2 1.4 copy-start.3
  12.6 11.4 %collective-permute-start = (f32[8,136,128]{2,1,0:T(8,128)S(1)}, f32[8,136,128]{2,1,0:T(8,128)S(1)}, u32[]{:S(2)}, u32[]{:S(2)}) collective-permute-start(f32[8,136,128]{2,1,0:T(8,128)S(1)} %pad_maximum_fusion), channel_id=1, source_target_pairs={{0,4},{4,8},{8,12},{12,16},{16,20},{20,24},{24,28},{28,32},{32,36}... | collective-permute-start | bytes 1671176 | tf_op jit(solution)/shard_map/ppermute | solution.py:29
  24.1 12.3 %collective-permute-start.1 = (f32[8,136,128]{2,1,0:T(8,128)S(1)}, f32[8,136,128]{2,1,0:T(8,128)S(1)}, u32[]{:S(2)}, u32[]{:S(2)}) collective-permute-start(f32[8,136,128]{2,1,0:T(8,128)S(1)} %pad_select_fusion), channel_id=1, source_target_pairs={{0,4},{4,8},{8,12},{12,16},{16,20},{20,24},{24,28},{28,32},{32,36}... | collective-permute-start | bytes 1671176 | tf_op jit(solution)/shard_map/ppermute | solution.py:29
  36.8 20.1 %collective-permute-start.2 = (f32[8,136,128]{2,1,0:T(8,128)S(1)}, f32[8,136,128]{2,1,0:T(8,128)S(1)}, u32[]{:S(2)}, u32[]{:S(2)}) collective-permute-start(f32[8,136,128]{2,1,0:T(8,128)S(1)} %maximum_select_fusion), channel_id=1, source_target_pairs={{0,8},{4,12},{8,16},{12,20},{16,24},{20,28},{24,32},{28,36},{32,40... | collective-permute-start | bytes 1671176 | tf_op jit(solution)/shard_map/ppermute | solution.py:29
  57.3 38.1 %collective-permute-start.3 = (f32[8,136,128]{2,1,0:T(8,128)S(1)}, f32[8,136,128]{2,1,0:T(8,128)S(1)}, u32[]{:S(2)}, u32[]{:S(2)}) collective-permute-start(f32[8,136,128]{2,1,0:T(8,128)S(1)} %maximum_select_fusion.1), channel_id=1, source_target_pairs={{0,16},{4,20},{8,24},{12,28},{16,32},{20,36},{24,40},{28,44},{32,4... | collective-permute-start | bytes 1671176 | tf_op jit(solution)/shard_map/ppermute | solution.py:29
  95.8 35.7 %collective-permute-start.4 = (f32[8,136,128]{2,1,0:T(8,128)S(1)}, f32[8,136,128]{2,1,0:T(8,128)S(1)}, u32[]{:S(2)}, u32[]{:S(2)}) collective-permute-start(f32[8,136,128]{2,1,0:T(8,128)S(1)} %maximum_select_fusion.2), channel_id=1, source_target_pairs={{0,32},{4,36},{8,40},{12,44},{16,48},{20,52},{24,56},{28,60},{32,6... | collective-permute-start | bytes 1671176 | tf_op jit(solution)/shard_map/ppermute | solution.py:29
  132.0 11.6 %collective-permute-start.5 = (f32[8,136,128]{2,1,0:T(8,128)S(1)}, f32[8,136,128]{2,1,0:T(8,128)S(1)}, u32[]{:S(2)}, u32[]{:S(2)}) collective-permute-start(f32[8,136,128]{2,1,0:T(8,128)S(1)} %maximum_select_fusion.3), channel_id=1, source_target_pairs={{0,64},{4,68},{8,72},{12,76},{16,80},{20,84},{24,88},{28,92},{32,9... | collective-permute-start | bytes 1671176 | tf_op jit(solution)/shard_map/ppermute | solution.py:29
  144.0 18.2 %collective-permute-start.6 = (f32[8,136,128]{2,1,0:T(8,128)S(1)}, f32[8,136,128]{2,1,0:T(8,128)}, u32[]{:S(2)}, u32[]{:S(2)}) collective-permute-start(f32[8,136,128]{2,1,0:T(8,128)S(1)} %maximum_select_fusion.4), channel_id=1, source_target_pairs={{0,128},{4,132},{8,136},{12,140},{16,144},{20,148},{24,152},{28,15... | collective-permute-start | bytes 1671176 | tf_op jit(solution)/shard_map/ppermute | solution.py:29
  159.0 7.7 %copy-start.4 = (bf16[128,1024]{0,1:T(8,128)(2,1)S(1)}, bf16[128,1024]{0,1:T(8,128)(2,1)}, u32[]{:S(2)}) copy-start(bf16[128,1024]{0,1:T(8,128)(2,1)} %copy-done.3) | copy-start | bytes 786436
  159.1 7.7 %copy-start.6 = (bf16[128,1024]{1,0:T(8,128)(2,1)S(1)}, bf16[128,1024]{1,0:T(8,128)(2,1)}, u32[]{:S(2)}) copy-start(bf16[128,1024]{1,0:T(8,128)(2,1)} %param.16) | copy-start | bytes 786436
  164.4 4.1 copy-start.5
  168.4 20.5 %copy-start.7 = (s32[128,2]{0,1:T(2,128)S(1)}, s32[128,2]{0,1:T(2,128)}, u32[]{:S(2)}) copy-start(s32[128,2]{0,1:T(2,128)} %param.24) | copy-start | bytes 3076
  188.9 176.7 %all-gather.6.cloned.1.call-start = ((), (), s32[]{:S(2)}) async-start(), calls=%async_computation.5 | async-start | bytes 8110080 | tf_op jit(solution)/shard_map/all_gather | solution.py:156
  233.6 15.9 %copy-start.1 = (bf16[128,1536]{1,0:T(8,128)(2,1)S(1)}, bf16[128,1536]{1,0:T(8,128)(2,1)}, u32[]{:S(2)}) copy-start(bf16[128,1536]{1,0:T(8,128)(2,1)} %reduce-scatter.2.cloned.1.call-done) | copy-start | bytes 1179652
  383.7 4.3 copy-start.8
  502.7 1.0 copy-start.2
Sparse Core Ops, SparseCore 0:
  10.1 132.7 all-gather.3
  189.0 44.5 reduce-scatter.1
  271.9 93.6 all-gather.5

commit v4 on v3

--- a/solution.py
+++ b/solution.py
@@ -5,6 +5,7 @@
 
 EXP = 8
 MOST = 10
+CTX = ("g", "q", "core")
 
 
 epsilon = 1e-06
@@ -59,7 +60,7 @@
     expert_up,
     expert_down,
 ):
-    ctx_count = lax.axis_size(("g", "j"))
+    ctx_count = lax.axis_size(CTX)
     head_count = lax.axis_size("head")
     head_index = lax.axis_index("head")
     tok_rows = queries.shape[0]
@@ -78,7 +79,7 @@
     local_state = jnp.einsum(
         "thd,the->hde", keys_decayed, value_blocks, preferred_element_type=jnp.float32
     )
-    entering = prefix_scan(jnp.exp(block_total), local_state, ("g", "j"), ctx_count)
+    entering = prefix_scan(jnp.exp(block_total), local_state, CTX, ctx_count)
     sequence_offsets = jnp.arange(tok_rows)
     causal = (sequence_offsets[:, None] >= sequence_offsets[None, :])[None, :, :]
     cum_heads = cumulative.T
@@ -101,12 +102,33 @@
     attn_mixed = (
         attended * rms_scale * attn_gain.reshape(local_heads, head_dim) * gate_open
     ).astype(jnp.bfloat16)
-    row_whole = lax.all_gather(out_weight, ("g", "j"), axis=1, tiled=True)
+    core = lax.axis_index("core")
+    swap = [(0, 1), (1, 0)]
+    half_width = share_width // 2
+    split_weight = out_weight.reshape(local_heads, -1, head_count, 2, half_width)
+    mine = jnp.where(core == 0, split_weight[:, :, :, 0], split_weight[:, :, :, 1])
+    theirs = jnp.where(core == 0, split_weight[:, :, :, 1], split_weight[:, :, :, 0])
+    received = lax.ppermute(theirs, "core", swap)
+    pair_rows = jnp.concatenate(
+        [jnp.where(core == 0, mine, received), jnp.where(core == 0, received, mine)], axis=1
+    )
+    row_whole = lax.all_gather(pair_rows, ("g", "q"), axis=1, tiled=True)
+    partner_mixed = lax.ppermute(attn_mixed, "core", swap)
+    both_mixed = jnp.concatenate(
+        [jnp.where(core == 0, attn_mixed, partner_mixed), jnp.where(core == 0, partner_mixed, attn_mixed)],
+        axis=0,
+    )
     partial_sum = jnp.einsum(
-        "thr,hrd->td", attn_mixed, row_whole, preferred_element_type=jnp.float32
-    )
-    projected = lax.psum_scatter(
+        "thr,hrqd->tqd", both_mixed, row_whole, preferred_element_type=jnp.float32
+    )
+    scattered = lax.psum_scatter(
         partial_sum.astype(jnp.bfloat16), "head", scatter_dimension=1, tiled=True
+    ).reshape(2, tok_rows, half_width)
+    own_rows = jnp.where(core == 0, scattered[0], scattered[1])
+    other_rows = lax.ppermute(jnp.where(core == 0, scattered[1], scattered[0]), "core", swap)
+    projected = jnp.concatenate(
+        [jnp.where(core == 0, own_rows, other_rows), jnp.where(core == 0, other_rows, own_rows)],
+        axis=1,
     ).astype(jnp.float32)
     share_start = head_index * share_width
     residual_share = lax.dynamic_slice_in_dim(residual, share_start, share_width, 1)
@@ -153,7 +175,7 @@
         .reshape(EXP, MOST, share_width)
     )
     by_group = lax.all_to_all(packed, "g", split_axis=0, concat_axis=0, tiled=True)
-    arrived = lax.all_gather(by_group, ("j", "head"), axis=1, tiled=False)
+    arrived = lax.all_gather(by_group, ("q", "core", "head"), axis=1, tiled=False)
     sources = ctx_count
     slots_now = arrived.shape[2]
     flat_rows = (
@@ -170,7 +192,7 @@
     partial_value = jnp.einsum(
         "nmf,fd->nmd", joined, expert_down, preferred_element_type=jnp.float32
     ).astype(jnp.bfloat16)
-    returned = lax.all_to_all(partial_value, ("g", "j"), split_axis=0, concat_axis=0, tiled=True)
+    returned = lax.all_to_all(partial_value, CTX, split_axis=0, concat_axis=0, tiled=True)
     summed = jnp.sum(returned.astype(jnp.float32).reshape(EXP, group, MOST, share_width), axis=1)
     mixture = jnp.einsum("est,esd->td", weighted, summed, precision=highest)
     return (hidden_share + mixture).astype(jnp.bfloat16)
@@ -180,9 +202,9 @@
     ctx_count = mesh.shape["ctx"]
     head_count = mesh.shape["head"]
     split = Mesh(
-        mesh.devices.reshape(EXP, ctx_count // EXP, head_count), ("g", "j", "head")
-    )
-    ctx = ("g", "j")
+        mesh.devices.reshape(EXP, ctx_count // EXP // 2, 2, head_count), ("g", "q", "core", "head")
+    )
+    ctx = CTX
     return jax.shard_map(
         body,
         mesh=split,
@@ -198,8 +220,8 @@
             P(),
             P(),
             P(ctx, None),
-            P(("g", "j", "head"), None),
-            P(("g", "j", "head"), None),
+            P(ctx + ("head",), None),
+            P(ctx + ("head",), None),
             P(ctx, "head"),
         ),
         out_specs=P(ctx, "head"),

time: 523 us -> 524 us (level)
  starting transfers between devices: 40 us -> 54.1 us
  waiting for transfers between devices: 241 us -> 234 us
    ppermute x0 -> x3, starting transfers between devices: none -> 22.6 us  [the longest x1 17.7 us: body(): partner_mixed = lax.ppermute(attn_mixed, 'core', swap)]
    ppermute x7, starting transfers between devices: 40 us -> 31.4 us  [shift(): lax.ppermute(value, axis, [(i, i + distance) for i in range(count - dista...]
    reduce_scatter x1, waiting for transfers between devices: 42.3 us -> 34.6 us  [body(): lax.psum_scatter(partial_sum.astype(jnp.bfloat16), 'head', scatter_dimens...]
  transfers between devices with their start and end apart: 10 -> 13, of which waited for: 9 -> 12; matrix products, arithmetic and copies ran while one was open for 3% -> 2% of each run, Pallas kernels for 0% -> 0%
where the time goes in v4:
time: 524 us; the launch traced here: 518 us
  waiting for transfers between devices  234 us (45%)
  blocking collectives  139 us (27%)
  starting transfers between devices  54.1 us (10%)
  matrix products  37.7 us (7%)
  local copies, waits for them, and re-layouts  27.7 us (5%)
  between operations  14.1 us (3%)
  other arithmetic  10.3 us (2%)
    ppermute x7, waiting for transfers between devices, shift(): lax.ppermute(value, axis, [(i, i + distance) for i in range(count - dista...  103 us
    all_gather x1, waiting for transfers between devices, body(): lax.all_gather(by_group, ('q', 'core', 'head'), axis=1, tiled=False)  93.4 us
    all_to_all x1, blocking collectives, body(): lax.all_to_all(partial_value, CTX, split_axis=0, concat_axis=0, tiled=True)  84.4 us
    reduce_scatter x1, waiting for transfers between devices, body(): lax.psum_scatter(partial_sum.astype(jnp.bfloat16), 'head', scatter_dimens...  34.6 us
    ppermute x7, starting transfers between devices, shift(): lax.ppermute(value, axis, [(i, i + distance) for i in range(count - dista...  31.4 us
    all_gather x1, blocking collectives, body(): joined = lax.all_gather(hidden_units, 'head', axis=2, tiled=True)  23.2 us
    all_to_all x1, blocking collectives, body(): lax.all_to_all(packed, 'g', split_axis=0, concat_axis=0, tiled=True)  20 us
    dot_general x1, matrix products, body(): jnp.einsum('thr,hrqd->tqd', both_mixed, row_whole, preferred_element_type...  18.2 us
  transfers between devices with their start and end apart: 13, of which 12 were waited for; matrix products, arithmetic and copies ran while one was open for 2% of the time, Pallas kernels for 0%

profile of v4, /device:TPU:1, one launch (start us, length us, event | category | flops | bytes accessed | tf_op | source)
XLA Modules:
  0.0 517.8 jit_solution(14185160484493393665)
XLA Ops:
  8.5 3.3 collective-permute-start.8
  14.9 2.1 collective-permute-start
  17.0 6.4 %collective-permute-done = f32[8,136,128]{2,1,0:T(8,128)S(1)} collective-permute-done((f32[8,136,128]{2,1,0:T(8,128)S(1)}, f32[8,136,128]{2,1,0:T(8,128)S(1)}, u32[]{:S(2)}, u32[]{:S(2)}) %collective-permute-start) | collective-permute-done | bytes 557088 | tf_op jit(solution)/shard_map/ppermute | solution.py:30
  23.5 4.4 collective-permute-start.1
  27.9 8.1 %collective-permute-done.1 = f32[8,136,128]{2,1,0:T(8,128)S(1)} collective-permute-done((f32[8,136,128]{2,1,0:T(8,128)S(1)}, f32[8,136,128]{2,1,0:T(8,128)S(1)}, u32[]{:S(2)}, u32[]{:S(2)}) %collective-permute-start.1) | collective-permute-done | bytes 557088 | tf_op jit(solution)/shard_map/ppermute | solution.py:30
  36.5 4.1 collective-permute-start.2
  40.6 15.2 %collective-permute-done.2 = f32[8,136,128]{2,1,0:T(8,128)S(1)} collective-permute-done((f32[8,136,128]{2,1,0:T(8,128)S(1)}, f32[8,136,128]{2,1,0:T(8,128)S(1)}, u32[]{:S(2)}, u32[]{:S(2)}) %collective-permute-start.2) | collective-permute-done | bytes 557088 | tf_op jit(solution)/shard_map/ppermute | solution.py:30
  56.2 5.9 %collective-permute-start.3 = (f32[8,136,128]{2,1,0:T(8,128)S(1)}, f32[8,136,128]{2,1,0:T(8,128)S(1)}, u32[]{:S(2)}, u32[]{:S(2)}) collective-permute-start(f32[8,136,128]{2,1,0:T(8,128)S(1)} %maximum_select_fusion.1), channel_id=1, source_target_pairs={{0,16},{4,20},{8,24},{12,28},{16,32},{20,36},{24,40},{28,44},{32,4... | collective-permute-start | bytes 1671176 | tf_op jit(solution)/shard_map/ppermute | solution.py:30
  62.2 27.3 %collective-permute-done.3 = f32[8,136,128]{2,1,0:T(8,128)S(1)} collective-permute-done((f32[8,136,128]{2,1,0:T(8,128)S(1)}, f32[8,136,128]{2,1,0:T(8,128)S(1)}, u32[]{:S(2)}, u32[]{:S(2)}) %collective-permute-start.3) | collective-permute-done | bytes 557088 | tf_op jit(solution)/shard_map/ppermute | solution.py:30
  89.9 5.9 %collective-permute-start.4 = (f32[8,136,128]{2,1,0:T(8,128)S(1)}, f32[8,136,128]{2,1,0:T(8,128)S(1)}, u32[]{:S(2)}, u32[]{:S(2)}) collective-permute-start(f32[8,136,128]{2,1,0:T(8,128)S(1)} %maximum_select_fusion.2), channel_id=1, source_target_pairs={{0,32},{4,36},{8,40},{12,44},{16,48},{20,52},{24,56},{28,60},{32,6... | collective-permute-start | bytes 1671176 | tf_op jit(solution)/shard_map/ppermute | solution.py:30
  95.8 30.3 %collective-permute-done.4 = f32[8,136,128]{2,1,0:T(8,128)S(1)} collective-permute-done((f32[8,136,128]{2,1,0:T(8,128)S(1)}, f32[8,136,128]{2,1,0:T(8,128)S(1)}, u32[]{:S(2)}, u32[]{:S(2)}) %collective-permute-start.4) | collective-permute-done | bytes 557088 | tf_op jit(solution)/shard_map/ppermute | solution.py:30
  126.6 3.5 collective-permute-start.5
  130.1 8.1 %collective-permute-done.5 = f32[8,136,128]{2,1,0:T(8,128)S(1)} collective-permute-done((f32[8,136,128]{2,1,0:T(8,128)S(1)}, f32[8,136,128]{2,1,0:T(8,128)S(1)}, u32[]{:S(2)}, u32[]{:S(2)}) %collective-permute-start.5) | collective-permute-done | bytes 557088 | tf_op jit(solution)/shard_map/ppermute | solution.py:30
  138.6 5.5 %collective-permute-start.6 = (f32[8,136,128]{2,1,0:T(8,128)S(1)}, f32[8,136,128]{2,1,0:T(8,128)}, u32[]{:S(2)}, u32[]{:S(2)}) collective-permute-start(f32[8,136,128]{2,1,0:T(8,128)S(1)} %maximum_select_fusion.4), channel_id=1, source_target_pairs={{0,128},{4,132},{8,136},{12,140},{16,144},{20,148},{24,152},{28,15... | collective-permute-start | bytes 1671176 | tf_op jit(solution)/shard_map/ppermute | solution.py:30
  144.8 7.6 %collective-permute-done.6 = f32[8,136,128]{2,1,0:T(8,128)} collective-permute-done((f32[8,136,128]{2,1,0:T(8,128)S(1)}, f32[8,136,128]{2,1,0:T(8,128)}, u32[]{:S(2)}, u32[]{:S(2)}) %collective-permute-start.6) | collective-permute-done | bytes 557088 | tf_op jit(solution)/shard_map/ppermute | solution.py:30
  154.5 2.2 fusion.10
  158.6 17.7 %collective-permute-start.7 = (bf16[128,8,128]{2,0,1:T(8,128)(2,1)S(1)}, bf16[128,8,128]{2,0,1:T(8,128)(2,1)S(1)}, u32[]{:S(2)}, u32[]{:S(2)}) collective-permute-start(bf16[128,8,128]{2,0,1:T(8,128)(2,1)S(1)} %multiply_convert_fusion.1), channel_id=1, source_target_pairs={{0,4},{4,0},{1,5},{5,1},{2,6},{6,2},{3,7},{7,3},{8,12},{12,8},{9,1... | collective-permute-start | bytes 786440 | tf_op jit(solution)/shard_map/ppermute | solution.py:116
  177.6 18.2 %bitcast_convert_fusion = bf16[256,4,768]{2,0,1:T(8,128)(2,1)} fusion(bf16[8,128,4,768]{3,0,2,1:T(8,128)(2,1)} %all-gather.4.cloned.1.call-done, bf16[128,8,128]{2,0,1:T(8,128)(2,1)S(1)} %get-tuple-element.22, bf16[128,8,128]{2,0,1:T(8,128)(2,1)S(1)} %get-tuple-element.21), kind=kOutput, calls=%fused_computation.4 | convolution fusion | flops 1612447744 | bytes 8388608 | tf_op jit(solution)/shard_map/thr,hrqd->tqd/dot_general | solution.py:121
  198.2 34.6 %reduce-scatter.2.cloned.1.call-done = bf16[256,1,768]{2,0,1:T(8,128)(2,1)} async-done(((bf16[256,4,768]{2,0,1:T(8,128)(2,1)}), bf16[256,1,768]{2,0,1:T(8,128)(2,1)}) %reduce-scatter.2.cloned.1.call-update) | async-done | bytes 393232 | tf_op jit(solution)/shard_map/reduce_scatter | solution.py:124
  233.8 1.6 collective-permute-start.9
  238.9 1.6 fusion.13
  240.5 12.0 %psum.7 = f32[128,33]{0,1:T(8,128)S(1)} all-reduce(f32[128,33]{0,1:T(8,128)S(1)} %pad_maximum_fusion.4), channel_id=1, replica_groups=mesh['g'=8,'q'=4,'core'=2,'head'=4] {'head'}, use_global_device_ids=true, to_apply=%region_7.8 | all-reduce | flops 4224 | bytes 33792 | tf_op jit(solution)/shard_map/psum | solution.py:144
  254.1 20.0 %all_to_all.10 = bf16[8,10,1536]{2,1,0:T(8,128)(2,1)S(1)} all-to-all(bf16[8,10,1536]{2,1,0:T(8,128)(2,1)S(1)} %reshape.188), channel_id=1, replica_groups=mesh['g'=8,'q'=4,'core'=2,'head'=4] {'g'}, dimensions={0} | all-to-all | bytes 491520 | tf_op jit(solution)/shard_map/all_to_all | solution.py:177
  274.9 93.4 %all-gather.6.cloned.1.call-done = bf16[8,320,1536]{2,0,1:T(8,128)(2,1)} async-done(((bf16[8,10,1536]{2,0,1:T(8,128)(2,1)}), bf16[8,320,1536]{2,0,1:T(8,128)(2,1)}) %all-gather.6.cloned.1.call-update) | async-done | bytes 7864336 | tf_op jit(solution)/shard_map/all_gather | solution.py:178
  368.4 12.5 %copy.179 = bf16[8,8,10,4,1536]{4,3,2,1,0:T(4,128)(2,1)} copy(bf16[8,8,10,4,1536]{4,0,2,3,1:T(8,128)(2,1)} %bitcast.100) | data formatting | bytes 15728640 | tf_op jit(solution)/shard_map/transpose | solution.py:183
  380.8 5.7 %copy.199 = bf16[80,8,4,1536]{3,1,2,0:T(8,128)(2,1)S(1)} copy(bf16[80,8,4,1536]{3,2,1,0:T(4,128)(2,1)} %bitcast.99) | data formatting | bytes 15728640
  386.5 4.3 fusion.73
  390.8 3.6 fusion.12
  396.6 23.2 %all_gather.15 = bf16[64,10,576]{0,1,2:T(8,128)(2,1)S(1)} all-gather(bf16[64,10,144]{0,1,2:T(8,128)(2,1)S(1)} %copy.181), channel_id=1, replica_groups=mesh['g'=8,'q'=4,'core'=2,'head'=4] {'head'}, dimensions={2}, use_global_device_ids=true | all-gather | bytes 921600 | tf_op jit(solution)/shard_map/all_gather | solution.py:191
  419.7 1.8 convolution_convert_fusion
  422.7 84.4 %all_to_all.11 = bf16[64,10,1536]{2,1,0:T(8,128)(2,1)S(1)} all-to-all(bf16[64,10,1536]{2,1,0:T(8,128)(2,1)S(1)} %copy.183), channel_id=1, replica_groups=mesh['g'=8,'q'=4,'core'=2,'head'=4] {'g','q','core'}, dimensions={0} | all-to-all | bytes 3932160 | tf_op jit(solution)/shard_map/all_to_all | solution.py:195
  508.0 2.8 fusion.3
  (121 shorter events, 26.4 us)
Async XLA Ops:
  6.5 413.2 %copy-start = (bf16[576,1536]{1,0:T(8,128)(2,1)S(1)}, bf16[576,1536]{1,0:T(8,128)(2,1)}, u32[]{:S(2)}) copy-start(bf16[576,1536]{1,0:T(8,128)(2,1)} %param.27) | copy-start | bytes 5308420
  6.5 7.0 %copy-start.11 = (f32[128,8]{0,1:T(8,128)S(1)}, f32[128,8]{0,1:T(8,128)}, u32[]{:S(2)}) copy-start(f32[128,8]{0,1:T(8,128)} %param.18) | copy-start | bytes 12292
  6.5 7.4 %copy-start.5 = (bf16[128,1024]{1,0:T(8,128)(2,1)S(1)}, bf16[128,1024]{1,0:T(8,128)(2,1)}, u32[]{:S(2)}) copy-start(bf16[128,1024]{1,0:T(8,128)(2,1)} %param.15) | copy-start | bytes 786436
  6.5 171.0 %all-gather.4.cloned.1.call-start = ((), (), s32[]{:S(2)}) async-start(), calls=%async_computation.3 | async-start | bytes 6488064 | tf_op jit(solution)/shard_map/all_gather | solution.py:115
  7.8 6.4 %copy-start.7 = (bf16[128,1024]{1,0:T(8,128)(2,1)S(1)}, bf16[128,1024]{1,0:T(8,128)(2,1)}, u32[]{:S(2)}) copy-start(bf16[128,1024]{1,0:T(8,128)(2,1)} %param.16) | copy-start | bytes 786436
  8.5 4.2 collective-permute-start.8
  13.5 219.2 %reduce-scatter.2.cloned.1.call-start = ((), (), s32[]{:S(2)}) async-start(), calls=%async_computation.4 | async-start | bytes 1966080 | tf_op jit(solution)/shard_map/reduce_scatter | solution.py:124
  14.1 0.7 copy-start.3
  14.9 8.5 %collective-permute-start = (f32[8,136,128]{2,1,0:T(8,128)S(1)}, f32[8,136,128]{2,1,0:T(8,128)S(1)}, u32[]{:S(2)}, u32[]{:S(2)}) collective-permute-start(f32[8,136,128]{2,1,0:T(8,128)S(1)} %pad_maximum_fusion), channel_id=1, source_target_pairs={{0,4},{4,8},{8,12},{12,16},{16,20},{20,24},{24,28},{28,32},{32,36}... | collective-permute-start | bytes 1671176 | tf_op jit(solution)/shard_map/ppermute | solution.py:30
  23.5 12.5 %collective-permute-start.1 = (f32[8,136,128]{2,1,0:T(8,128)S(1)}, f32[8,136,128]{2,1,0:T(8,128)S(1)}, u32[]{:S(2)}, u32[]{:S(2)}) collective-permute-start(f32[8,136,128]{2,1,0:T(8,128)S(1)} %pad_select_fusion), channel_id=1, source_target_pairs={{0,4},{4,8},{8,12},{12,16},{16,20},{20,24},{24,28},{28,32},{32,36}... | collective-permute-start | bytes 1671176 | tf_op jit(solution)/shard_map/ppermute | solution.py:30
  36.5 19.3 %collective-permute-start.2 = (f32[8,136,128]{2,1,0:T(8,128)S(1)}, f32[8,136,128]{2,1,0:T(8,128)S(1)}, u32[]{:S(2)}, u32[]{:S(2)}) collective-permute-start(f32[8,136,128]{2,1,0:T(8,128)S(1)} %maximum_select_fusion), channel_id=1, source_target_pairs={{0,8},{4,12},{8,16},{12,20},{16,24},{20,28},{24,32},{28,36},{32,40... | collective-permute-start | bytes 1671176 | tf_op jit(solution)/shard_map/ppermute | solution.py:30
  56.2 33.2 %collective-permute-start.3 = (f32[8,136,128]{2,1,0:T(8,128)S(1)}, f32[8,136,128]{2,1,0:T(8,128)S(1)}, u32[]{:S(2)}, u32[]{:S(2)}) collective-permute-start(f32[8,136,128]{2,1,0:T(8,128)S(1)} %maximum_select_fusion.1), channel_id=1, source_target_pairs={{0,16},{4,20},{8,24},{12,28},{16,32},{20,36},{24,40},{28,44},{32,4... | collective-permute-start | bytes 1671176 | tf_op jit(solution)/shard_map/ppermute | solution.py:30
  89.9 36.3 %collective-permute-start.4 = (f32[8,136,128]{2,1,0:T(8,128)S(1)}, f32[8,136,128]{2,1,0:T(8,128)S(1)}, u32[]{:S(2)}, u32[]{:S(2)}) collective-permute-start(f32[8,136,128]{2,1,0:T(8,128)S(1)} %maximum_select_fusion.2), channel_id=1, source_target_pairs={{0,32},{4,36},{8,40},{12,44},{16,48},{20,52},{24,56},{28,60},{32,6... | collective-permute-start | bytes 1671176 | tf_op jit(solution)/shard_map/ppermute | solution.py:30
  126.6 17.6 %copy-start.6 = (bf16[128,1024]{1,0:T(8,128)(2,1)S(1)}, bf16[128,1024]{1,0:T(8,128)(2,1)}, u32[]{:S(2)}) copy-start(bf16[128,1024]{1,0:T(8,128)(2,1)} %param.17) | copy-start | bytes 786436
  126.6 11.6 %collective-permute-start.5 = (f32[8,136,128]{2,1,0:T(8,128)S(1)}, f32[8,136,128]{2,1,0:T(8,128)S(1)}, u32[]{:S(2)}, u32[]{:S(2)}) collective-permute-start(f32[8,136,128]{2,1,0:T(8,128)S(1)} %maximum_select_fusion.3), channel_id=1, source_target_pairs={{0,64},{4,68},{8,72},{12,76},{16,80},{20,84},{24,88},{28,92},{32,9... | collective-permute-start | bytes 1671176 | tf_op jit(solution)/shard_map/ppermute | solution.py:30
  138.6 13.8 %collective-permute-start.6 = (f32[8,136,128]{2,1,0:T(8,128)S(1)}, f32[8,136,128]{2,1,0:T(8,128)}, u32[]{:S(2)}, u32[]{:S(2)}) collective-permute-start(f32[8,136,128]{2,1,0:T(8,128)S(1)} %maximum_select_fusion.4), channel_id=1, source_target_pairs={{0,128},{4,132},{8,136},{12,140},{16,144},{20,148},{24,152},{28,15... | collective-permute-start | bytes 1671176 | tf_op jit(solution)/shard_map/ppermute | solution.py:30
  144.7 12.0 %copy-start.4 = (bf16[128,1024]{0,1:T(8,128)(2,1)S(1)}, bf16[128,1024]{0,1:T(8,128)(2,1)}, u32[]{:S(2)}) copy-start(bf16[128,1024]{0,1:T(8,128)(2,1)} %copy-done.3) | copy-start | bytes 786436
  144.7 12.0 %copy-start.8 = (bf16[128,1024]{1,0:T(8,128)(2,1)S(1)}, bf16[128,1024]{1,0:T(8,128)(2,1)}, u32[]{:S(2)}) copy-start(bf16[128,1024]{1,0:T(8,128)(2,1)} %param.16) | copy-start | bytes 786436
  154.5 3.9 copy-start.10
  158.6 18.9 %collective-permute-start.7 = (bf16[128,8,128]{2,0,1:T(8,128)(2,1)S(1)}, bf16[128,8,128]{2,0,1:T(8,128)(2,1)S(1)}, u32[]{:S(2)}, u32[]{:S(2)}) collective-permute-start(bf16[128,8,128]{2,0,1:T(8,128)(2,1)S(1)} %multiply_convert_fusion.1), channel_id=1, source_target_pairs={{0,4},{4,0},{1,5},{5,1},{2,6},{6,2},{3,7},{7,3},{8,12},{12,8},{9,1... | collective-permute-start | bytes 786440 | tf_op jit(solution)/shard_map/ppermute | solution.py:116
  177.5 18.3 %copy-start.9 = (s32[128,2]{0,1:T(2,128)S(1)}, s32[128,2]{0,1:T(2,128)}, u32[]{:S(2)}) copy-start(s32[128,2]{0,1:T(2,128)} %param.24) | copy-start | bytes 3076
  195.7 172.6 %all-gather.6.cloned.1.call-start = ((), (), s32[]{:S(2)}) async-start(), calls=%async_computation.5 | async-start | bytes 8110080 | tf_op jit(solution)/shard_map/all_gather | solution.py:178
  233.8 2.7 collective-permute-start.9
  237.6 16.5 %copy-start.1 = (bf16[128,768]{1,0:T(8,128)(2,1)}, bf16[128,768]{1,0:T(8,128)(2,1)S(1)}, u32[]{:S(2)}) copy-start(bf16[128,768]{1,0:T(8,128)(2,1)S(1)} %get-tuple-element.20) | copy-start | bytes 589828
  386.5 4.3 copy-start.12
  507.1 0.9 copy-start.2
Sparse Core Ops, SparseCore 0:
  13.6 129.6 all-gather.3
  195.9 36.8 reduce-scatter.1
  275.1 93.2 all-gather.5

commit v5 on v4

--- a/solution.py
+++ b/solution.py
@@ -79,7 +79,29 @@
     local_state = jnp.einsum(
         "thd,the->hde", keys_decayed, value_blocks, preferred_element_type=jnp.float32
     )
-    entering = prefix_scan(jnp.exp(block_total), local_state, CTX, ctx_count)
+    core = lax.axis_index("core")
+    swap = [(0, 1), (1, 0)]
+    factor = jnp.exp(block_total)
+    partner_factor, partner_state = unpack_state(
+        lax.ppermute(pack_state(factor, local_state), "core", swap)
+    )
+    first_factor = jnp.where(core == 0, factor, partner_factor)
+    first_state = jnp.where(core == 0, local_state, partner_state)
+    second_factor = jnp.where(core == 0, partner_factor, factor)
+    second_state = jnp.where(core == 0, partner_state, local_state)
+    chip_factor = first_factor * second_factor
+    chip_state = second_factor[:, None, None] * first_state + second_state
+    half = local_heads // 2
+    half_factor = jnp.where(core == 0, chip_factor[:half], chip_factor[half:])
+    half_state = jnp.where(core == 0, chip_state[:half], chip_state[half:])
+    mine = prefix_scan(half_factor, half_state, ("g", "q"), ctx_count // 2)
+    other = lax.ppermute(mine, "core", swap)
+    chip_entering = jnp.concatenate(
+        [jnp.where(core == 0, mine, other), jnp.where(core == 0, other, mine)], axis=0
+    )
+    entering = jnp.where(
+        core == 0, chip_entering, first_factor[:, None, None] * chip_entering + first_state
+    )
     sequence_offsets = jnp.arange(tok_rows)
     causal = (sequence_offsets[:, None] >= sequence_offsets[None, :])[None, :, :]
     cum_heads = cumulative.T
@@ -102,8 +124,6 @@
     attn_mixed = (
         attended * rms_scale * attn_gain.reshape(local_heads, head_dim) * gate_open
     ).astype(jnp.bfloat16)
-    core = lax.axis_index("core")
-    swap = [(0, 1), (1, 0)]
     half_width = share_width // 2
     split_weight = out_weight.reshape(local_heads, -1, head_count, 2, half_width)
     mine = jnp.where(core == 0, split_weight[:, :, :, 0], split_weight[:, :, :, 1])

time: 524 us -> 464 us (0.89)
  waiting for transfers between devices: 234 us -> 174 us
    ppermute x7 -> x6, waiting for transfers between devices: 103 us -> 52.1 us  [shift(): lax.ppermute(value, axis, [(i, i + distance) for i in range(count - dista...]
    ppermute x1, starting transfers between devices: 17.7 us -> 0.63 us  [body(): partner_mixed = lax.ppermute(attn_mixed, 'core', swap)]
    ppermute x7 -> x6, starting transfers between devices: 31.4 us -> 42.9 us  [shift(): lax.ppermute(value, axis, [(i, i + distance) for i in range(count - dista...]
    reduce_scatter x1, waiting for transfers between devices: 34.6 us -> 23.6 us  [body(): lax.psum_scatter(partial_sum.astype(jnp.bfloat16), 'head', scatter_dimens...]
  transfers between devices with their start and end apart: 13 -> 14, of which waited for: 12 -> 13; matrix products, arithmetic and copies ran while one was open for 2% -> 3% of each run, Pallas kernels for 0% -> 0%
where the time goes in v5:
time: 464 us; the launch traced here: 458 us
  waiting for transfers between devices  174 us (38%)
  blocking collectives  139 us (30%)
  starting transfers between devices  51.2 us (11%)
  matrix products  39 us (8%)
  local copies, waits for them, and re-layouts  28 us (6%)
  between operations  14.1 us (3%)
  other arithmetic  11.9 us (3%)
    all_gather x1, waiting for transfers between devices, body(): lax.all_gather(by_group, ('q', 'core', 'head'), axis=1, tiled=False)  93.4 us
    all_to_all x1, blocking collectives, body(): lax.all_to_all(partial_value, CTX, split_axis=0, concat_axis=0, tiled=True)  84.4 us
    ppermute x6, waiting for transfers between devices, shift(): lax.ppermute(value, axis, [(i, i + distance) for i in range(count - dista...  52.1 us
    ppermute x6, starting transfers between devices, shift(): lax.ppermute(value, axis, [(i, i + distance) for i in range(count - dista...  42.9 us
    reduce_scatter x1, waiting for transfers between devices, body(): lax.psum_scatter(partial_sum.astype(jnp.bfloat16), 'head', scatter_dimens...  23.6 us
    all_gather x1, blocking collectives, body(): joined = lax.all_gather(hidden_units, 'head', axis=2, tiled=True)  23.2 us
    all_to_all x1, blocking collectives, body(): lax.all_to_all(packed, 'g', split_axis=0, concat_axis=0, tiled=True)  20 us
    dot_general x1, matrix products, body(): jnp.einsum('thr,hrqd->tqd', both_mixed, row_whole, preferred_element_type...  18.2 us
  transfers between devices with their start and end apart: 14, of which 13 were waited for; matrix products, arithmetic and copies ran while one was open for 3% of the time, Pallas kernels for 0%

profile of v5, /device:TPU:1, one launch (start us, length us, event | category | flops | bytes accessed | tf_op | source)
XLA Modules:
  0.0 457.9 jit_solution(12007850858215065400)
XLA Ops:
  8.5 3.3 collective-permute-start.9
  16.8 1.7 collective-permute-done
  19.0 1.9 collective-permute-start.1
  20.9 5.6 %collective-permute-done.1 = f32[4,136,128]{2,1,0:T(8,128)S(1)} collective-permute-done((f32[4,136,128]{2,1,0:T(8,128)S(1)}, f32[4,136,128]{2,1,0:T(8,128)S(1)}, u32[]{:S(2)}, u32[]{:S(2)}) %collective-permute-start.1) | collective-permute-done | bytes 278560 | tf_op jit(solution)/shard_map/ppermute | solution.py:30
  26.6 4.1 collective-permute-start.2
  30.7 5.9 %collective-permute-done.2 = f32[4,136,128]{2,1,0:T(8,128)S(1)} collective-permute-done((f32[4,136,128]{2,1,0:T(8,128)S(1)}, f32[4,136,128]{2,1,0:T(8,128)S(1)}, u32[]{:S(2)}, u32[]{:S(2)}) %collective-permute-start.2) | collective-permute-done | bytes 278560 | tf_op jit(solution)/shard_map/ppermute | solution.py:30
  37.0 7.6 %collective-permute-start.3 = (f32[4,136,128]{2,1,0:T(8,128)S(1)}, f32[4,136,128]{2,1,0:T(8,128)S(1)}, u32[]{:S(2)}, u32[]{:S(2)}) collective-permute-start(f32[4,136,128]{2,1,0:T(8,128)S(1)} %maximum_select_fusion), channel_id=1, source_target_pairs={{0,16},{8,24},{16,32},{24,40},{32,48},{40,56},{48,64},{56,72},{64,... | collective-permute-start | bytes 835592 | tf_op jit(solution)/shard_map/ppermute | solution.py:30
  44.6 9.2 %collective-permute-done.3 = f32[4,136,128]{2,1,0:T(8,128)S(1)} collective-permute-done((f32[4,136,128]{2,1,0:T(8,128)S(1)}, f32[4,136,128]{2,1,0:T(8,128)S(1)}, u32[]{:S(2)}, u32[]{:S(2)}) %collective-permute-start.3) | collective-permute-done | bytes 278560 | tf_op jit(solution)/shard_map/ppermute | solution.py:30
  54.2 15.5 %collective-permute-start.4 = (f32[4,136,128]{2,1,0:T(8,128)S(1)}, f32[4,136,128]{2,1,0:T(8,128)S(1)}, u32[]{:S(2)}, u32[]{:S(2)}) collective-permute-start(f32[4,136,128]{2,1,0:T(8,128)S(1)} %maximum_select_fusion.1), channel_id=1, source_target_pairs={{0,32},{8,40},{16,48},{24,56},{32,64},{40,72},{48,80},{56,88},{64,... | collective-permute-start | bytes 835592 | tf_op jit(solution)/shard_map/ppermute | solution.py:30
  69.7 16.6 %collective-permute-done.4 = f32[4,136,128]{2,1,0:T(8,128)S(1)} collective-permute-done((f32[4,136,128]{2,1,0:T(8,128)S(1)}, f32[4,136,128]{2,1,0:T(8,128)S(1)}, u32[]{:S(2)}, u32[]{:S(2)}) %collective-permute-start.4) | collective-permute-done | bytes 278560 | tf_op jit(solution)/shard_map/ppermute | solution.py:30
  86.6 6.3 %collective-permute-start.5 = (f32[4,136,128]{2,1,0:T(8,128)S(1)}, f32[4,136,128]{2,1,0:T(8,128)S(1)}, u32[]{:S(2)}, u32[]{:S(2)}) collective-permute-start(f32[4,136,128]{2,1,0:T(8,128)S(1)} %maximum_select_fusion.2), channel_id=1, source_target_pairs={{0,64},{8,72},{16,80},{24,88},{32,96},{40,104},{48,112},{56,120},{... | collective-permute-start | bytes 835592 | tf_op jit(solution)/shard_map/ppermute | solution.py:30
  92.9 11.2 %collective-permute-done.5 = f32[4,136,128]{2,1,0:T(8,128)S(1)} collective-permute-done((f32[4,136,128]{2,1,0:T(8,128)S(1)}, f32[4,136,128]{2,1,0:T(8,128)S(1)}, u32[]{:S(2)}, u32[]{:S(2)}) %collective-permute-start.5) | collective-permute-done | bytes 278560 | tf_op jit(solution)/shard_map/ppermute | solution.py:30
  104.5 7.5 %collective-permute-start.6 = (f32[4,136,128]{2,1,0:T(8,128)S(1)}, f32[4,136,128]{2,1,0:T(8,128)S(1)}, u32[]{:S(2)}, u32[]{:S(2)}) collective-permute-start(f32[4,136,128]{2,1,0:T(8,128)S(1)} %maximum_select_fusion.3), channel_id=1, source_target_pairs={{0,128},{8,136},{16,144},{24,152},{32,160},{40,168},{48,176},{56,1... | collective-permute-start | bytes 835592 | tf_op jit(solution)/shard_map/ppermute | solution.py:30
  113.0 3.5 collective-permute-done.6
  117.6 2.3 collective-permute-start.7
  122.5 2.5 fusion.10
  125.0 1.6 multiply_reduce_fusion.1
  128.7 18.2 %bitcast_convert_fusion = bf16[256,4,768]{2,0,1:T(8,128)(2,1)} fusion(bf16[8,128,4,768]{3,0,2,1:T(8,128)(2,1)} %all-gather.4.cloned.1.call-done, bf16[128,8,128]{2,0,1:T(8,128)(2,1)S(1)} %get-tuple-element.23, bf16[128,8,128]{2,0,1:T(8,128)(2,1)S(1)} %get-tuple-element.22), kind=kOutput, calls=%fused_computation.4 | convolution fusion | flops 1612447744 | bytes 8388608 | tf_op jit(solution)/shard_map/thr,hrqd->tqd/dot_general | solution.py:141
  149.4 23.6 %reduce-scatter.2.cloned.1.call-done = bf16[256,1,768]{2,0,1:T(8,128)(2,1)} async-done(((bf16[256,4,768]{2,0,1:T(8,128)(2,1)}), bf16[256,1,768]{2,0,1:T(8,128)(2,1)}) %reduce-scatter.2.cloned.1.call-update) | async-done | bytes 393232 | tf_op jit(solution)/shard_map/reduce_scatter | solution.py:144
  174.0 1.6 collective-permute-start.10
  179.1 1.6 fusion.13
  180.7 12.0 %psum.7 = f32[128,33]{0,1:T(8,128)S(1)} all-reduce(f32[128,33]{0,1:T(8,128)S(1)} %pad_maximum_fusion.7), channel_id=1, replica_groups=mesh['g'=8,'q'=4,'core'=2,'head'=4] {'head'}, use_global_device_ids=true, to_apply=%region_7.8 | all-reduce | flops 4224 | bytes 33792 | tf_op jit(solution)/shard_map/psum | solution.py:164
  194.3 20.0 %all_to_all.10 = bf16[8,10,1536]{2,1,0:T(8,128)(2,1)S(1)} all-to-all(bf16[8,10,1536]{2,1,0:T(8,128)(2,1)S(1)} %reshape.198), channel_id=1, replica_groups=mesh['g'=8,'q'=4,'core'=2,'head'=4] {'g'}, dimensions={0} | all-to-all | bytes 491520 | tf_op jit(solution)/shard_map/all_to_all | solution.py:197
  215.1 93.4 %all-gather.6.cloned.1.call-done = bf16[8,320,1536]{2,0,1:T(8,128)(2,1)} async-done(((bf16[8,10,1536]{2,0,1:T(8,128)(2,1)}), bf16[8,320,1536]{2,0,1:T(8,128)(2,1)}) %all-gather.6.cloned.1.call-update) | async-done | bytes 7864336 | tf_op jit(solution)/shard_map/all_gather | solution.py:198
  308.5 12.5 %copy.191 = bf16[8,8,10,4,1536]{4,3,2,1,0:T(4,128)(2,1)} copy(bf16[8,8,10,4,1536]{4,0,2,3,1:T(8,128)(2,1)} %bitcast.104) | data formatting | bytes 15728640 | tf_op jit(solution)/shard_map/transpose | solution.py:203
  321.0 5.7 %copy.211 = bf16[80,8,4,1536]{3,1,2,0:T(8,128)(2,1)S(1)} copy(bf16[80,8,4,1536]{3,2,1,0:T(4,128)(2,1)} %bitcast.103) | data formatting | bytes 15728640
  326.7 4.3 fusion.76
  331.0 3.6 fusion.12
  336.7 23.2 %all_gather.15 = bf16[64,10,576]{0,1,2:T(8,128)(2,1)S(1)} all-gather(bf16[64,10,144]{0,1,2:T(8,128)(2,1)S(1)} %copy.193), channel_id=1, replica_groups=mesh['g'=8,'q'=4,'core'=2,'head'=4] {'head'}, dimensions={2}, use_global_device_ids=true | all-gather | bytes 921600 | tf_op jit(solution)/shard_map/all_gather | solution.py:211
  359.9 1.8 convolution_convert_fusion
  362.9 84.4 %all_to_all.11 = bf16[64,10,1536]{2,1,0:T(8,128)(2,1)S(1)} all-to-all(bf16[64,10,1536]{2,1,0:T(8,128)(2,1)S(1)} %copy.195), channel_id=1, replica_groups=mesh['g'=8,'q'=4,'core'=2,'head'=4] {'g','q','core'}, dimensions={0} | all-to-all | bytes 3932160 | tf_op jit(solution)/shard_map/all_to_all | solution.py:215
  448.2 2.8 fusion.3
  (130 shorter events, 28.9 us)
Async XLA Ops:
  6.5 353.4 %copy-start = (bf16[576,1536]{1,0:T(8,128)(2,1)S(1)}, bf16[576,1536]{1,0:T(8,128)(2,1)}, u32[]{:S(2)}) copy-start(bf16[576,1536]{1,0:T(8,128)(2,1)} %param.27) | copy-start | bytes 5308420
  6.5 7.0 %copy-start.11 = (f32[128,8]{0,1:T(8,128)S(1)}, f32[128,8]{0,1:T(8,128)}, u32[]{:S(2)}) copy-start(f32[128,8]{0,1:T(8,128)} %param.18) | copy-start | bytes 12292
  6.5 7.4 %copy-start.7 = (bf16[128,1024]{1,0:T(8,128)(2,1)S(1)}, bf16[128,1024]{1,0:T(8,128)(2,1)}, u32[]{:S(2)}) copy-start(bf16[128,1024]{1,0:T(8,128)(2,1)} %param.15) | copy-start | bytes 786436
  6.5 122.2 %all-gather.4.cloned.1.call-start = ((), (), s32[]{:S(2)}) async-start(), calls=%async_computation.3 | async-start | bytes 6488064 | tf_op jit(solution)/shard_map/all_gather | solution.py:135
  8.5 4.2 collective-permute-start.9
  13.5 159.5 %reduce-scatter.2.cloned.1.call-start = ((), (), s32[]{:S(2)}) async-start(), calls=%async_computation.4 | async-start | bytes 1966080 | tf_op jit(solution)/shard_map/reduce_scatter | solution.py:144
  14.1 1.4 copy-start.4
  16.3 2.2 collective-permute-start
  18.5 18.4 %copy-start.1 = (f32[8,136,128]{2,1,0:T(8,128)}, f32[8,136,128]{2,1,0:T(8,128)S(1)}, u32[]{:S(2)}) copy-start(f32[8,136,128]{2,1,0:T(8,128)S(1)} %collective-permute-done) | copy-start | bytes 1671172
  19.0 7.5 %collective-permute-start.1 = (f32[4,136,128]{2,1,0:T(8,128)S(1)}, f32[4,136,128]{2,1,0:T(8,128)S(1)}, u32[]{:S(2)}, u32[]{:S(2)}) collective-permute-start(f32[4,136,128]{2,1,0:T(8,128)S(1)} %pad_maximum_fusion.4), channel_id=1, source_target_pairs={{0,8},{8,16},{16,24},{24,32},{32,40},{40,48},{48,56},{56,64},{64,7... | collective-permute-start | bytes 835592 | tf_op jit(solution)/shard_map/ppermute | solution.py:30
  26.6 10.1 %collective-permute-start.2 = (f32[4,136,128]{2,1,0:T(8,128)S(1)}, f32[4,136,128]{2,1,0:T(8,128)S(1)}, u32[]{:S(2)}, u32[]{:S(2)}) collective-permute-start(f32[4,136,128]{2,1,0:T(8,128)S(1)} %broadcast_select_fusion.5), channel_id=1, source_target_pairs={{0,8},{8,16},{16,24},{24,32},{32,40},{40,48},{48,56},{56,64},{64,7... | collective-permute-start | bytes 835592 | tf_op jit(solution)/shard_map/ppermute | solution.py:30
  37.0 16.8 %collective-permute-start.3 = (f32[4,136,128]{2,1,0:T(8,128)S(1)}, f32[4,136,128]{2,1,0:T(8,128)S(1)}, u32[]{:S(2)}, u32[]{:S(2)}) collective-permute-start(f32[4,136,128]{2,1,0:T(8,128)S(1)} %maximum_select_fusion), channel_id=1, source_target_pairs={{0,16},{8,24},{16,32},{24,40},{32,48},{40,56},{48,64},{56,72},{64,... | collective-permute-start | bytes 835592 | tf_op jit(solution)/shard_map/ppermute | solution.py:30
  54.1 58.0 %copy-start.8 = (bf16[128,1024]{1,0:T(8,128)(2,1)S(1)}, bf16[128,1024]{1,0:T(8,128)(2,1)}, u32[]{:S(2)}) copy-start(bf16[128,1024]{1,0:T(8,128)(2,1)} %param.17) | copy-start | bytes 786436
  54.2 32.1 %collective-permute-start.4 = (f32[4,136,128]{2,1,0:T(8,128)S(1)}, f32[4,136,128]{2,1,0:T(8,128)S(1)}, u32[]{:S(2)}, u32[]{:S(2)}) collective-permute-start(f32[4,136,128]{2,1,0:T(8,128)S(1)} %maximum_select_fusion.1), channel_id=1, source_target_pairs={{0,32},{8,40},{16,48},{24,56},{32,64},{40,72},{48,80},{56,88},{64,... | collective-permute-start | bytes 835592 | tf_op jit(solution)/shard_map/ppermute | solution.py:30
  86.6 17.6 %collective-permute-start.5 = (f32[4,136,128]{2,1,0:T(8,128)S(1)}, f32[4,136,128]{2,1,0:T(8,128)S(1)}, u32[]{:S(2)}, u32[]{:S(2)}) collective-permute-start(f32[4,136,128]{2,1,0:T(8,128)S(1)} %maximum_select_fusion.2), channel_id=1, source_target_pairs={{0,64},{8,72},{16,80},{24,88},{32,96},{40,104},{48,112},{56,120},{... | collective-permute-start | bytes 835592 | tf_op jit(solution)/shard_map/ppermute | solution.py:30
  104.5 12.0 %collective-permute-start.6 = (f32[4,136,128]{2,1,0:T(8,128)S(1)}, f32[4,136,128]{2,1,0:T(8,128)S(1)}, u32[]{:S(2)}, u32[]{:S(2)}) collective-permute-start(f32[4,136,128]{2,1,0:T(8,128)S(1)} %maximum_select_fusion.3), channel_id=1, source_target_pairs={{0,128},{8,136},{16,144},{24,152},{32,160},{40,168},{48,176},{56,1... | collective-permute-start | bytes 835592 | tf_op jit(solution)/shard_map/ppermute | solution.py:30
  117.6 3.8 collective-permute-start.7
  121.2 3.8 copy-start.5
  121.2 3.7 copy-start.6
  122.5 4.1 copy-start.10
  126.8 1.8 collective-permute-start.8
  128.7 18.3 %copy-start.9 = (s32[128,2]{0,1:T(2,128)S(1)}, s32[128,2]{0,1:T(2,128)}, u32[]{:S(2)}) copy-start(s32[128,2]{0,1:T(2,128)} %param.24) | copy-start | bytes 3076
  146.9 161.6 %all-gather.6.cloned.1.call-start = ((), (), s32[]{:S(2)}) async-start(), calls=%async_computation.5 | async-start | bytes 8110080 | tf_op jit(solution)/shard_map/all_gather | solution.py:198
  174.0 2.7 collective-permute-start.10
  177.8 16.5 %copy-start.2 = (bf16[128,768]{1,0:T(8,128)(2,1)}, bf16[128,768]{1,0:T(8,128)(2,1)S(1)}, u32[]{:S(2)}) copy-start(bf16[128,768]{1,0:T(8,128)(2,1)S(1)} %get-tuple-element.21) | copy-start | bytes 589828
  326.7 4.3 copy-start.12
  447.2 0.9 copy-start.3
Sparse Core Ops, SparseCore 0:
  13.6 99.2 all-gather.3
  147.1 25.8 reduce-scatter.1
  215.3 93.2 all-gather.5

commit v6 on v5

--- a/solution.py
+++ b/solution.py
@@ -195,14 +195,19 @@
         .reshape(EXP, MOST, share_width)
     )
     by_group = lax.all_to_all(packed, "g", split_axis=0, concat_axis=0, tiled=True)
-    arrived = lax.all_gather(by_group, ("q", "core", "head"), axis=1, tiled=False)
+    own_parity = lax.all_gather(by_group, ("q", "head"), axis=1, tiled=False)
+    other_parity = lax.ppermute(own_parity, "core", swap)
+    pairs = group // 2
+    arrived = jnp.stack(
+        [
+            jnp.where(core == 0, own_parity, other_parity),
+            jnp.where(core == 0, other_parity, own_parity),
+        ],
+        axis=2,
+    ).reshape(EXP, pairs, head_count, 2, MOST, share_width)
     sources = ctx_count
-    slots_now = arrived.shape[2]
-    flat_rows = (
-        arrived.reshape(EXP, group, head_count, slots_now, share_width)
-        .transpose(0, 1, 3, 2, 4)
-        .reshape(sources * slots_now, model_width)
-    )
+    slots_now = MOST
+    flat_rows = arrived.transpose(0, 1, 3, 4, 2, 5).reshape(sources * slots_now, model_width)
     gate_part = jnp.einsum("rd,fd->rf", flat_rows, expert_gate, preferred_element_type=jnp.float32)
     up_part = jnp.einsum("rd,fd->rf", flat_rows, expert_up, preferred_element_type=jnp.float32)
     hidden_units = (
@@ -212,8 +217,14 @@
     partial_value = jnp.einsum(
         "nmf,fd->nmd", joined, expert_down, preferred_element_type=jnp.float32
     ).astype(jnp.bfloat16)
-    returned = lax.all_to_all(partial_value, CTX, split_axis=0, concat_axis=0, tiled=True)
-    summed = jnp.sum(returned.astype(jnp.float32).reshape(EXP, group, MOST, share_width), axis=1)
+    by_parity = partial_value.reshape(EXP * pairs, 2, slots_now, share_width)
+    keep = jnp.where(core == 0, by_parity[:, 0], by_parity[:, 1])
+    give = jnp.where(core == 0, by_parity[:, 1], by_parity[:, 0])
+    pair_sum = (
+        keep.astype(jnp.float32) + lax.ppermute(give, "core", swap).astype(jnp.float32)
+    ).astype(jnp.bfloat16)
+    returned = lax.all_to_all(pair_sum, ("g", "q"), split_axis=0, concat_axis=0, tiled=True)
+    summed = jnp.sum(returned.astype(jnp.float32).reshape(EXP, pairs, MOST, share_width), axis=1)
     mixture = jnp.einsum("est,esd->td", weighted, summed, precision=highest)
     return (hidden_share + mixture).astype(jnp.bfloat16)
 

time: 464 us -> 456 us (0.983)
  the two profiles are of different devices: /device:TPU:1 before, /device:TPU:32 now
where the time goes in v6:
time: 456 us; the launch traced here: 449 us
  waiting for transfers between devices  181 us (40%)
  blocking collectives  117 us (26%)
  matrix products  40 us (9%)
  local copies, waits for them, and re-layouts  35.4 us (8%)
  starting transfers between devices  34.4 us (8%)
  other arithmetic  27.4 us (6%)
  between operations  13.9 us (3%)
    all_gather x1, waiting for transfers between devices, body(): own_parity = lax.all_gather(by_group, ('q', 'head'), axis=1, tiled=False)  74.9 us
    ppermute x6, waiting for transfers between devices, shift(): lax.ppermute(value, axis, [(i, i + distance) for i in range(count - dista...  57.7 us
    all_to_all x1, blocking collectives, body(): lax.all_to_all(pair_sum, ('g', 'q'), split_axis=0, concat_axis=0, tiled=T...  55.5 us
    ppermute x6, starting transfers between devices, shift(): lax.ppermute(value, axis, [(i, i + distance) for i in range(count - dista...  33.4 us
    reduce_scatter x1, waiting for transfers between devices, body(): lax.psum_scatter(partial_sum.astype(jnp.bfloat16), 'head', scatter_dimens...  31.8 us
    all_gather x1, blocking collectives, body(): joined = lax.all_gather(hidden_units, 'head', axis=2, tiled=True)  23.6 us
    all_to_all x1, blocking collectives, body(): lax.all_to_all(packed, 'g', split_axis=0, concat_axis=0, tiled=True)  22.5 us
    dot_general x1, matrix products, body(): jnp.einsum('thr,hrqd->tqd', both_mixed, row_whole, preferred_element_type...  18.2 us
  transfers between devices with their start and end apart: 16, of which 15 were waited for; matrix products, arithmetic and copies ran while one was open for 4% of the time, Pallas kernels for 0%

profile of v6, /device:TPU:32, one launch (start us, length us, event | category | flops | bytes accessed | tf_op | source)
XLA Modules:
  0.0 449.1 jit_solution(288270928071305970)
XLA Ops:
  16.2 3.8 collective-permute-start.1
  20.0 6.7 %collective-permute-done.1 = f32[4,136,128]{2,1,0:T(8,128)S(1)} collective-permute-done((f32[4,136,128]{2,1,0:T(8,128)S(1)}, f32[4,136,128]{2,1,0:T(8,128)S(1)}, u32[]{:S(2)}, u32[]{:S(2)}) %collective-permute-start.1) | collective-permute-done | bytes 278560 | tf_op jit(solution)/shard_map/ppermute | solution.py:30
  26.9 3.8 collective-permute-start.2
  30.7 8.0 %collective-permute-done.2 = f32[4,136,128]{2,1,0:T(8,128)S(1)} collective-permute-done((f32[4,136,128]{2,1,0:T(8,128)S(1)}, f32[4,136,128]{2,1,0:T(8,128)S(1)}, u32[]{:S(2)}, u32[]{:S(2)}) %collective-permute-start.2) | collective-permute-done | bytes 278560 | tf_op jit(solution)/shard_map/ppermute | solution.py:30
  39.1 8.6 %collective-permute-start.3 = (f32[4,136,128]{2,1,0:T(8,128)S(1)}, f32[4,136,128]{2,1,0:T(8,128)S(1)}, u32[]{:S(2)}, u32[]{:S(2)}) collective-permute-start(f32[4,136,128]{2,1,0:T(8,128)S(1)} %maximum_select_fusion), channel_id=1, source_target_pairs={{0,16},{8,24},{16,32},{24,40},{32,48},{40,56},{48,64},{56,72},{64,... | collective-permute-start | bytes 835592 | tf_op jit(solution)/shard_map/ppermute | solution.py:30
  47.7 10.6 %collective-permute-done.3 = f32[4,136,128]{2,1,0:T(8,128)S(1)} collective-permute-done((f32[4,136,128]{2,1,0:T(8,128)S(1)}, f32[4,136,128]{2,1,0:T(8,128)S(1)}, u32[]{:S(2)}, u32[]{:S(2)}) %collective-permute-start.3) | collective-permute-done | bytes 278560 | tf_op jit(solution)/shard_map/ppermute | solution.py:30
  58.6 7.4 %collective-permute-start.4 = (f32[4,136,128]{2,1,0:T(8,128)S(1)}, f32[4,136,128]{2,1,0:T(8,128)S(1)}, u32[]{:S(2)}, u32[]{:S(2)}) collective-permute-start(f32[4,136,128]{2,1,0:T(8,128)S(1)} %maximum_select_fusion.1), channel_id=1, source_target_pairs={{0,32},{8,40},{16,48},{24,56},{32,64},{40,72},{48,80},{56,88},{64,... | collective-permute-start | bytes 835592 | tf_op jit(solution)/shard_map/ppermute | solution.py:30
  66.0 16.1 %collective-permute-done.4 = f32[4,136,128]{2,1,0:T(8,128)S(1)} collective-permute-done((f32[4,136,128]{2,1,0:T(8,128)S(1)}, f32[4,136,128]{2,1,0:T(8,128)S(1)}, u32[]{:S(2)}, u32[]{:S(2)}) %collective-permute-start.4) | collective-permute-done | bytes 278560 | tf_op jit(solution)/shard_map/ppermute | solution.py:30
  82.4 6.5 %collective-permute-start.5 = (f32[4,136,128]{2,1,0:T(8,128)S(1)}, f32[4,136,128]{2,1,0:T(8,128)S(1)}, u32[]{:S(2)}, u32[]{:S(2)}) collective-permute-start(f32[4,136,128]{2,1,0:T(8,128)S(1)} %maximum_select_fusion.2), channel_id=1, source_target_pairs={{0,64},{8,72},{16,80},{24,88},{32,96},{40,104},{48,112},{56,120},{... | collective-permute-start | bytes 835592 | tf_op jit(solution)/shard_map/ppermute | solution.py:30
  88.9 12.2 %collective-permute-done.5 = f32[4,136,128]{2,1,0:T(8,128)S(1)} collective-permute-done((f32[4,136,128]{2,1,0:T(8,128)S(1)}, f32[4,136,128]{2,1,0:T(8,128)S(1)}, u32[]{:S(2)}, u32[]{:S(2)}) %collective-permute-start.5) | collective-permute-done | bytes 278560 | tf_op jit(solution)/shard_map/ppermute | solution.py:30
  101.4 3.3 collective-permute-start.6
  105.6 4.1 collective-permute-done.6
  120.0 18.2 %bitcast_convert_fusion = bf16[256,4,768]{2,0,1:T(8,128)(2,1)} fusion(bf16[8,128,4,768]{3,0,2,1:T(8,128)(2,1)} %all-gather.4.cloned.1.call-done, bf16[128,8,128]{2,0,1:T(8,128)(2,1)S(1)} %get-tuple-element.27, bf16[128,8,128]{2,0,1:T(8,128)(2,1)S(1)} %get-tuple-element.26), kind=kOutput, calls=%fused_computation.7 | convolution fusion | flops 1612447744 | bytes 8388608 | tf_op jit(solution)/shard_map/thr,hrqd->tqd/dot_general | solution.py:141
  140.6 31.8 %reduce-scatter.2.cloned.1.call-done = bf16[256,1,768]{2,0,1:T(8,128)(2,1)} async-done(((bf16[256,4,768]{2,0,1:T(8,128)(2,1)}), bf16[256,1,768]{2,0,1:T(8,128)(2,1)}) %reduce-scatter.2.cloned.1.call-update) | async-done | bytes 393232 | tf_op jit(solution)/shard_map/reduce_scatter | solution.py:144
  179.0 15.8 %psum.7 = f32[128,33]{0,1:T(8,128)S(1)} all-reduce(f32[128,33]{0,1:T(8,128)S(1)} %pad_maximum_fusion.8), channel_id=1, replica_groups=mesh['g'=8,'q'=4,'core'=2,'head'=4] {'head'}, use_global_device_ids=true, to_apply=%region_7.8 | all-reduce | flops 4224 | bytes 33792 | tf_op jit(solution)/shard_map/psum | solution.py:164
  196.4 22.5 %all_to_all.10 = bf16[8,10,1536]{2,1,0:T(8,128)(2,1)S(1)} all-to-all(bf16[8,10,1536]{2,1,0:T(8,128)(2,1)S(1)} %reshape.209), channel_id=1, replica_groups=mesh['g'=8,'q'=4,'core'=2,'head'=4] {'g'}, dimensions={0} | all-to-all | bytes 491520 | tf_op jit(solution)/shard_map/all_to_all | solution.py:197
  219.8 74.9 %all-gather.6.cloned.1.call-done = bf16[8,160,1536]{2,0,1:T(8,128)(2,1)} async-done(((bf16[8,10,1536]{2,0,1:T(8,128)(2,1)}), bf16[8,160,1536]{2,0,1:T(8,128)(2,1)}) %all-gather.6.cloned.1.call-update) | async-done | bytes 3932176 | tf_op jit(solution)/shard_map/all_gather | solution.py:198
  294.7 7.0 %collective-permute-done.11 = bf16[8,16,10,1536]{3,0,2,1:T(8,128)(2,1)S(1)} collective-permute-done((bf16[8,16,10,1536]{3,0,2,1:T(8,128)(2,1)}, bf16[8,16,10,1536]{3,0,2,1:T(8,128)(2,1)S(1)}, u32[]{:S(2)}, u32[]{:S(2)}) %collective-permute-start.11) | collective-permute-done | bytes 3932192 | tf_op jit(solution)/shard_map/ppermute | solution.py:199
  301.7 2.6 broadcast_select_fusion.1
  304.3 5.0 %copy.207 = bf16[8,4,4,1,10,1536]{5,2,4,3,1,0:T(4,128)(2,1)} copy(bf16[8,4,4,1,10,1536]{5,0,4,2,1,3:T(8,128)(2,1)S(1)} %bitcast.113) | data formatting | bytes 7864320 | tf_op jit(solution)/shard_map/stack | solution.py:201
  309.3 5.0 %copy.208 = bf16[8,4,4,1,10,1536]{5,2,4,3,1,0:T(4,128)(2,1)} copy(bf16[8,4,4,1,10,1536]{5,0,4,2,1,3:T(8,128)(2,1)S(1)} %bitcast.112) | data formatting | bytes 7864320 | tf_op jit(solution)/shard_map/stack | solution.py:201
  314.3 12.4 %pad_maximum_fusion = bf16[8,4,4,2,10,1536]{5,2,4,3,1,0:T(4,128)(2,1)} fusion(bf16[8,4,4,1,10,1536]{5,2,4,3,1,0:T(4,128)(2,1)} %copy.208, bf16[8,4,4,1,10,1536]{5,2,4,3,1,0:T(4,128)(2,1)} %copy.207), kind=kLoop, calls=%fused_computation | loop fusion | flops 3932160 | bytes 15728640 | tf_op jit(solution)/shard_map/stack | solution.py:201
  326.7 5.7 %copy.232 = bf16[80,8,4,1536]{3,1,2,0:T(8,128)(2,1)S(1)} copy(bf16[80,8,4,1536]{3,2,1,0:T(4,128)(2,1)} %bitcast.111) | data formatting | bytes 15728640
  332.4 4.3 fusion.78
  336.7 3.3 fusion.13
  342.2 23.6 %all_gather.15 = bf16[64,10,576]{0,1,2:T(8,128)(2,1)S(1)} all-gather(bf16[64,10,144]{0,1,2:T(8,128)(2,1)S(1)} %copy.210), channel_id=1, replica_groups=mesh['g'=8,'q'=4,'core'=2,'head'=4] {'head'}, dimensions={2}, use_global_device_ids=true | all-gather | bytes 921600 | tf_op jit(solution)/shard_map/all_gather | solution.py:216
  365.7 3.1 convolution_convert_fusion
  368.8 5.0 %reshape.212 = bf16[32,2,10,1536]{3,1,0,2:T(2,128)(2,1)} reshape(bf16[64,10,1536]{2,0,1:T(8,128)(2,1)} %convolution_convert_fusion) | data formatting | bytes 3932160 | tf_op jit(solution)/shard_map/reshape | solution.py:220
  373.8 5.1 %fusion.73 = (bf16[32,1,10,1536]{3,1,0,2:T(2,128)(2,1)S(1)}, bf16[32,1,10,1536]{3,1,0,2:T(2,128)(2,1)S(1)}) fusion(bf16[32,2,10,1536]{3,1,0,2:T(2,128)(2,1)} %reshape.212), kind=kLoop, calls=%fused_computation.163 | loop fusion | bytes 3932160 | tf_op jit(solution)/shard_map/slice | solution.py:221
  379.4 2.6 collective-permute-done.12
  383.1 55.5 %all_to_all.11 = bf16[32,10,1536]{2,1,0:T(8,128)(2,1)S(1)} all-to-all(bf16[32,10,1536]{2,1,0:T(8,128)(2,1)S(1)} %copy.214), channel_id=1, replica_groups=mesh['g'=8,'q'=4,'core'=2,'head'=4] {'g','q'}, dimensions={0} | all-to-all | bytes 1966080 | tf_op jit(solution)/shard_map/all_to_all | solution.py:226
  439.6 2.8 fusion.3
  (141 shorter events, 38.1 us)
Async XLA Ops:
  6.5 359.2 %copy-start = (bf16[576,1536]{1,0:T(8,128)(2,1)S(1)}, bf16[576,1536]{1,0:T(8,128)(2,1)}, u32[]{:S(2)}) copy-start(bf16[576,1536]{1,0:T(8,128)(2,1)} %param.27) | copy-start | bytes 5308420
  6.5 4.2 copy-start.11
  6.5 4.5 %copy-start.7 = (bf16[128,1024]{1,0:T(8,128)(2,1)S(1)}, bf16[128,1024]{1,0:T(8,128)(2,1)}, u32[]{:S(2)}) copy-start(bf16[128,1024]{1,0:T(8,128)(2,1)} %param.15) | copy-start | bytes 786436
  6.5 113.4 %all-gather.4.cloned.1.call-start = ((), (), s32[]{:S(2)}) async-start(), calls=%async_computation.3 | async-start | bytes 6488064 | tf_op jit(solution)/shard_map/all_gather | solution.py:135
  8.5 1.4 collective-permute-start.9
  10.6 161.8 %reduce-scatter.2.cloned.1.call-start = ((), (), s32[]{:S(2)}) async-start(), calls=%async_computation.4 | async-start | bytes 1966080 | tf_op jit(solution)/shard_map/reduce_scatter | solution.py:144
  11.3 1.4 copy-start.4
  13.5 2.2 collective-permute-start
  15.6 23.3 %copy-start.1 = (f32[8,136,128]{2,1,0:T(8,128)}, f32[8,136,128]{2,1,0:T(8,128)S(1)}, u32[]{:S(2)}) copy-start(f32[8,136,128]{2,1,0:T(8,128)S(1)} %collective-permute-done) | copy-start | bytes 1671172
  16.2 10.6 %collective-permute-start.1 = (f32[4,136,128]{2,1,0:T(8,128)S(1)}, f32[4,136,128]{2,1,0:T(8,128)S(1)}, u32[]{:S(2)}, u32[]{:S(2)}) collective-permute-start(f32[4,136,128]{2,1,0:T(8,128)S(1)} %pad_maximum_fusion.5), channel_id=1, source_target_pairs={{0,8},{8,16},{16,24},{24,32},{32,40},{40,48},{48,56},{56,64},{64,7... | collective-permute-start | bytes 835592 | tf_op jit(solution)/shard_map/ppermute | solution.py:30
  26.9 11.8 %collective-permute-start.2 = (f32[4,136,128]{2,1,0:T(8,128)S(1)}, f32[4,136,128]{2,1,0:T(8,128)S(1)}, u32[]{:S(2)}, u32[]{:S(2)}) collective-permute-start(f32[4,136,128]{2,1,0:T(8,128)S(1)} %broadcast_select_fusion.7), channel_id=1, source_target_pairs={{0,8},{8,16},{16,24},{24,32},{32,40},{40,48},{48,56},{56,64},{64,7... | collective-permute-start | bytes 835592 | tf_op jit(solution)/shard_map/ppermute | solution.py:30
  39.1 19.2 %collective-permute-start.3 = (f32[4,136,128]{2,1,0:T(8,128)S(1)}, f32[4,136,128]{2,1,0:T(8,128)S(1)}, u32[]{:S(2)}, u32[]{:S(2)}) collective-permute-start(f32[4,136,128]{2,1,0:T(8,128)S(1)} %maximum_select_fusion), channel_id=1, source_target_pairs={{0,16},{8,24},{16,32},{24,40},{32,48},{40,56},{48,64},{56,72},{64,... | collective-permute-start | bytes 835592 | tf_op jit(solution)/shard_map/ppermute | solution.py:30
  58.5 46.2 %copy-start.8 = (bf16[128,1024]{1,0:T(8,128)(2,1)S(1)}, bf16[128,1024]{1,0:T(8,128)(2,1)}, u32[]{:S(2)}) copy-start(bf16[128,1024]{1,0:T(8,128)(2,1)} %param.17) | copy-start | bytes 786436
  58.6 23.5 %collective-permute-start.4 = (f32[4,136,128]{2,1,0:T(8,128)S(1)}, f32[4,136,128]{2,1,0:T(8,128)S(1)}, u32[]{:S(2)}, u32[]{:S(2)}) collective-permute-start(f32[4,136,128]{2,1,0:T(8,128)S(1)} %maximum_select_fusion.1), channel_id=1, source_target_pairs={{0,32},{8,40},{16,48},{24,56},{32,64},{40,72},{48,80},{56,88},{64,... | collective-permute-start | bytes 835592 | tf_op jit(solution)/shard_map/ppermute | solution.py:30
  82.4 18.6 %collective-permute-start.5 = (f32[4,136,128]{2,1,0:T(8,128)S(1)}, f32[4,136,128]{2,1,0:T(8,128)S(1)}, u32[]{:S(2)}, u32[]{:S(2)}) collective-permute-start(f32[4,136,128]{2,1,0:T(8,128)S(1)} %maximum_select_fusion.2), channel_id=1, source_target_pairs={{0,64},{8,72},{16,80},{24,88},{32,96},{40,104},{48,112},{56,120},{... | collective-permute-start | bytes 835592 | tf_op jit(solution)/shard_map/ppermute | solution.py:30
  101.4 8.4 %collective-permute-start.6 = (f32[4,136,128]{2,1,0:T(8,128)S(1)}, f32[4,136,128]{2,1,0:T(8,128)S(1)}, u32[]{:S(2)}, u32[]{:S(2)}) collective-permute-start(f32[4,136,128]{2,1,0:T(8,128)S(1)} %maximum_select_fusion.3), channel_id=1, source_target_pairs={{0,128},{8,136},{16,144},{24,152},{32,160},{40,168},{48,176},{56,1... | collective-permute-start | bytes 835592 | tf_op jit(solution)/shard_map/ppermute | solution.py:30
  110.8 1.9 collective-permute-start.7
  112.1 4.1 copy-start.5
  112.1 4.1 copy-start.6
  113.7 4.1 copy-start.10
  118.1 1.8 collective-permute-start.8
  120.0 18.3 %copy-start.9 = (s32[128,2]{0,1:T(2,128)S(1)}, s32[128,2]{0,1:T(2,128)}, u32[]{:S(2)}) copy-start(s32[128,2]{0,1:T(2,128)} %param.24) | copy-start | bytes 3076
  138.2 156.5 %all-gather.6.cloned.1.call-start = ((), (), s32[]{:S(2)}) async-start(), calls=%async_computation.5 | async-start | bytes 4177920 | tf_op jit(solution)/shard_map/all_gather | solution.py:198
  173.5 1.5 collective-permute-start.10
  176.1 20.3 %copy-start.2 = (bf16[128,768]{1,0:T(8,128)(2,1)}, bf16[128,768]{1,0:T(8,128)(2,1)S(1)}, u32[]{:S(2)}) copy-start(bf16[128,768]{1,0:T(8,128)(2,1)S(1)} %get-tuple-element.25) | copy-start | bytes 589828
  294.7 7.0 %collective-permute-start.11 = (bf16[8,16,10,1536]{3,0,2,1:T(8,128)(2,1)}, bf16[8,16,10,1536]{3,0,2,1:T(8,128)(2,1)S(1)}, u32[]{:S(2)}, u32[]{:S(2)}) collective-permute-start(bf16[8,16,10,1536]{3,0,2,1:T(8,128)(2,1)} %bitcast.116), channel_id=1, source_target_pairs={{0,4},{4,0},{1,5},{5,1},{2,6},{6,2},{3,7},{7,3},{8,12},{12,8},{9,1... | collective-permute-start | bytes 11796488 | tf_op jit(solution)/shard_map/ppermute | solution.py:199
  332.4 4.3 copy-start.12
  379.1 2.8 collective-permute-start.12
  438.7 0.9 copy-start.3
Sparse Core Ops, SparseCore 0:
  10.8 99.5 all-gather.3
  138.3 34.0 reduce-scatter.1
  219.9 74.7 all-gather.5

commit v7 on v5

--- a/solution.py
+++ b/solution.py
@@ -195,25 +195,32 @@
         .reshape(EXP, MOST, share_width)
     )
     by_group = lax.all_to_all(packed, "g", split_axis=0, concat_axis=0, tiled=True)
-    arrived = lax.all_gather(by_group, ("q", "core", "head"), axis=1, tiled=False)
-    sources = ctx_count
-    slots_now = arrived.shape[2]
-    flat_rows = (
-        arrived.reshape(EXP, group, head_count, slots_now, share_width)
-        .transpose(0, 1, 3, 2, 4)
-        .reshape(sources * slots_now, model_width)
-    )
-    gate_part = jnp.einsum("rd,fd->rf", flat_rows, expert_gate, preferred_element_type=jnp.float32)
-    up_part = jnp.einsum("rd,fd->rf", flat_rows, expert_up, preferred_element_type=jnp.float32)
-    hidden_units = (
-        (jax.nn.silu(gate_part) * up_part).astype(jnp.bfloat16).reshape(sources, slots_now, -1)
-    )
-    joined = lax.all_gather(hidden_units, "head", axis=2, tiled=True)
-    partial_value = jnp.einsum(
-        "nmf,fd->nmd", joined, expert_down, preferred_element_type=jnp.float32
+    wide = lax.all_gather(by_group, "head", axis=2, tiled=True)
+    own_parity = lax.all_gather(wide, "q", axis=0, tiled=False)
+    other_parity = lax.ppermute(own_parity, "core", swap)
+    pairs = group // 2
+    halves = []
+    for part in (own_parity, other_parity):
+        part_rows = part.reshape(-1, model_width)
+        gate_part = jnp.einsum(
+            "rd,fd->rf", part_rows, expert_gate, preferred_element_type=jnp.float32
+        )
+        up_part = jnp.einsum("rd,fd->rf", part_rows, expert_up, preferred_element_type=jnp.float32)
+        halves.append((jax.nn.silu(gate_part) * up_part).astype(jnp.bfloat16))
+    hidden_units = jnp.concatenate(halves, axis=0)
+    joined = lax.all_gather(hidden_units, "head", axis=1, tiled=True)
+    partial_value = (
+        jnp.dot(joined, expert_down, preferred_element_type=jnp.float32)
+        .astype(jnp.bfloat16)
+        .reshape(2, pairs, EXP, MOST, share_width)
+    )
+    pair_sum = (
+        partial_value[0].astype(jnp.float32)
+        + lax.ppermute(partial_value[1], "core", swap).astype(jnp.float32)
     ).astype(jnp.bfloat16)
-    returned = lax.all_to_all(partial_value, CTX, split_axis=0, concat_axis=0, tiled=True)
-    summed = jnp.sum(returned.astype(jnp.float32).reshape(EXP, group, MOST, share_width), axis=1)
+    outgoing = pair_sum.transpose(1, 0, 2, 3).reshape(EXP * pairs, MOST, share_width)
+    returned = lax.all_to_all(outgoing, ("g", "q"), split_axis=0, concat_axis=0, tiled=True)
+    summed = jnp.sum(returned.astype(jnp.float32).reshape(EXP, pairs, MOST, share_width), axis=1)
     mixture = jnp.einsum("est,esd->td", weighted, summed, precision=highest)
     return (hidden_share + mixture).astype(jnp.bfloat16)
 

time: 464 us -> 443 us (0.955)
  blocking collectives: 139 us -> 104 us
  local copies, waits for them, and re-layouts: 28 us -> 46.1 us
  waiting for transfers between devices: 174 us -> 163 us
  other arithmetic: 11.9 us -> 16.6 us
    all_to_all x1, blocking collectives: 84.4 us -> 45.3 us  [body(): lax.all_to_all(outgoing, ('g', 'q'), split_axis=0, concat_axis=0, tiled=T...]
    reshape x2 -> x3, local copies, waits for them, and re-layouts: 1.04 us -> 15.3 us  [the longest x2 15.2 us: body(): part_rows = part.reshape(-1, model_width)]
    transpose x1 -> x0, local copies, waits for them, and re-layouts: 12.5 us -> none  [body(): flat_rows = arrived.reshape(EXP, group, head_count, slots_now, share_widt...]
    all_gather x1, waiting for transfers between devices: 93.4 us -> 81.7 us  [body(): own_parity = lax.all_gather(wide, 'q', axis=0, tiled=False)]
    all_gather x0 -> x3, local copies, waits for them, and re-layouts: none -> 11.3 us  [the longest x2 9.8 us: body(): own_parity = lax.all_gather(wide, 'q', axis=0, tiled=False)]
    ppermute x0 -> x1, local copies, waits for them, and re-layouts: none -> 7.35 us  [body(): other_parity = lax.ppermute(own_parity, 'core', swap)]
    unnamed x30 -> x47, local copies, waits for them, and re-layouts: 7.16 us -> 1.91 us
    all_gather x1 -> x2, blocking collectives: 23.2 us -> 26.7 us  [the longest x1 14.5 us: body(): wide = lax.all_gather(by_group, 'head', axis=2, tiled=True)]
  transfers between devices with their start and end apart: 14 -> 16, of which waited for: 13 -> 13; matrix products, arithmetic and copies ran while one was open for 3% -> 9% of each run, Pallas kernels for 0% -> 0%
where the time goes in v7:
time: 443 us; the launch traced here: 440 us
  waiting for transfers between devices  163 us (37%)
  blocking collectives  104 us (23%)
  starting transfers between devices  54 us (12%)
  local copies, waits for them, and re-layouts  46.1 us (10%)
  matrix products  42.5 us (10%)
  other arithmetic  16.6 us (4%)
  between operations  13.8 us (3%)
    all_gather x1, waiting for transfers between devices, body(): own_parity = lax.all_gather(wide, 'q', axis=0, tiled=False)  81.7 us
    ppermute x6, waiting for transfers between devices, shift(): lax.ppermute(value, axis, [(i, i + distance) for i in range(count - dista...  52 us
    all_to_all x1, blocking collectives, body(): lax.all_to_all(outgoing, ('g', 'q'), split_axis=0, concat_axis=0, tiled=T...  45.3 us
    ppermute x6, starting transfers between devices, shift(): lax.ppermute(value, axis, [(i, i + distance) for i in range(count - dista...  42.8 us
    reduce_scatter x1, waiting for transfers between devices, body(): lax.psum_scatter(partial_sum.astype(jnp.bfloat16), 'head', scatter_dimens...  23.7 us
    all_to_all x1, blocking collectives, body(): lax.all_to_all(packed, 'g', split_axis=0, concat_axis=0, tiled=True)  20 us
    dot_general x1, matrix products, body(): jnp.einsum('thr,hrqd->tqd', both_mixed, row_whole, preferred_element_type...  18.2 us
    reshape x2, local copies, waits for them, and re-layouts, body(): part_rows = part.reshape(-1, model_width)  15.2 us
  transfers between devices with their start and end apart: 16, of which 13 were waited for; matrix products, arithmetic and copies ran while one was open for 9% of the time, Pallas kernels for 0%

profile of v7, /device:TPU:1, one launch (start us, length us, event | category | flops | bytes accessed | tf_op | source)
XLA Modules:
  0.0 439.6 jit_solution(2378384130264842564)
XLA Ops:
  8.5 3.3 collective-permute-start.9
  20.9 5.6 %collective-permute-done.1 = f32[4,136,128]{2,1,0:T(8,128)S(1)} collective-permute-done((f32[4,136,128]{2,1,0:T(8,128)S(1)}, f32[4,136,128]{2,1,0:T(8,128)S(1)}, u32[]{:S(2)}, u32[]{:S(2)}) %collective-permute-start.1) | collective-permute-done | bytes 278560 | tf_op jit(solution)/shard_map/ppermute | solution.py:30
  26.6 4.1 collective-permute-start.2
  30.7 5.9 %collective-permute-done.2 = f32[4,136,128]{2,1,0:T(8,128)S(1)} collective-permute-done((f32[4,136,128]{2,1,0:T(8,128)S(1)}, f32[4,136,128]{2,1,0:T(8,128)S(1)}, u32[]{:S(2)}, u32[]{:S(2)}) %collective-permute-start.2) | collective-permute-done | bytes 278560 | tf_op jit(solution)/shard_map/ppermute | solution.py:30
  37.0 7.6 %collective-permute-start.3 = (f32[4,136,128]{2,1,0:T(8,128)S(1)}, f32[4,136,128]{2,1,0:T(8,128)S(1)}, u32[]{:S(2)}, u32[]{:S(2)}) collective-permute-start(f32[4,136,128]{2,1,0:T(8,128)S(1)} %maximum_select_fusion), channel_id=1, source_target_pairs={{0,16},{8,24},{16,32},{24,40},{32,48},{40,56},{48,64},{56,72},{64,... | collective-permute-start | bytes 835592 | tf_op jit(solution)/shard_map/ppermute | solution.py:30
  44.6 9.2 %collective-permute-done.3 = f32[4,136,128]{2,1,0:T(8,128)S(1)} collective-permute-done((f32[4,136,128]{2,1,0:T(8,128)S(1)}, f32[4,136,128]{2,1,0:T(8,128)S(1)}, u32[]{:S(2)}, u32[]{:S(2)}) %collective-permute-start.3) | collective-permute-done | bytes 278560 | tf_op jit(solution)/shard_map/ppermute | solution.py:30
  54.1 15.5 %collective-permute-start.4 = (f32[4,136,128]{2,1,0:T(8,128)S(1)}, f32[4,136,128]{2,1,0:T(8,128)S(1)}, u32[]{:S(2)}, u32[]{:S(2)}) collective-permute-start(f32[4,136,128]{2,1,0:T(8,128)S(1)} %maximum_select_fusion.1), channel_id=1, source_target_pairs={{0,32},{8,40},{16,48},{24,56},{32,64},{40,72},{48,80},{56,88},{64,... | collective-permute-start | bytes 835592 | tf_op jit(solution)/shard_map/ppermute | solution.py:30
  69.7 16.6 %collective-permute-done.4 = f32[4,136,128]{2,1,0:T(8,128)S(1)} collective-permute-done((f32[4,136,128]{2,1,0:T(8,128)S(1)}, f32[4,136,128]{2,1,0:T(8,128)S(1)}, u32[]{:S(2)}, u32[]{:S(2)}) %collective-permute-start.4) | collective-permute-done | bytes 278560 | tf_op jit(solution)/shard_map/ppermute | solution.py:30
  86.6 6.4 %collective-permute-start.5 = (f32[4,136,128]{2,1,0:T(8,128)S(1)}, f32[4,136,128]{2,1,0:T(8,128)S(1)}, u32[]{:S(2)}, u32[]{:S(2)}) collective-permute-start(f32[4,136,128]{2,1,0:T(8,128)S(1)} %maximum_select_fusion.2), channel_id=1, source_target_pairs={{0,64},{8,72},{16,80},{24,88},{32,96},{40,104},{48,112},{56,120},{... | collective-permute-start | bytes 835592 | tf_op jit(solution)/shard_map/ppermute | solution.py:30
  93.0 11.3 %collective-permute-done.5 = f32[4,136,128]{2,1,0:T(8,128)S(1)} collective-permute-done((f32[4,136,128]{2,1,0:T(8,128)S(1)}, f32[4,136,128]{2,1,0:T(8,128)S(1)}, u32[]{:S(2)}, u32[]{:S(2)}) %collective-permute-start.5) | collective-permute-done | bytes 278560 | tf_op jit(solution)/shard_map/ppermute | solution.py:30
  104.6 7.3 %collective-permute-start.6 = (f32[4,136,128]{2,1,0:T(8,128)S(1)}, f32[4,136,128]{2,1,0:T(8,128)S(1)}, u32[]{:S(2)}, u32[]{:S(2)}) collective-permute-start(f32[4,136,128]{2,1,0:T(8,128)S(1)} %maximum_select_fusion.3), channel_id=1, source_target_pairs={{0,128},{8,136},{16,144},{24,152},{32,160},{40,168},{48,176},{56,1... | collective-permute-start | bytes 835592 | tf_op jit(solution)/shard_map/ppermute | solution.py:30
  112.9 3.4 collective-permute-done.6
  117.4 2.4 collective-permute-start.7
  122.4 2.5 fusion.9
  128.6 18.2 %bitcast_convert_fusion = bf16[256,4,768]{2,0,1:T(8,128)(2,1)} fusion(bf16[8,128,4,768]{3,0,2,1:T(8,128)(2,1)} %all-gather.4.cloned.1.call-done, bf16[128,8,128]{2,0,1:T(8,128)(2,1)S(1)} %get-tuple-element.25, bf16[128,8,128]{2,0,1:T(8,128)(2,1)S(1)} %get-tuple-element.24), kind=kOutput, calls=%fused_computation.4 | convolution fusion | flops 1612447744 | bytes 8388608 | tf_op jit(solution)/shard_map/thr,hrqd->tqd/dot_general | solution.py:141
  149.3 23.7 %reduce-scatter.2.cloned.1.call-done = bf16[256,1,768]{2,0,1:T(8,128)(2,1)} async-done(((bf16[256,4,768]{2,0,1:T(8,128)(2,1)}), bf16[256,1,768]{2,0,1:T(8,128)(2,1)}) %reduce-scatter.2.cloned.1.call-update) | async-done | bytes 393232 | tf_op jit(solution)/shard_map/reduce_scatter | solution.py:144
  180.7 12.0 %psum.7 = f32[128,33]{0,1:T(8,128)S(1)} all-reduce(f32[128,33]{0,1:T(8,128)S(1)} %pad_maximum_fusion.8), channel_id=1, replica_groups=mesh['g'=8,'q'=4,'core'=2,'head'=4] {'head'}, use_global_device_ids=true, to_apply=%region_7.8 | all-reduce | flops 4224 | bytes 33792 | tf_op jit(solution)/shard_map/psum | solution.py:164
  194.9 20.0 %all_to_all.10 = bf16[8,10,1536]{2,1,0:T(8,128)(2,1)S(1)} all-to-all(bf16[8,10,1536]{2,1,0:T(8,128)(2,1)S(1)} %reshape.205), channel_id=1, replica_groups=mesh['g'=8,'q'=4,'core'=2,'head'=4] {'g'}, dimensions={0} | all-to-all | bytes 491520 | tf_op jit(solution)/shard_map/all_to_all | solution.py:197
  214.9 14.5 %all_gather.16 = bf16[8,10,6144]{2,1,0:T(8,128)(2,1)S(1)} all-gather(bf16[8,10,1536]{2,1,0:T(8,128)(2,1)S(1)} %all_to_all.10), channel_id=1, replica_groups=mesh['g'=8,'q'=4,'core'=2,'head'=4] {'head'}, dimensions={2}, use_global_device_ids=true | all-gather | bytes 1228800 | tf_op jit(solution)/shard_map/all_gather | solution.py:198
  231.0 81.7 %all-gather.6.cloned.1.call-done = bf16[32,10,6144]{2,0,1:T(8,128)(2,1)} async-done(((bf16[8,10,6144]{2,0,1:T(8,128)(2,1)}), bf16[32,10,6144]{2,0,1:T(8,128)(2,1)}) %all-gather.6.cloned.1.call-update) | async-done | bytes 3932176 | tf_op jit(solution)/shard_map/all_gather | solution.py:199
  312.7 4.7 %copy.194 = bf16[4,8,10,6144]{3,1,2,0:T(8,128)(2,1)} copy(bf16[4,8,10,6144]{3,1,0,2:T(8,128)(2,1)} %bitcast.104) | data formatting | bytes 7864320 | tf_op jit(solution)/shard_map/all_gather | solution.py:199
  318.3 5.1 %copy.193 = bf16[32,10,6144]{2,1,0:T(8,128)(2,1)} copy(bf16[32,10,6144]{2,0,1:T(8,128)(2,1)S(1)} %copy-done.3) | data formatting | bytes 7864320 | tf_op jit(solution)/shard_map/all_gather | solution.py:199
  323.4 7.7 %reshape.206 = bf16[320,6144]{1,0:T(8,128)(2,1)} reshape(bf16[32,10,6144]{2,1,0:T(8,128)(2,1)} %copy.193) | data formatting | bytes 7864320 | tf_op jit(solution)/shard_map/reshape | solution.py:204
  331.1 3.8 fusion.76
  337.2 7.4 %copy.195 = bf16[4,8,10,6144]{3,2,1,0:T(8,128)(2,1)} copy(bf16[4,8,10,6144]{3,1,2,0:T(8,128)(2,1)} %collective-permute-done.11) | data formatting | bytes 7864320 | tf_op jit(solution)/shard_map/ppermute | solution.py:200
  344.5 7.6 %reshape.207 = bf16[320,6144]{1,0:T(8,128)(2,1)} reshape(bf16[4,8,10,6144]{3,2,1,0:T(8,128)(2,1)} %copy.195) | data formatting | bytes 7864320 | tf_op jit(solution)/shard_map/reshape | solution.py:204
  352.1 3.8 fusion.77
  357.7 12.2 %all_gather.19 = bf16[640,576]{0,1:T(8,128)(2,1)S(1)} all-gather(bf16[640,144]{0,1:T(8,128)(2,1)S(1)} %pad_maximum_fusion.7), channel_id=1, replica_groups=mesh['g'=8,'q'=4,'core'=2,'head'=4] {'head'}, dimensions={1}, use_global_device_ids=true | all-gather | bytes 921600 | tf_op jit(solution)/shard_map/all_gather | solution.py:211
  378.4 3.0 reshape.211
  381.4 2.5 fusion.6
  384.0 45.3 %all_to_all.11 = bf16[32,10,1536]{2,1,0:T(8,128)(2,1)S(1)} all-to-all(bf16[32,10,1536]{2,1,0:T(8,128)(2,1)S(1)} %bitcast.105), channel_id=1, replica_groups=mesh['g'=8,'q'=4,'core'=2,'head'=4] {'g','q'}, dimensions={0} | all-to-all | bytes 1966080 | tf_op jit(solution)/shard_map/all_to_all | solution.py:222
  430.3 2.8 fusion.3
  (161 shorter events, 48.8 us)
Async XLA Ops:
  6.5 363.3 %copy-start = (bf16[576,1536]{1,0:T(8,128)(2,1)S(1)}, bf16[576,1536]{1,0:T(8,128)(2,1)}, u32[]{:S(2)}) copy-start(bf16[576,1536]{1,0:T(8,128)(2,1)} %param.27) | copy-start | bytes 5308420
  6.5 7.0 %copy-start.19 = (f32[128,8]{0,1:T(8,128)S(1)}, f32[128,8]{0,1:T(8,128)}, u32[]{:S(2)}) copy-start(f32[128,8]{0,1:T(8,128)} %param.18) | copy-start | bytes 12292
  6.5 7.4 %copy-start.13 = (bf16[128,1024]{1,0:T(8,128)(2,1)S(1)}, bf16[128,1024]{1,0:T(8,128)(2,1)}, u32[]{:S(2)}) copy-start(bf16[128,1024]{1,0:T(8,128)(2,1)} %param.15) | copy-start | bytes 786436
  6.5 122.1 %all-gather.4.cloned.1.call-start = ((), (), s32[]{:S(2)}) async-start(), calls=%async_computation.3 | async-start | bytes 6488064 | tf_op jit(solution)/shard_map/all_gather | solution.py:135
  8.5 4.2 collective-permute-start.9
  13.5 159.5 %reduce-scatter.2.cloned.1.call-start = ((), (), s32[]{:S(2)}) async-start(), calls=%async_computation.4 | async-start | bytes 1966080 | tf_op jit(solution)/shard_map/reduce_scatter | solution.py:144
  16.3 2.2 collective-permute-start
  18.5 18.4 %copy-start.5 = (f32[8,136,128]{2,1,0:T(8,128)}, f32[8,136,128]{2,1,0:T(8,128)S(1)}, u32[]{:S(2)}) copy-start(f32[8,136,128]{2,1,0:T(8,128)S(1)} %collective-permute-done) | copy-start | bytes 1671172
  19.0 7.5 %collective-permute-start.1 = (f32[4,136,128]{2,1,0:T(8,128)S(1)}, f32[4,136,128]{2,1,0:T(8,128)S(1)}, u32[]{:S(2)}, u32[]{:S(2)}) collective-permute-start(f32[4,136,128]{2,1,0:T(8,128)S(1)} %pad_maximum_fusion.4), channel_id=1, source_target_pairs={{0,8},{8,16},{16,24},{24,32},{32,40},{40,48},{48,56},{56,64},{64,7... | collective-permute-start | bytes 835592 | tf_op jit(solution)/shard_map/ppermute | solution.py:30
  26.6 10.1 %collective-permute-start.2 = (f32[4,136,128]{2,1,0:T(8,128)S(1)}, f32[4,136,128]{2,1,0:T(8,128)S(1)}, u32[]{:S(2)}, u32[]{:S(2)}) collective-permute-start(f32[4,136,128]{2,1,0:T(8,128)S(1)} %broadcast_select_fusion.5), channel_id=1, source_target_pairs={{0,8},{8,16},{16,24},{24,32},{32,40},{40,48},{48,56},{56,64},{64,7... | collective-permute-start | bytes 835592 | tf_op jit(solution)/shard_map/ppermute | solution.py:30
  37.0 16.8 %collective-permute-start.3 = (f32[4,136,128]{2,1,0:T(8,128)S(1)}, f32[4,136,128]{2,1,0:T(8,128)S(1)}, u32[]{:S(2)}, u32[]{:S(2)}) collective-permute-start(f32[4,136,128]{2,1,0:T(8,128)S(1)} %maximum_select_fusion), channel_id=1, source_target_pairs={{0,16},{8,24},{16,32},{24,40},{32,48},{40,56},{48,64},{56,72},{64,... | collective-permute-start | bytes 835592 | tf_op jit(solution)/shard_map/ppermute | solution.py:30
  54.1 57.9 %copy-start.14 = (bf16[128,1024]{1,0:T(8,128)(2,1)S(1)}, bf16[128,1024]{1,0:T(8,128)(2,1)}, u32[]{:S(2)}) copy-start(bf16[128,1024]{1,0:T(8,128)(2,1)} %param.17) | copy-start | bytes 786436
  54.1 32.1 %collective-permute-start.4 = (f32[4,136,128]{2,1,0:T(8,128)S(1)}, f32[4,136,128]{2,1,0:T(8,128)S(1)}, u32[]{:S(2)}, u32[]{:S(2)}) collective-permute-start(f32[4,136,128]{2,1,0:T(8,128)S(1)} %maximum_select_fusion.1), channel_id=1, source_target_pairs={{0,32},{8,40},{16,48},{24,56},{32,64},{40,72},{48,80},{56,88},{64,... | collective-permute-start | bytes 835592 | tf_op jit(solution)/shard_map/ppermute | solution.py:30
  86.6 17.7 %collective-permute-start.5 = (f32[4,136,128]{2,1,0:T(8,128)S(1)}, f32[4,136,128]{2,1,0:T(8,128)S(1)}, u32[]{:S(2)}, u32[]{:S(2)}) collective-permute-start(f32[4,136,128]{2,1,0:T(8,128)S(1)} %maximum_select_fusion.2), channel_id=1, source_target_pairs={{0,64},{8,72},{16,80},{24,88},{32,96},{40,104},{48,112},{56,120},{... | collective-permute-start | bytes 835592 | tf_op jit(solution)/shard_map/ppermute | solution.py:30
  104.6 11.8 %collective-permute-start.6 = (f32[4,136,128]{2,1,0:T(8,128)S(1)}, f32[4,136,128]{2,1,0:T(8,128)S(1)}, u32[]{:S(2)}, u32[]{:S(2)}) collective-permute-start(f32[4,136,128]{2,1,0:T(8,128)S(1)} %maximum_select_fusion.3), channel_id=1, source_target_pairs={{0,128},{8,136},{16,144},{24,152},{32,160},{40,168},{48,176},{56,1... | collective-permute-start | bytes 835592 | tf_op jit(solution)/shard_map/ppermute | solution.py:30
  117.4 3.9 collective-permute-start.7
  121.1 3.8 copy-start.11
  122.4 4.1 copy-start.18
  126.7 1.8 collective-permute-start.8
  128.6 18.3 %copy-start.17 = (s32[128,2]{0,1:T(2,128)S(1)}, s32[128,2]{0,1:T(2,128)}, u32[]{:S(2)}) copy-start(s32[128,2]{0,1:T(2,128)} %param.24) | copy-start | bytes 3076
  146.8 165.9 %all-gather.6.cloned.1.call-start = ((), (), s32[]{:S(2)}) async-start(), calls=%async_computation.5 | async-start | bytes 4915200 | tf_op jit(solution)/shard_map/all_gather | solution.py:199
  174.0 2.6 collective-permute-start.10
  177.7 17.2 %copy-start.6 = (bf16[128,768]{1,0:T(8,128)(2,1)}, bf16[128,768]{1,0:T(8,128)(2,1)S(1)}, u32[]{:S(2)}) copy-start(bf16[128,768]{1,0:T(8,128)(2,1)S(1)} %get-tuple-element.22) | copy-start | bytes 589828
  177.7 17.2 %copy-start.8 = (bf16[128,768]{1,0:T(8,128)(2,1)}, bf16[128,768]{1,0:T(8,128)(2,1)S(1)}, u32[]{:S(2)}) copy-start(bf16[128,768]{1,0:T(8,128)(2,1)S(1)} %get-tuple-element.23) | copy-start | bytes 589828
  312.7 5.5 %copy-start.3 = (bf16[32,10,6144]{2,0,1:T(8,128)(2,1)S(1)}, bf16[32,10,6144]{2,0,1:T(8,128)(2,1)}, u32[]{:S(2)}) copy-start(bf16[32,10,6144]{2,0,1:T(8,128)(2,1)} %all-gather.6.cloned.1.call-done) | copy-start | bytes 11796484
  317.4 19.7 %collective-permute-start.11 = (bf16[4,8,10,6144]{3,1,2,0:T(8,128)(2,1)}, bf16[4,8,10,6144]{3,1,2,0:T(8,128)(2,1)}, u32[]{:S(2)}, u32[]{:S(2)}) collective-permute-start(bf16[4,8,10,6144]{3,1,2,0:T(8,128)(2,1)} %copy.194), channel_id=1, source_target_pairs={{0,4},{4,0},{1,5},{5,1},{2,6},{6,2},{3,7},{7,3},{8,12},{12,8},{9,1... | collective-permute-start | bytes 11796488 | tf_op jit(solution)/shard_map/ppermute | solution.py:200
  323.4 7.7 %copy-start.4 = (bf16[144,6144]{1,0:T(8,128)(2,1)S(1)}, bf16[144,6144]{1,0:T(8,128)(2,1)}, u32[]{:S(2)}) copy-start(bf16[144,6144]{1,0:T(8,128)(2,1)} %param.25) | copy-start | bytes 5308420
  331.0 3.8 copy-start.1
  331.0 3.9 copy-start.20
  352.1 3.8 copy-start.2
  352.1 3.8 copy-start.21
  376.3 5.1 %collective-permute-start.12 = (bf16[4,8,10,1536]{3,1,2,0:T(8,128)(2,1)}, bf16[4,8,10,1536]{3,1,2,0:T(8,128)(2,1)S(1)}, u32[]{:S(2)}, u32[]{:S(2)}) collective-permute-start(bf16[4,8,10,1536]{3,1,2,0:T(8,128)(2,1)} %copy.196), channel_id=1, source_target_pairs={{0,4},{4,0},{1,5},{5,1},{2,6},{6,2},{3,7},{7,3},{8,12},{12,8},{9,1... | collective-permute-start | bytes 2949128 | tf_op jit(solution)/shard_map/ppermute | solution.py:219
  (6 other events, 9.7 us)
Sparse Core Ops, SparseCore 0:
  13.6 99.2 all-gather.3
  147.0 25.9 reduce-scatter.1
  231.1 81.5 all-gather.5

commit v8 on v7

--- a/solution.py
+++ b/solution.py
@@ -195,7 +195,7 @@
         .reshape(EXP, MOST, share_width)
     )
     by_group = lax.all_to_all(packed, "g", split_axis=0, concat_axis=0, tiled=True)
-    wide = lax.all_gather(by_group, "head", axis=2, tiled=True)
+    wide = lax.all_gather(by_group.reshape(EXP * MOST, share_width), "head", axis=1, tiled=True)
     own_parity = lax.all_gather(wide, "q", axis=0, tiled=False)
     other_parity = lax.ppermute(own_parity, "core", swap)
     pairs = group // 2

time: 443 us -> 409 us (0.923)
  local copies, waits for them, and re-layouts: 46.1 us -> 14.7 us
    reshape x2 -> x1, local copies, waits for them, and re-layouts: 15.2 us -> 1.78 us  [body(): by_group.reshape(EXP * MOST, share_width)]
    all_gather x3 -> x0, local copies, waits for them, and re-layouts: 11.3 us -> none  [the longest x2 9.8 us: body(): own_parity = lax.all_gather(wide, 'q', axis=0, tiled=False)]
    ppermute x1 -> x0, local copies, waits for them, and re-layouts: 7.35 us -> none  [body(): other_parity = lax.ppermute(own_parity, 'core', swap)]
  transfers between devices with their start and end apart: 16 -> 16, of which waited for: 13 -> 14; matrix products, arithmetic and copies ran while one was open for 9% -> 6% of each run, Pallas kernels for 0% -> 0%
where the time goes in v8:
time: 409 us; the launch traced here: 406 us
  waiting for transfers between devices  165 us (40%)
  blocking collectives  103 us (25%)
  starting transfers between devices  53.8 us (13%)
  matrix products  40 us (10%)
  other arithmetic  15.7 us (4%)
  local copies, waits for them, and re-layouts  14.7 us (4%)
  between operations  13.7 us (3%)
    all_gather x1, waiting for transfers between devices, body(): own_parity = lax.all_gather(wide, 'q', axis=0, tiled=False)  82.1 us
    ppermute x6, waiting for transfers between devices, shift(): lax.ppermute(value, axis, [(i, i + distance) for i in range(count - dista...  52.6 us
    all_to_all x1, blocking collectives, body(): lax.all_to_all(outgoing, ('g', 'q'), split_axis=0, concat_axis=0, tiled=T...  45.3 us
    ppermute x6, starting transfers between devices, shift(): lax.ppermute(value, axis, [(i, i + distance) for i in range(count - dista...  42.2 us
    reduce_scatter x1, waiting for transfers between devices, body(): lax.psum_scatter(partial_sum.astype(jnp.bfloat16), 'head', scatter_dimens...  23.6 us
    all_to_all x1, blocking collectives, body(): lax.all_to_all(packed, 'g', split_axis=0, concat_axis=0, tiled=True)  20.5 us
    dot_general x1, matrix products, body(): jnp.einsum('thr,hrqd->tqd', both_mixed, row_whole, preferred_element_type...  18.2 us
    all_gather x1, blocking collectives, body(): lax.all_gather(by_group.reshape(EXP * MOST, share_width), 'head', axis=1,...  13.2 us
  transfers between devices with their start and end apart: 16, of which 14 were waited for; matrix products, arithmetic and copies ran while one was open for 6% of the time, Pallas kernels for 0%

profile of v8, /device:TPU:1, one launch (start us, length us, event | category | flops | bytes accessed | tf_op | source)
XLA Modules:
  0.0 405.8 jit_solution(14363872480596723360)
XLA Ops:
  8.5 3.3 collective-permute-start.9
  16.8 1.7 collective-permute-done
  19.0 1.9 collective-permute-start.1
  20.9 5.6 %collective-permute-done.1 = f32[4,136,128]{2,1,0:T(8,128)S(1)} collective-permute-done((f32[4,136,128]{2,1,0:T(8,128)S(1)}, f32[4,136,128]{2,1,0:T(8,128)S(1)}, u32[]{:S(2)}, u32[]{:S(2)}) %collective-permute-start.1) | collective-permute-done | bytes 278560 | tf_op jit(solution)/shard_map/ppermute | solution.py:30
  26.6 4.1 %collective-permute-start.2 = (f32[4,136,128]{2,1,0:T(8,128)S(1)}, f32[4,136,128]{2,1,0:T(8,128)S(1)}, u32[]{:S(2)}, u32[]{:S(2)}) collective-permute-start(f32[4,136,128]{2,1,0:T(8,128)S(1)} %broadcast_select_fusion.5), channel_id=1, source_target_pairs={{0,8},{8,16},{16,24},{24,32},{32,40},{40,48},{48,56},{56,64},{64,7... | collective-permute-start | bytes 835592 | tf_op jit(solution)/shard_map/ppermute | solution.py:30
  30.7 5.9 %collective-permute-done.2 = f32[4,136,128]{2,1,0:T(8,128)S(1)} collective-permute-done((f32[4,136,128]{2,1,0:T(8,128)S(1)}, f32[4,136,128]{2,1,0:T(8,128)S(1)}, u32[]{:S(2)}, u32[]{:S(2)}) %collective-permute-start.2) | collective-permute-done | bytes 278560 | tf_op jit(solution)/shard_map/ppermute | solution.py:30
  37.0 7.5 %collective-permute-start.3 = (f32[4,136,128]{2,1,0:T(8,128)S(1)}, f32[4,136,128]{2,1,0:T(8,128)S(1)}, u32[]{:S(2)}, u32[]{:S(2)}) collective-permute-start(f32[4,136,128]{2,1,0:T(8,128)S(1)} %maximum_select_fusion), channel_id=1, source_target_pairs={{0,16},{8,24},{16,32},{24,40},{32,48},{40,56},{48,64},{56,72},{64,... | collective-permute-start | bytes 835592 | tf_op jit(solution)/shard_map/ppermute | solution.py:30
  44.6 9.5 %collective-permute-done.3 = f32[4,136,128]{2,1,0:T(8,128)S(1)} collective-permute-done((f32[4,136,128]{2,1,0:T(8,128)S(1)}, f32[4,136,128]{2,1,0:T(8,128)S(1)}, u32[]{:S(2)}, u32[]{:S(2)}) %collective-permute-start.3) | collective-permute-done | bytes 278560 | tf_op jit(solution)/shard_map/ppermute | solution.py:30
  54.4 15.2 %collective-permute-start.4 = (f32[4,136,128]{2,1,0:T(8,128)S(1)}, f32[4,136,128]{2,1,0:T(8,128)S(1)}, u32[]{:S(2)}, u32[]{:S(2)}) collective-permute-start(f32[4,136,128]{2,1,0:T(8,128)S(1)} %maximum_select_fusion.1), channel_id=1, source_target_pairs={{0,32},{8,40},{16,48},{24,56},{32,64},{40,72},{48,80},{56,88},{64,... | collective-permute-start | bytes 835592 | tf_op jit(solution)/shard_map/ppermute | solution.py:30
  69.7 16.7 %collective-permute-done.4 = f32[4,136,128]{2,1,0:T(8,128)S(1)} collective-permute-done((f32[4,136,128]{2,1,0:T(8,128)S(1)}, f32[4,136,128]{2,1,0:T(8,128)S(1)}, u32[]{:S(2)}, u32[]{:S(2)}) %collective-permute-start.4) | collective-permute-done | bytes 278560 | tf_op jit(solution)/shard_map/ppermute | solution.py:30
  86.7 7.1 %collective-permute-start.5 = (f32[4,136,128]{2,1,0:T(8,128)S(1)}, f32[4,136,128]{2,1,0:T(8,128)S(1)}, u32[]{:S(2)}, u32[]{:S(2)}) collective-permute-start(f32[4,136,128]{2,1,0:T(8,128)S(1)} %maximum_select_fusion.2), channel_id=1, source_target_pairs={{0,64},{8,72},{16,80},{24,88},{32,96},{40,104},{48,112},{56,120},{... | collective-permute-start | bytes 835592 | tf_op jit(solution)/shard_map/ppermute | solution.py:30
  93.8 11.4 %collective-permute-done.5 = f32[4,136,128]{2,1,0:T(8,128)S(1)} collective-permute-done((f32[4,136,128]{2,1,0:T(8,128)S(1)}, f32[4,136,128]{2,1,0:T(8,128)S(1)}, u32[]{:S(2)}, u32[]{:S(2)}) %collective-permute-start.5) | collective-permute-done | bytes 278560 | tf_op jit(solution)/shard_map/ppermute | solution.py:30
  105.5 6.5 %collective-permute-start.6 = (f32[4,136,128]{2,1,0:T(8,128)S(1)}, f32[4,136,128]{2,1,0:T(8,128)S(1)}, u32[]{:S(2)}, u32[]{:S(2)}) collective-permute-start(f32[4,136,128]{2,1,0:T(8,128)S(1)} %maximum_select_fusion.3), channel_id=1, source_target_pairs={{0,128},{8,136},{16,144},{24,152},{32,160},{40,168},{48,176},{56,1... | collective-permute-start | bytes 835592 | tf_op jit(solution)/shard_map/ppermute | solution.py:30
  113.0 3.5 collective-permute-done.6
  117.5 2.4 collective-permute-start.7
  122.5 2.5 fusion.9
  128.7 18.2 %bitcast_convert_fusion = bf16[256,4,768]{2,0,1:T(8,128)(2,1)} fusion(bf16[8,128,4,768]{3,0,2,1:T(8,128)(2,1)} %all-gather.4.cloned.1.call-done, bf16[128,8,128]{2,0,1:T(8,128)(2,1)S(1)} %get-tuple-element.25, bf16[128,8,128]{2,0,1:T(8,128)(2,1)S(1)} %get-tuple-element.24), kind=kOutput, calls=%fused_computation.4 | convolution fusion | flops 1612447744 | bytes 8388608 | tf_op jit(solution)/shard_map/thr,hrqd->tqd/dot_general | solution.py:141
  149.3 23.6 %reduce-scatter.2.cloned.1.call-done = bf16[256,1,768]{2,0,1:T(8,128)(2,1)} async-done(((bf16[256,4,768]{2,0,1:T(8,128)(2,1)}), bf16[256,1,768]{2,0,1:T(8,128)(2,1)}) %reduce-scatter.2.cloned.1.call-update) | async-done | bytes 393232 | tf_op jit(solution)/shard_map/reduce_scatter | solution.py:144
  180.8 12.0 %psum.7 = f32[128,33]{0,1:T(8,128)S(1)} all-reduce(f32[128,33]{0,1:T(8,128)S(1)} %pad_maximum_fusion.8), channel_id=1, replica_groups=mesh['g'=8,'q'=4,'core'=2,'head'=4] {'head'}, use_global_device_ids=true, to_apply=%region_7.8 | all-reduce | flops 4224 | bytes 33792 | tf_op jit(solution)/shard_map/psum | solution.py:164
  195.7 20.5 %all_to_all.10 = bf16[8,10,1536]{2,1,0:T(8,128)(2,1)} all-to-all(bf16[8,10,1536]{2,1,0:T(8,128)(2,1)} %reshape.208), channel_id=1, replica_groups=mesh['g'=8,'q'=4,'core'=2,'head'=4] {'g'}, dimensions={0} | all-to-all | bytes 491520 | tf_op jit(solution)/shard_map/all_to_all | solution.py:197
  216.1 1.8 reshape.209
  217.9 13.2 %all_gather.16 = bf16[80,6144]{1,0:T(8,128)(2,1)} all-gather(bf16[80,1536]{1,0:T(8,128)(2,1)} %reshape.209), channel_id=1, replica_groups=mesh['g'=8,'q'=4,'core'=2,'head'=4] {'head'}, dimensions={1}, use_global_device_ids=true | all-gather | bytes 1228800 | tf_op jit(solution)/shard_map/all_gather | solution.py:198
  231.2 82.1 %all-gather.6.cloned.1.call-done = bf16[320,6144]{1,0:T(8,128)(2,1)} async-done(((bf16[80,6144]{1,0:T(8,128)(2,1)}), bf16[320,6144]{1,0:T(8,128)(2,1)}) %all-gather.6.cloned.1.call-update) | async-done | bytes 3932176 | tf_op jit(solution)/shard_map/all_gather | solution.py:199
  314.1 4.1 %fusion.76 = f32[320,144]{0,1:T(8,128)S(1)} fusion(bf16[320,6144]{1,0:T(8,128)(2,1)} %all-gather.6.cloned.1.call-done, bf16[144,6144]{1,0:T(8,128)(2,1)S(1)} %copy-done.1), kind=kOutput, calls=%fused_computation.163 | convolution fusion | flops 566231040 | bytes 5885952 | tf_op jit(solution)/shard_map/rd,fd->rf/dot_general | solution.py:205
  324.1 11.7 %all_gather.19 = bf16[640,576]{0,1:T(8,128)(2,1)S(1)} all-gather(bf16[640,144]{0,1:T(8,128)(2,1)S(1)} %pad_maximum_fusion.7), channel_id=1, replica_groups=mesh['g'=8,'q'=4,'core'=2,'head'=4] {'head'}, dimensions={1}, use_global_device_ids=true | all-gather | bytes 921600 | tf_op jit(solution)/shard_map/all_gather | solution.py:211
  335.8 1.7 convolution_convert_fusion
  337.5 1.8 fusion.71
  342.2 2.3 collective-permute-start.12
  344.6 3.0 reshape.215
  347.6 2.5 fusion.6
  350.2 45.3 %all_to_all.11 = bf16[32,10,1536]{2,1,0:T(8,128)(2,1)S(1)} all-to-all(bf16[32,10,1536]{2,1,0:T(8,128)(2,1)S(1)} %bitcast.105), channel_id=1, replica_groups=mesh['g'=8,'q'=4,'core'=2,'head'=4] {'g','q'}, dimensions={0} | all-to-all | bytes 1966080 | tf_op jit(solution)/shard_map/all_to_all | solution.py:222
  396.5 2.8 fusion.3
  (150 shorter events, 40.9 us)
Async XLA Ops:
  6.5 329.3 %copy-start = (bf16[576,1536]{1,0:T(8,128)(2,1)S(1)}, bf16[576,1536]{1,0:T(8,128)(2,1)}, u32[]{:S(2)}) copy-start(bf16[576,1536]{1,0:T(8,128)(2,1)} %param.27) | copy-start | bytes 5308420
  6.5 7.0 %copy-start.17 = (f32[128,8]{0,1:T(8,128)S(1)}, f32[128,8]{0,1:T(8,128)}, u32[]{:S(2)}) copy-start(f32[128,8]{0,1:T(8,128)} %param.18) | copy-start | bytes 12292
  6.5 122.1 %all-gather.4.cloned.1.call-start = ((), (), s32[]{:S(2)}) async-start(), calls=%async_computation.3 | async-start | bytes 6488064 | tf_op jit(solution)/shard_map/all_gather | solution.py:135
  7.7 6.2 %copy-start.12 = (bf16[128,1024]{1,0:T(8,128)(2,1)S(1)}, bf16[128,1024]{1,0:T(8,128)(2,1)}, u32[]{:S(2)}) copy-start(bf16[128,1024]{1,0:T(8,128)(2,1)} %param.15) | copy-start | bytes 786436
  8.5 4.2 %collective-permute-start.9 = (bf16[8,2,4,768]{3,0,2,1:T(8,128)(2,1)S(1)}, bf16[8,2,4,768]{3,0,2,1:T(8,128)(2,1)S(1)}, u32[]{:S(2)}, u32[]{:S(2)}) collective-permute-start(bf16[8,2,4,768]{3,0,2,1:T(8,128)(2,1)S(1)} %bitcast.113), channel_id=1, source_target_pairs={{0,4},{4,0},{1,5},{5,1},{2,6},{6,2},{3,7},{7,3},{8,12},{12,8},{9,1... | collective-permute-start | bytes 294920 | tf_op jit(solution)/shard_map/ppermute | solution.py:131
  13.5 159.5 %reduce-scatter.2.cloned.1.call-start = ((), (), s32[]{:S(2)}) async-start(), calls=%async_computation.4 | async-start | bytes 1966080 | tf_op jit(solution)/shard_map/reduce_scatter | solution.py:144
  14.1 1.4 copy-start.9
  16.3 2.2 collective-permute-start
  18.5 18.3 %copy-start.3 = (f32[8,136,128]{2,1,0:T(8,128)}, f32[8,136,128]{2,1,0:T(8,128)S(1)}, u32[]{:S(2)}) copy-start(f32[8,136,128]{2,1,0:T(8,128)S(1)} %collective-permute-done) | copy-start | bytes 1671172
  19.0 7.5 %collective-permute-start.1 = (f32[4,136,128]{2,1,0:T(8,128)S(1)}, f32[4,136,128]{2,1,0:T(8,128)S(1)}, u32[]{:S(2)}, u32[]{:S(2)}) collective-permute-start(f32[4,136,128]{2,1,0:T(8,128)S(1)} %pad_maximum_fusion.4), channel_id=1, source_target_pairs={{0,8},{8,16},{16,24},{24,32},{32,40},{40,48},{48,56},{56,64},{64,7... | collective-permute-start | bytes 835592 | tf_op jit(solution)/shard_map/ppermute | solution.py:30
  26.6 10.1 %collective-permute-start.2 = (f32[4,136,128]{2,1,0:T(8,128)S(1)}, f32[4,136,128]{2,1,0:T(8,128)S(1)}, u32[]{:S(2)}, u32[]{:S(2)}) collective-permute-start(f32[4,136,128]{2,1,0:T(8,128)S(1)} %broadcast_select_fusion.5), channel_id=1, source_target_pairs={{0,8},{8,16},{16,24},{24,32},{32,40},{40,48},{48,56},{56,64},{64,7... | collective-permute-start | bytes 835592 | tf_op jit(solution)/shard_map/ppermute | solution.py:30
  37.0 17.1 %collective-permute-start.3 = (f32[4,136,128]{2,1,0:T(8,128)S(1)}, f32[4,136,128]{2,1,0:T(8,128)S(1)}, u32[]{:S(2)}, u32[]{:S(2)}) collective-permute-start(f32[4,136,128]{2,1,0:T(8,128)S(1)} %maximum_select_fusion), channel_id=1, source_target_pairs={{0,16},{8,24},{16,32},{24,40},{32,48},{40,56},{48,64},{56,72},{64,... | collective-permute-start | bytes 835592 | tf_op jit(solution)/shard_map/ppermute | solution.py:30
  54.4 57.7 %copy-start.13 = (bf16[128,1024]{1,0:T(8,128)(2,1)S(1)}, bf16[128,1024]{1,0:T(8,128)(2,1)}, u32[]{:S(2)}) copy-start(bf16[128,1024]{1,0:T(8,128)(2,1)} %param.17) | copy-start | bytes 786436
  54.4 31.9 %collective-permute-start.4 = (f32[4,136,128]{2,1,0:T(8,128)S(1)}, f32[4,136,128]{2,1,0:T(8,128)S(1)}, u32[]{:S(2)}, u32[]{:S(2)}) collective-permute-start(f32[4,136,128]{2,1,0:T(8,128)S(1)} %maximum_select_fusion.1), channel_id=1, source_target_pairs={{0,32},{8,40},{16,48},{24,56},{32,64},{40,72},{48,80},{56,88},{64,... | collective-permute-start | bytes 835592 | tf_op jit(solution)/shard_map/ppermute | solution.py:30
  86.7 18.4 %collective-permute-start.5 = (f32[4,136,128]{2,1,0:T(8,128)S(1)}, f32[4,136,128]{2,1,0:T(8,128)S(1)}, u32[]{:S(2)}, u32[]{:S(2)}) collective-permute-start(f32[4,136,128]{2,1,0:T(8,128)S(1)} %maximum_select_fusion.2), channel_id=1, source_target_pairs={{0,64},{8,72},{16,80},{24,88},{32,96},{40,104},{48,112},{56,120},{... | collective-permute-start | bytes 835592 | tf_op jit(solution)/shard_map/ppermute | solution.py:30
  105.5 10.9 %collective-permute-start.6 = (f32[4,136,128]{2,1,0:T(8,128)S(1)}, f32[4,136,128]{2,1,0:T(8,128)S(1)}, u32[]{:S(2)}, u32[]{:S(2)}) collective-permute-start(f32[4,136,128]{2,1,0:T(8,128)S(1)} %maximum_select_fusion.3), channel_id=1, source_target_pairs={{0,128},{8,136},{16,144},{24,152},{32,160},{40,168},{48,176},{56,1... | collective-permute-start | bytes 835592 | tf_op jit(solution)/shard_map/ppermute | solution.py:30
  113.0 6.9 %copy-start.8 = (bf16[128,1024]{0,1:T(8,128)(2,1)S(1)}, bf16[128,1024]{0,1:T(8,128)(2,1)}, u32[]{:S(2)}) copy-start(bf16[128,1024]{0,1:T(8,128)(2,1)} %copy.170) | copy-start | bytes 786436
  117.5 3.9 collective-permute-start.7
  120.2 4.7 %copy-start.10 = (bf16[128,1024]{0,1:T(8,128)(2,1)S(1)}, bf16[128,1024]{0,1:T(8,128)(2,1)}, u32[]{:S(2)}) copy-start(bf16[128,1024]{0,1:T(8,128)(2,1)} %copy-done.9) | copy-start | bytes 786436
  120.2 4.7 %copy-start.11 = (bf16[128,1024]{1,0:T(8,128)(2,1)S(1)}, bf16[128,1024]{1,0:T(8,128)(2,1)}, u32[]{:S(2)}) copy-start(bf16[128,1024]{1,0:T(8,128)(2,1)} %param.14) | copy-start | bytes 786436
  122.4 4.1 %copy-start.16 = (f32[1024]{0:T(1024)S(1)}, f32[1024]{0:T(1024)}, u32[]{:S(2)}) copy-start(f32[1024]{0:T(1024)} %param.19) | copy-start | bytes 12292
  126.8 1.8 collective-permute-start.8
  128.7 18.3 %copy-start.15 = (s32[128,2]{0,1:T(2,128)S(1)}, s32[128,2]{0,1:T(2,128)}, u32[]{:S(2)}) copy-start(s32[128,2]{0,1:T(2,128)} %param.24) | copy-start | bytes 3076
  146.9 166.4 %all-gather.6.cloned.1.call-start = ((), (), s32[]{:S(2)}) async-start(), calls=%async_computation.5 | async-start | bytes 4915200 | tf_op jit(solution)/shard_map/all_gather | solution.py:199
  174.0 2.7 collective-permute-start.10
  177.8 17.1 %copy-start.4 = (bf16[128,768]{1,0:T(8,128)(2,1)}, bf16[128,768]{1,0:T(8,128)(2,1)S(1)}, u32[]{:S(2)}) copy-start(bf16[128,768]{1,0:T(8,128)(2,1)S(1)} %get-tuple-element.22) | copy-start | bytes 589828
  177.8 17.1 %copy-start.6 = (bf16[128,768]{1,0:T(8,128)(2,1)}, bf16[128,768]{1,0:T(8,128)(2,1)S(1)}, u32[]{:S(2)}) copy-start(bf16[128,768]{1,0:T(8,128)(2,1)S(1)} %get-tuple-element.23) | copy-start | bytes 589828
  195.7 118.4 %copy-start.1 = (bf16[144,6144]{1,0:T(8,128)(2,1)S(1)}, bf16[144,6144]{1,0:T(8,128)(2,1)}, u32[]{:S(2)}) copy-start(bf16[144,6144]{1,0:T(8,128)(2,1)} %param.25) | copy-start | bytes 5308420
  313.3 4.9 %copy-start.2 = (bf16[320,6144]{1,0:T(8,128)(2,1)S(1)}, bf16[320,6144]{1,0:T(8,128)(2,1)}, u32[]{:S(2)}) copy-start(bf16[320,6144]{1,0:T(8,128)(2,1)} %all-gather.6.cloned.1.call-done) | copy-start | bytes 11796484
  313.3 5.0 %copy-start.18 = (bf16[144,6144]{1,0:T(8,128)(2,1)S(1)}, bf16[144,6144]{1,0:T(8,128)(2,1)}, u32[]{:S(2)}) copy-start(bf16[144,6144]{1,0:T(8,128)(2,1)} %param.26) | copy-start | bytes 5308420
  313.3 7.5 %collective-permute-start.11 = (bf16[4,80,6144]{2,1,0:T(8,128)(2,1)}, bf16[4,80,6144]{2,1,0:T(8,128)(2,1)S(1)}, u32[]{:S(2)}, u32[]{:S(2)}) collective-permute-start(bf16[4,80,6144]{2,1,0:T(8,128)(2,1)} %bitcast.106), channel_id=1, source_target_pairs={{0,4},{4,0},{1,5},{5,1},{2,6},{6,2},{3,7},{7,3},{8,12},{12,8},{9,1... | collective-permute-start | bytes 11796488 | tf_op jit(solution)/shard_map/ppermute | solution.py:200
  342.2 5.4 %collective-permute-start.12 = (bf16[4,8,10,1536]{3,1,2,0:T(8,128)(2,1)}, bf16[4,8,10,1536]{3,1,2,0:T(8,128)(2,1)S(1)}, u32[]{:S(2)}, u32[]{:S(2)}) collective-permute-start(bf16[4,8,10,1536]{3,1,2,0:T(8,128)(2,1)} %copy.180), channel_id=1, source_target_pairs={{0,4},{4,0},{1,5},{5,1},{2,6},{6,2},{3,7},{7,3},{8,12},{12,8},{9,1... | collective-permute-start | bytes 2949128 | tf_op jit(solution)/shard_map/ppermute | solution.py:219
  (3 other events, 3.0 us)
Sparse Core Ops, SparseCore 0:
  13.6 98.8 all-gather.3
  147.0 25.9 reduce-scatter.1
  231.3 81.9 all-gather.5

commit v9 on v8

--- a/solution.py
+++ b/solution.py
@@ -196,7 +196,14 @@
     )
     by_group = lax.all_to_all(packed, "g", split_axis=0, concat_axis=0, tiled=True)
     wide = lax.all_gather(by_group.reshape(EXP * MOST, share_width), "head", axis=1, tiled=True)
-    own_parity = lax.all_gather(wide, "q", axis=0, tiled=False)
+    q_count = lax.axis_size("q")
+    q_place = lax.axis_index("q")
+    shifted = [wide] + [
+        lax.ppermute(wide, "q", [(i, (i + s) % q_count) for i in range(q_count)])
+        for s in range(1, q_count)
+    ]
+    order = (q_place - jnp.arange(q_count)) % q_count
+    own_parity = jnp.take(jnp.stack(shifted), order, axis=0)
     other_parity = lax.ppermute(own_parity, "core", swap)
     pairs = group // 2
     halves = []

time: 409 us -> 423 us (1.034)
  waiting for transfers between devices: 165 us -> 144 us
  blocking collectives: 103 us -> 117 us
  other arithmetic: 15.7 us -> 25.9 us
  starting transfers between devices: 53.8 us -> 60.2 us
    all_gather x1 -> x0, waiting for transfers between devices: 82.1 us -> none  [body(): own_parity = lax.all_gather(wide, 'q', axis=0, tiled=False)]
    ppermute x0 -> x3, waiting for transfers between devices: none -> 62.7 us  [body(): lax.ppermute(wide, 'q', [(i, (i + s) % q_count) for i in range(q_count)])]
    all_to_all x1, blocking collectives: 45.3 us -> 61.7 us  [body(): lax.all_to_all(outgoing, ('g', 'q'), split_axis=0, concat_axis=0, tiled=T...]
    select_n x0 -> x3, other arithmetic: none -> 7.14 us  [body(): own_parity = jnp.take(jnp.stack(shifted), order, axis=0)]
    ppermute x0 -> x3, starting transfers between devices: none -> 4.88 us  [body(): lax.ppermute(wide, 'q', [(i, (i + s) % q_count) for i in range(q_count)])]
    gather x0 -> x1, local copies, waits for them, and re-layouts: none -> 4.79 us  [body(): own_parity = jnp.take(jnp.stack(shifted), order, axis=0)]
  transfers between devices with their start and end apart: 16 -> 18, of which waited for: 14 -> 15; matrix products, arithmetic and copies ran while one was open for 6% -> 6% of each run, Pallas kernels for 0% -> 0%
where the time goes in v9:
time: 423 us; the launch traced here: 419 us
  waiting for transfers between devices  144 us (34%)
  blocking collectives  117 us (28%)
  starting transfers between devices  60.2 us (14%)
  matrix products  41.6 us (10%)
  other arithmetic  25.9 us (6%)
  local copies, waits for them, and re-layouts  16.5 us (4%)
  between operations  14.1 us (3%)
    ppermute x3, waiting for transfers between devices, body(): lax.ppermute(wide, 'q', [(i, (i + s) % q_count) for i in range(q_count)])  62.7 us
    all_to_all x1, blocking collectives, body(): lax.all_to_all(outgoing, ('g', 'q'), split_axis=0, concat_axis=0, tiled=T...  61.7 us
    ppermute x6, waiting for transfers between devices, shift(): lax.ppermute(value, axis, [(i, i + distance) for i in range(count - dista...  51.9 us
    ppermute x6, starting transfers between devices, shift(): lax.ppermute(value, axis, [(i, i + distance) for i in range(count - dista...  42.8 us
    reduce_scatter x1, waiting for transfers between devices, body(): lax.psum_scatter(partial_sum.astype(jnp.bfloat16), 'head', scatter_dimens...  23.7 us
    all_to_all x1, blocking collectives, body(): lax.all_to_all(packed, 'g', split_axis=0, concat_axis=0, tiled=True)  20 us
    dot_general x1, matrix products, body(): jnp.einsum('thr,hrqd->tqd', both_mixed, row_whole, preferred_element_type...  18.2 us
    all_gather x1, blocking collectives, body(): lax.all_gather(by_group.reshape(EXP * MOST, share_width), 'head', axis=1,...  12.2 us
  transfers between devices with their start and end apart: 18, of which 15 were waited for; matrix products, arithmetic and copies ran while one was open for 6% of the time, Pallas kernels for 0%

profile of v9, /device:TPU:1, one launch (start us, length us, event | category | flops | bytes accessed | tf_op | source)
XLA Modules:
  0.0 419.2 jit_solution(910877798898436175)
XLA Ops:
  8.5 3.3 collective-permute-start.9
  20.9 5.6 %collective-permute-done.1 = f32[4,136,128]{2,1,0:T(8,128)S(1)} collective-permute-done((f32[4,136,128]{2,1,0:T(8,128)S(1)}, f32[4,136,128]{2,1,0:T(8,128)S(1)}, u32[]{:S(2)}, u32[]{:S(2)}) %collective-permute-start.1) | collective-permute-done | bytes 278560 | tf_op jit(solution)/shard_map/ppermute | solution.py:30
  26.6 4.1 collective-permute-start.2
  30.7 5.9 %collective-permute-done.2 = f32[4,136,128]{2,1,0:T(8,128)S(1)} collective-permute-done((f32[4,136,128]{2,1,0:T(8,128)S(1)}, f32[4,136,128]{2,1,0:T(8,128)S(1)}, u32[]{:S(2)}, u32[]{:S(2)}) %collective-permute-start.2) | collective-permute-done | bytes 278560 | tf_op jit(solution)/shard_map/ppermute | solution.py:30
  37.0 7.6 %collective-permute-start.3 = (f32[4,136,128]{2,1,0:T(8,128)S(1)}, f32[4,136,128]{2,1,0:T(8,128)S(1)}, u32[]{:S(2)}, u32[]{:S(2)}) collective-permute-start(f32[4,136,128]{2,1,0:T(8,128)S(1)} %maximum_select_fusion), channel_id=1, source_target_pairs={{0,16},{8,24},{16,32},{24,40},{32,48},{40,56},{48,64},{56,72},{64,... | collective-permute-start | bytes 835592 | tf_op jit(solution)/shard_map/ppermute | solution.py:30
  44.6 9.2 %collective-permute-done.3 = f32[4,136,128]{2,1,0:T(8,128)S(1)} collective-permute-done((f32[4,136,128]{2,1,0:T(8,128)S(1)}, f32[4,136,128]{2,1,0:T(8,128)S(1)}, u32[]{:S(2)}, u32[]{:S(2)}) %collective-permute-start.3) | collective-permute-done | bytes 278560 | tf_op jit(solution)/shard_map/ppermute | solution.py:30
  54.2 15.4 %collective-permute-start.4 = (f32[4,136,128]{2,1,0:T(8,128)S(1)}, f32[4,136,128]{2,1,0:T(8,128)S(1)}, u32[]{:S(2)}, u32[]{:S(2)}) collective-permute-start(f32[4,136,128]{2,1,0:T(8,128)S(1)} %maximum_select_fusion.1), channel_id=1, source_target_pairs={{0,32},{8,40},{16,48},{24,56},{32,64},{40,72},{48,80},{56,88},{64,... | collective-permute-start | bytes 835592 | tf_op jit(solution)/shard_map/ppermute | solution.py:30
  69.5 16.7 %collective-permute-done.4 = f32[4,136,128]{2,1,0:T(8,128)S(1)} collective-permute-done((f32[4,136,128]{2,1,0:T(8,128)S(1)}, f32[4,136,128]{2,1,0:T(8,128)S(1)}, u32[]{:S(2)}, u32[]{:S(2)}) %collective-permute-start.4) | collective-permute-done | bytes 278560 | tf_op jit(solution)/shard_map/ppermute | solution.py:30
  86.5 6.0 %collective-permute-start.5 = (f32[4,136,128]{2,1,0:T(8,128)S(1)}, f32[4,136,128]{2,1,0:T(8,128)S(1)}, u32[]{:S(2)}, u32[]{:S(2)}) collective-permute-start(f32[4,136,128]{2,1,0:T(8,128)S(1)} %maximum_select_fusion.2), channel_id=1, source_target_pairs={{0,64},{8,72},{16,80},{24,88},{32,96},{40,104},{48,112},{56,120},{... | collective-permute-start | bytes 835592 | tf_op jit(solution)/shard_map/ppermute | solution.py:30
  92.5 11.1 %collective-permute-done.5 = f32[4,136,128]{2,1,0:T(8,128)S(1)} collective-permute-done((f32[4,136,128]{2,1,0:T(8,128)S(1)}, f32[4,136,128]{2,1,0:T(8,128)S(1)}, u32[]{:S(2)}, u32[]{:S(2)}) %collective-permute-start.5) | collective-permute-done | bytes 278560 | tf_op jit(solution)/shard_map/ppermute | solution.py:30
  104.0 7.9 %collective-permute-start.6 = (f32[4,136,128]{2,1,0:T(8,128)S(1)}, f32[4,136,128]{2,1,0:T(8,128)S(1)}, u32[]{:S(2)}, u32[]{:S(2)}) collective-permute-start(f32[4,136,128]{2,1,0:T(8,128)S(1)} %maximum_select_fusion.3), channel_id=1, source_target_pairs={{0,128},{8,136},{16,144},{24,152},{32,160},{40,168},{48,176},{56,1... | collective-permute-start | bytes 835592 | tf_op jit(solution)/shard_map/ppermute | solution.py:30
  112.9 3.4 collective-permute-done.6
  122.4 2.5 fusion.9
  128.6 18.2 %bitcast_convert_fusion = bf16[256,4,768]{2,0,1:T(8,128)(2,1)} fusion(bf16[8,128,4,768]{3,0,2,1:T(8,128)(2,1)} %all-gather.2.cloned.1.call-done, bf16[128,8,128]{2,0,1:T(8,128)(2,1)S(1)} %get-tuple-element.25, bf16[128,8,128]{2,0,1:T(8,128)(2,1)S(1)} %get-tuple-element.24), kind=kOutput, calls=%fused_computation.8 | convolution fusion | flops 1612447744 | bytes 8388608 | tf_op jit(solution)/shard_map/thr,hrqd->tqd/dot_general | solution.py:141
  149.2 23.7 %reduce-scatter.2.cloned.1.call-done = bf16[256,1,768]{2,0,1:T(8,128)(2,1)} async-done(((bf16[256,4,768]{2,0,1:T(8,128)(2,1)}), bf16[256,1,768]{2,0,1:T(8,128)(2,1)}) %reduce-scatter.2.cloned.1.call-update) | async-done | bytes 393232 | tf_op jit(solution)/shard_map/reduce_scatter | solution.py:144
  180.6 12.0 %psum.7 = f32[128,33]{0,1:T(8,128)S(1)} all-reduce(f32[128,33]{0,1:T(8,128)S(1)} %pad_maximum_fusion.9), channel_id=1, replica_groups=mesh['g'=8,'q'=4,'core'=2,'head'=4] {'head'}, use_global_device_ids=true, to_apply=%region_7.8 | all-reduce | flops 4224 | bytes 33792 | tf_op jit(solution)/shard_map/psum | solution.py:164
  194.8 20.0 %all_to_all.10 = bf16[8,10,1536]{2,1,0:T(8,128)(2,1)S(1)} all-to-all(bf16[8,10,1536]{2,1,0:T(8,128)(2,1)S(1)} %reshape.262), channel_id=1, replica_groups=mesh['g'=8,'q'=4,'core'=2,'head'=4] {'g'}, dimensions={0} | all-to-all | bytes 491520 | tf_op jit(solution)/shard_map/all_to_all | solution.py:197
  214.9 12.2 %all_gather.10 = bf16[80,6144]{1,0:T(8,128)(2,1)S(1)} all-gather(bf16[80,1536]{1,0:T(8,128)(2,1)S(1)} %reshape.263), channel_id=1, replica_groups=mesh['g'=8,'q'=4,'core'=2,'head'=4] {'head'}, dimensions={1}, use_global_device_ids=true | all-gather | bytes 1228800 | tf_op jit(solution)/shard_map/all_gather | solution.py:198
  227.2 2.4 collective-permute-start.11
  232.1 12.5 %collective-permute-done.11 = bf16[80,6144]{1,0:T(8,128)(2,1)S(1)} collective-permute-done((bf16[80,6144]{1,0:T(8,128)(2,1)S(1)}, bf16[80,6144]{1,0:T(8,128)(2,1)S(1)}, u32[]{:S(2)}, u32[]{:S(2)}) %collective-permute-start.11) | collective-permute-done | bytes 983072 | tf_op jit(solution)/shard_map/ppermute | solution.py:202
  244.6 50.2 %collective-permute-done.12 = bf16[80,6144]{1,0:T(8,128)(2,1)S(1)} collective-permute-done((bf16[80,6144]{1,0:T(8,128)(2,1)S(1)}, bf16[80,6144]{1,0:T(8,128)(2,1)S(1)}, u32[]{:S(2)}, u32[]{:S(2)}) %collective-permute-start.12) | collective-permute-done | bytes 983072 | tf_op jit(solution)/shard_map/ppermute | solution.py:202
  296.9 4.8 %gather_fusion = bf16[4,80,6144]{2,1,0:T(8,128)(2,1)} fusion(bf16[4,80,6144]{2,1,0:T(8,128)(2,1)} %pad_maximum_fusion, s32[1024]{0:T(1024)S(1)} %pad_clamp_fusion), kind=kCustom, calls=%fused_computation | custom fusion | bytes 7864336 | tf_op jit(solution)/shard_map/jit(_take)/gather | solution.py:206
  301.7 4.4 %broadcast_select_fusion = bf16[4,80,6144]{2,1,0:T(8,128)(2,1)} fusion(bf16[4,80,6144]{2,1,0:T(8,128)(2,1)} %gather_fusion, pred[4]{0:T(512)(128)(4,1)S(1)} %compare_and_fusion), kind=kLoop, calls=%fused_computation.5 | loop fusion | flops 1966080 | bytes 7864324 | tf_op jit(solution)/shard_map/jit(_take)/select_n | solution.py:206
  306.9 2.7 bitcast_select_fusion
  313.5 3.7 fusion.80
  317.2 3.7 multiply_convert_fusion.5
  321.0 10.8 %all_gather.11 = bf16[640,576]{0,1:T(8,128)(2,1)S(1)} all-gather(bf16[640,144]{0,1:T(8,128)(2,1)S(1)} %pad_maximum_fusion.8), channel_id=1, replica_groups=mesh['g'=8,'q'=4,'core'=2,'head'=4] {'head'}, dimensions={1}, use_global_device_ids=true | all-gather | bytes 921600 | tf_op jit(solution)/shard_map/all_gather | solution.py:218
  338.2 3.6 collective-permute-start.15
  341.9 3.0 reshape.268
  344.9 2.5 fusion.6
  347.5 61.7 %all_to_all.11 = bf16[32,10,1536]{2,1,0:T(8,128)(2,1)S(1)} all-to-all(bf16[32,10,1536]{2,1,0:T(8,128)(2,1)S(1)} %bitcast.112), channel_id=1, replica_groups=mesh['g'=8,'q'=4,'core'=2,'head'=4] {'g','q'}, dimensions={0} | all-to-all | bytes 1966080 | tf_op jit(solution)/shard_map/all_to_all | solution.py:229
  409.5 2.8 fusion.3
  (154 shorter events, 51.4 us)
Async XLA Ops:
  6.5 325.3 %copy-start = (bf16[576,1536]{1,0:T(8,128)(2,1)S(1)}, bf16[576,1536]{1,0:T(8,128)(2,1)}, u32[]{:S(2)}) copy-start(bf16[576,1536]{1,0:T(8,128)(2,1)} %param.27) | copy-start | bytes 5308420
  6.5 7.0 %copy-start.13 = (f32[128,8]{0,1:T(8,128)S(1)}, f32[128,8]{0,1:T(8,128)}, u32[]{:S(2)}) copy-start(f32[128,8]{0,1:T(8,128)} %param.18) | copy-start | bytes 12292
  6.5 7.4 %copy-start.8 = (bf16[128,1024]{1,0:T(8,128)(2,1)S(1)}, bf16[128,1024]{1,0:T(8,128)(2,1)}, u32[]{:S(2)}) copy-start(bf16[128,1024]{1,0:T(8,128)(2,1)} %param.15) | copy-start | bytes 786436
  6.5 122.1 %all-gather.2.cloned.1.call-start = ((), (), s32[]{:S(2)}) async-start(), calls=%async_computation.3 | async-start | bytes 6488064 | tf_op jit(solution)/shard_map/all_gather | solution.py:135
  8.5 4.2 %collective-permute-start.9 = (bf16[8,2,4,768]{3,0,2,1:T(8,128)(2,1)S(1)}, bf16[8,2,4,768]{3,0,2,1:T(8,128)(2,1)S(1)}, u32[]{:S(2)}, u32[]{:S(2)}) collective-permute-start(bf16[8,2,4,768]{3,0,2,1:T(8,128)(2,1)S(1)} %bitcast.121), channel_id=1, source_target_pairs={{0,4},{4,0},{1,5},{5,1},{2,6},{6,2},{3,7},{7,3},{8,12},{12,8},{9,1... | collective-permute-start | bytes 294920 | tf_op jit(solution)/shard_map/ppermute | solution.py:131
  13.5 159.5 %reduce-scatter.2.cloned.1.call-start = ((), (), s32[]{:S(2)}) async-start(), calls=%async_computation.4 | async-start | bytes 1966080 | tf_op jit(solution)/shard_map/reduce_scatter | solution.py:144
  16.3 2.2 collective-permute-start
  18.5 18.4 %copy-start.2 = (f32[8,136,128]{2,1,0:T(8,128)}, f32[8,136,128]{2,1,0:T(8,128)S(1)}, u32[]{:S(2)}) copy-start(f32[8,136,128]{2,1,0:T(8,128)S(1)} %collective-permute-done) | copy-start | bytes 1671172
  19.0 7.5 %collective-permute-start.1 = (f32[4,136,128]{2,1,0:T(8,128)S(1)}, f32[4,136,128]{2,1,0:T(8,128)S(1)}, u32[]{:S(2)}, u32[]{:S(2)}) collective-permute-start(f32[4,136,128]{2,1,0:T(8,128)S(1)} %pad_maximum_fusion.5), channel_id=1, source_target_pairs={{0,8},{8,16},{16,24},{24,32},{32,40},{40,48},{48,56},{56,64},{64,7... | collective-permute-start | bytes 835592 | tf_op jit(solution)/shard_map/ppermute | solution.py:30
  26.6 10.1 %collective-permute-start.2 = (f32[4,136,128]{2,1,0:T(8,128)S(1)}, f32[4,136,128]{2,1,0:T(8,128)S(1)}, u32[]{:S(2)}, u32[]{:S(2)}) collective-permute-start(f32[4,136,128]{2,1,0:T(8,128)S(1)} %broadcast_select_fusion.6), channel_id=1, source_target_pairs={{0,8},{8,16},{16,24},{24,32},{32,40},{40,48},{48,56},{56,64},{64,7... | collective-permute-start | bytes 835592 | tf_op jit(solution)/shard_map/ppermute | solution.py:30
  36.8 75.2 %copy-start.9 = (bf16[128,1024]{1,0:T(8,128)(2,1)S(1)}, bf16[128,1024]{1,0:T(8,128)(2,1)}, u32[]{:S(2)}) copy-start(bf16[128,1024]{1,0:T(8,128)(2,1)} %param.17) | copy-start | bytes 786436
  37.0 16.8 %collective-permute-start.3 = (f32[4,136,128]{2,1,0:T(8,128)S(1)}, f32[4,136,128]{2,1,0:T(8,128)S(1)}, u32[]{:S(2)}, u32[]{:S(2)}) collective-permute-start(f32[4,136,128]{2,1,0:T(8,128)S(1)} %maximum_select_fusion), channel_id=1, source_target_pairs={{0,16},{8,24},{16,32},{24,40},{32,48},{40,56},{48,64},{56,72},{64,... | collective-permute-start | bytes 835592 | tf_op jit(solution)/shard_map/ppermute | solution.py:30
  54.2 32.1 %collective-permute-start.4 = (f32[4,136,128]{2,1,0:T(8,128)S(1)}, f32[4,136,128]{2,1,0:T(8,128)S(1)}, u32[]{:S(2)}, u32[]{:S(2)}) collective-permute-start(f32[4,136,128]{2,1,0:T(8,128)S(1)} %maximum_select_fusion.1), channel_id=1, source_target_pairs={{0,32},{8,40},{16,48},{24,56},{32,64},{40,72},{48,80},{56,88},{64,... | collective-permute-start | bytes 835592 | tf_op jit(solution)/shard_map/ppermute | solution.py:30
  86.5 17.1 %collective-permute-start.5 = (f32[4,136,128]{2,1,0:T(8,128)S(1)}, f32[4,136,128]{2,1,0:T(8,128)S(1)}, u32[]{:S(2)}, u32[]{:S(2)}) collective-permute-start(f32[4,136,128]{2,1,0:T(8,128)S(1)} %maximum_select_fusion.2), channel_id=1, source_target_pairs={{0,64},{8,72},{16,80},{24,88},{32,96},{40,104},{48,112},{56,120},{... | collective-permute-start | bytes 835592 | tf_op jit(solution)/shard_map/ppermute | solution.py:30
  104.0 12.4 %collective-permute-start.6 = (f32[4,136,128]{2,1,0:T(8,128)S(1)}, f32[4,136,128]{2,1,0:T(8,128)S(1)}, u32[]{:S(2)}, u32[]{:S(2)}) collective-permute-start(f32[4,136,128]{2,1,0:T(8,128)S(1)} %maximum_select_fusion.3), channel_id=1, source_target_pairs={{0,128},{8,136},{16,144},{24,152},{32,160},{40,168},{48,176},{56,1... | collective-permute-start | bytes 835592 | tf_op jit(solution)/shard_map/ppermute | solution.py:30
  117.4 3.9 collective-permute-start.7
  120.9 5.6 %copy-start.12 = (f32[1024]{0:T(1024)S(1)}, f32[1024]{0:T(1024)}, u32[]{:S(2)}) copy-start(f32[1024]{0:T(1024)} %param.19) | copy-start | bytes 12292
  121.1 3.7 copy-start.6
  121.1 3.7 copy-start.7
  126.7 1.8 collective-permute-start.8
  128.6 18.2 %copy-start.11 = (s32[128,2]{0,1:T(2,128)S(1)}, s32[128,2]{0,1:T(2,128)}, u32[]{:S(2)}) copy-start(s32[128,2]{0,1:T(2,128)} %param.24) | copy-start | bytes 3076
  174.0 2.6 collective-permute-start.10
  177.7 49.5 %copy-start.3 = (bf16[128,768]{1,0:T(8,128)(2,1)}, bf16[128,768]{1,0:T(8,128)(2,1)S(1)}, u32[]{:S(2)}) copy-start(bf16[128,768]{1,0:T(8,128)(2,1)S(1)} %get-tuple-element.23) | copy-start | bytes 589828
  227.2 17.4 %collective-permute-start.11 = (bf16[80,6144]{1,0:T(8,128)(2,1)S(1)}, bf16[80,6144]{1,0:T(8,128)(2,1)S(1)}, u32[]{:S(2)}, u32[]{:S(2)}) collective-permute-start(bf16[80,6144]{1,0:T(8,128)(2,1)S(1)} %all_gather.10), channel_id=1, source_target_pairs={{0,8},{8,16},{16,24},{24,0},{1,9},{9,17},{17,25},{25,1},{2,10},{10... | collective-permute-start | bytes 2949128 | tf_op jit(solution)/shard_map/ppermute | solution.py:202
  229.6 65.2 %collective-permute-start.12 = (bf16[80,6144]{1,0:T(8,128)(2,1)S(1)}, bf16[80,6144]{1,0:T(8,128)(2,1)S(1)}, u32[]{:S(2)}, u32[]{:S(2)}) collective-permute-start(bf16[80,6144]{1,0:T(8,128)(2,1)S(1)} %all_gather.10), channel_id=1, source_target_pairs={{0,16},{8,24},{16,0},{24,8},{1,17},{9,25},{17,1},{25,9},{2,18},{10... | collective-permute-start | bytes 2949128 | tf_op jit(solution)/shard_map/ppermute | solution.py:202
  229.7 65.1 %collective-permute-start.13 = (bf16[80,6144]{1,0:T(8,128)(2,1)S(1)}, bf16[80,6144]{1,0:T(8,128)(2,1)S(1)}, u32[]{:S(2)}, u32[]{:S(2)}) collective-permute-start(bf16[80,6144]{1,0:T(8,128)(2,1)S(1)} %all_gather.10), channel_id=1, source_target_pairs={{0,24},{8,0},{16,8},{24,16},{1,25},{9,1},{17,9},{25,17},{2,26},{10... | collective-permute-start | bytes 2949128 | tf_op jit(solution)/shard_map/ppermute | solution.py:202
  306.2 7.3 %collective-permute-start.14 = (bf16[4,80,6144]{2,1,0:T(8,128)(2,1)}, bf16[4,80,6144]{2,1,0:T(8,128)(2,1)}, u32[]{:S(2)}, u32[]{:S(2)}) collective-permute-start(bf16[4,80,6144]{2,1,0:T(8,128)(2,1)} %broadcast_select_fusion), channel_id=1, source_target_pairs={{0,4},{4,0},{1,5},{5,1},{2,6},{6,2},{3,7},{7,3},{8,12},{12,8},{9,1... | collective-permute-start | bytes 11796488 | tf_op jit(solution)/shard_map/ppermute | solution.py:207
  306.9 2.7 copy-start.1
  309.6 1.6 copy-start.14
  338.2 6.7 %collective-permute-start.15 = (bf16[4,8,10,1536]{3,1,2,0:T(8,128)(2,1)}, bf16[4,8,10,1536]{3,1,2,0:T(8,128)(2,1)S(1)}, u32[]{:S(2)}, u32[]{:S(2)}) collective-permute-start(bf16[4,8,10,1536]{3,1,2,0:T(8,128)(2,1)} %copy.180), channel_id=1, source_target_pairs={{0,4},{4,0},{1,5},{5,1},{2,6},{6,2},{3,7},{7,3},{8,12},{12,8},{9,1... | collective-permute-start | bytes 2949128 | tf_op jit(solution)/shard_map/ppermute | solution.py:226
  347.5 62.0 %copy-start.4 = (bf16[128,768]{1,0:T(8,128)(2,1)S(1)}, bf16[128,768]{1,0:T(8,128)(2,1)}, u32[]{:S(2)}) copy-start(bf16[128,768]{1,0:T(8,128)(2,1)} %copy-done.3) | copy-start | bytes 589828
  347.5 62.0 %copy-start.10 = (f32[8,10,128]{2,0,1:T(8,128)S(1)}, f32[8,10,128]{2,0,1:T(8,128)}, u32[]{:S(2)}) copy-start(f32[8,10,128]{2,0,1:T(8,128)} %get-tuple-element.19) | copy-start | bytes 122884
  (1 other events, 1.4 us)
Sparse Core Ops, SparseCore 0:
  13.6 99.2 all-gather.1
  146.9 25.9 reduce-scatter.1
